TPU v7x, 256 devices: a whole 4x4x8 slice. The times are simulated.
256 devices in a mesh: group: 8 (over y, core), dev: 32 (over x, z).
Axes of the slice: x: 4, y: 4, z: 8, core: 2. Of those that a mesh axis runs over, the one named last changes fastest.
Arguments:
- embeddings: bfloat16 [262144, 768], P(('group', 'dev')), may hold values from -6 to 6
- cluster_ids: int32 [1024], P(('group', 'dev')), may hold values from 0 to 1023, as said below
Outputs:
- nearest: float32 [262144], P(('group', 'dev'))
Inputs may be any that keep to these rules, and one draw needn't show every extreme that they name: `cluster_ids`: each cluster is a run of 1 to 29 consecutive blocks inside one cluster group of 128 blocks (a group's first block starts a cluster, its last block is a cluster of one block), and its id is the index of its first block; some cluster of every group has exactly 29 blocks.
All inputs are finite; a program needn't handle non-finite values.
Results may differ from a plain program's by a relative error of at most 0.0012.
Values may be sent and summed in bfloat16 or wider, within the bound.
No kernel may reach another device: no remote copies, remote signals or barrier semaphores. Data moves between devices by JAX's collectives and lax.ppermute only.
A program may use at most 192 MiB of HBM per device.

v0:
```python
import jax
import jax.numpy as jnp
from jax import lax
from jax.sharding import PartitionSpec as P


def shift(value, axis, steps, cyclic=False):
    count = lax.axis_size(axis)
    if cyclic:
        pairs = [(source, (source + steps) % count) for source in range(count)]
    else:
        pairs = [(source, source + steps) for source in range(max(0, -steps), min(count, count - steps))]
    return lax.ppermute(value, axis, pairs)


def unit_rows(embeddings):
    values_f = embeddings.astype(jnp.float32)
    squares = jnp.sum(values_f * values_f, axis=1, keepdims=True)
    return (values_f * lax.rsqrt(squares + 1e-06)).astype(jnp.bfloat16)


def body(embeddings, cluster_ids):
    rows, dim = embeddings.shape
    blocks = cluster_ids.shape[0]
    width = rows // blocks
    half = blocks // 2
    count = lax.axis_size("dev")
    stride = count // 4
    place = lax.axis_index("dev")
    first_block = (lax.axis_index("group") * count + place) * blocks
    unit = unit_rows(embeddings)

    own_tags = jnp.repeat(cluster_ids, width)
    local = jnp.arange(rows, dtype=jnp.int32)
    scores = jnp.dot(unit, unit.T, preferred_element_type=jnp.float32)
    keep = (own_tags[:, None] == own_tags[None, :]) & (local[:, None] != local[None, :])
    best = jnp.max(jnp.where(keep, scores + 2.0, jnp.zeros_like(scores)), axis=1)

    lag = first_block + jnp.arange(blocks, dtype=jnp.int32) - cluster_ids
    meta = jnp.zeros((16, dim), jnp.bfloat16).at[0, :blocks].set(lag.astype(jnp.bfloat16))
    extra = meta.shape[0]
    packet = jnp.concatenate([unit, meta], axis=0)
    everything = tuple(range(blocks))
    low, high = everything[:half], everything[half:]

    def part(pk, chosen):
        return jnp.concatenate([pk[chosen[0] * width:(chosen[-1] + 1) * width], pk[-extra:]], axis=0)

    def tile(a, a_blocks, b, b_blocks, k, valid):
        nb = len(b_blocks)
        lags = b[nb * width, b_blocks[0]:b_blocks[-1] + 1].astype(jnp.int32)
        block_reach = k * blocks + jnp.array(b_blocks, jnp.int32) - lags
        a_rows = jnp.concatenate([
            jnp.repeat(jnp.array(a_blocks, jnp.int32), width),
            jnp.full((a.shape[0] - len(a_blocks) * width,), -4 * rows, jnp.int32)])
        b_rows = jnp.concatenate([
            jnp.repeat(block_reach, width),
            jnp.full((b.shape[0] - nb * width,), 4 * rows, jnp.int32)])
        matched = (jnp.min(block_reach) <= max(a_blocks)) & valid

        def compute(unused):
            sims = jnp.dot(a, b.T, preferred_element_type=jnp.float32)
            same = b_rows[None, :] <= a_rows[:, None]
            shifted = jnp.where(same, sims + 2.0, jnp.zeros_like(sims))
            return (jnp.max(shifted, axis=1)[: len(a_blocks) * width],
                    jnp.max(shifted, axis=0)[: nb * width])

        def skipped(unused):
            return (jnp.zeros((len(a_blocks) * width,), jnp.float32),
                    jnp.zeros((nb * width,), jnp.float32))

        return lax.cond(matched, compute, skipped, 0)

    far = shift(unit, "dev", stride, cyclic=True)
    far_ok = [(place >= stride) | (place < m) for m in range(4)]
    ahead = [packet]
    behind = [packet]
    def plan_of():
        return [
            (1, ("own",), everything, ("ahead", 1), everything, 1, True, ("best",), ("ahead", 1)),
            (1, ("behind", 1), everything, ("ahead", 1), everything, 2, place >= 1, ("behind", 1), ("ahead", 1)),
            (1, ("far",), everything, ("behind", 1), everything, stride - 1, far_ok[1], ("far",), ("behind", 1)),
            (2, ("behind", 1), everything, ("ahead", 2), everything, 3, place >= 1, ("behind", 1), ("ahead", 2)),
            (2, ("behind", 2), everything, ("ahead", 2), everything, 4, place >= 2, ("behind", 2), ("ahead", 2)),
            (2, ("far",), everything, ("behind", 2), everything, stride - 2, far_ok[2], ("far",), ("behind", 2)),
            (3, ("behind", 2), everything, ("ahead", 3), low, 5, place >= 2, ("behind", 2), ("ahead", 3)),
            (3, ("far",), everything, ("behind", 3), high, stride - 3, far_ok[3], ("far",), ("behind", 3)),
        ]

    def fetch(where):
        if where[0] == "own":
            return unit
        if where[0] == "far":
            return far
        return (ahead if where[0] == "ahead" else behind)[where[1]]

    sends = {}

    def gather(dest, chosen, value):
        nonlocal best
        if dest == ("best",):
            best = best.at[chosen[0] * width:(chosen[-1] + 1) * width].max(value)
        elif dest in sends:
            sends[dest] = (chosen, jnp.maximum(sends[dest][1], value))
        else:
            sends[dest] = (chosen, value)

    hops = 3
    plan = plan_of()
    for hop in range(1, hops + 1):
        if hop < hops:
            a_next = shift(ahead[-1], "dev", -1)
            b_next = shift(behind[-1], "dev", 1, cyclic=True)
        else:
            a_next = shift(part(ahead[-1], low), "dev", -1)
            b_next = shift(part(behind[-1], high), "dev", 1, cyclic=True)
        ready = [entry for entry in plan if entry[0] == hop - 1]
        pieces = [tile(fetch(e[1]), e[2], fetch(e[3]), e[4], e[5], e[6]) for e in ready]
        if hop == 1:
            a_next, b_next, far, best = lax.optimization_barrier((a_next, b_next, far, best))
        else:
            a_next, b_next, pieces = lax.optimization_barrier((a_next, b_next, pieces))
        for e, (row_part, column_part) in zip(ready, pieces):
            gather(e[7], e[2], row_part)
            gather(e[8], e[4], column_part)
        ahead.append(a_next)
        behind.append(b_next)
    ready = [entry for entry in plan if entry[0] == hops]
    for e in ready:
        row_part, column_part = tile(fetch(e[1]), e[2], fetch(e[3]), e[4], e[5], e[6])
        gather(e[7], e[2], row_part)
        gather(e[8], e[4], column_part)

    for dest, (chosen, value) in sends.items():
        if dest[0] == "ahead":
            arrived = shift(value, "dev", dest[1])
        elif dest[0] == "behind":
            arrived = shift(value, "dev", -dest[1], cyclic=True)
        else:
            arrived = shift(value, "dev", -stride, cyclic=True)
        best = best.at[chosen[0] * width:(chosen[-1] + 1) * width].max(arrived)
    return best - 2.0


def solution(mesh):
    return jax.shard_map(
        body,
        mesh=mesh,
        in_specs=(P(("group", "dev"), None), P(("group", "dev"))),
        out_specs=P(("group", "dev")),
        check_vma=False,
    )
```

profile of v0, /device:TPU:4, one launch (start us, length us, event | category | flops | bytes accessed | tf_op | source)
XLA Modules:
  0.0 170.6 jit_solution(16108500195619433625)
XLA Ops:
  0.0 1.9 %fusion.11 = f32[1024]{0:T(1024)S(1)} fusion(bf16[1024,768]{1,0:T(8,128)(2,1)} %param.64), kind=kLoop, calls=%fused_computation.40 | loop fusion | flops 2358272 | bytes 1576960 | tf_op jit(solution)/shard_map/reduce_sum | solution.py:18
  1.9 0.0 copy-start.1
  1.9 0.3 fusion.12
  2.3 0.3 copy-done.1
  2.6 0.1 fusion.13
  2.7 2.0 %collective-permute-start.1 = (bf16[1040,768]{1,0:T(8,128)(2,1)S(1)}, bf16[1040,768]{1,0:T(8,128)(2,1)}, u32[]{:S(2)}, u32[]{:S(2)}) collective-permute-start(bf16[1040,768]{1,0:T(8,128)(2,1)S(1)} %fusion.13), channel_id=1, source_target_pairs={{0,1},{1,2},{2,3},{3,4},{4,5},{5,6},{6,7},{7,8},{8,9},{9,10},{10,1... | collective-permute-start | bytes 4792328 | tf_op jit(solution)/shard_map/ppermute | solution.py:13
  4.7 5.8 %collective-permute-start = (bf16[1040,768]{1,0:T(8,128)(2,1)S(1)}, bf16[1040,768]{1,0:T(8,128)(2,1)}, u32[]{:S(2)}, u32[]{:S(2)}) collective-permute-start(bf16[1040,768]{1,0:T(8,128)(2,1)S(1)} %fusion.13), channel_id=1, source_target_pairs={{1,0},{2,1},{3,2},{4,3},{5,4},{6,5},{7,6},{8,7},{9,8},{10,9},{11,1... | collective-permute-start | bytes 4792328 | tf_op jit(solution)/shard_map/ppermute | solution.py:13
  10.5 1.6 collective-permute-start.2
  12.1 0.1 broadcast_bitcast_fusion.16
  12.2 2.1 %select_reduce_fusion = f32[1024]{0:T(1024)S(1)} fusion(s32[1024]{0:T(1024)S(1)} %bitcast.120, bf16[1024,768]{1,0:T(8,128)(2,1)S(1)} %fusion.12), kind=kOutput, calls=%fused_computation.33 | convolution fusion | flops 1616903168 | bytes 1581056 | tf_op jit(solution)/shard_map/dot_general | solution.py:35
  14.2 63.1 %collective-permute-done.2 = bf16[1024,768]{1,0:T(8,128)(2,1)} collective-permute-done((bf16[1024,768]{1,0:T(8,128)(2,1)S(1)}, bf16[1024,768]{1,0:T(8,128)(2,1)}, u32[]{:S(2)}, u32[]{:S(2)}) %collective-permute-start.2) | collective-permute-done | bytes 1572896 | tf_op jit(solution)/shard_map/ppermute | solution.py:13
  77.3 1.9 %collective-permute-start.3 = (bf16[1040,768]{1,0:T(8,128)(2,1)}, bf16[1040,768]{1,0:T(8,128)(2,1)}, u32[]{:S(2)}, u32[]{:S(2)}) collective-permute-start(bf16[1040,768]{1,0:T(8,128)(2,1)} %collective-permute-done), channel_id=1, source_target_pairs={{1,0},{2,1},{3,2},{4,3},{5,4},{6,5},{7,6},{8,7},{9,8},{10,9},{11,1... | collective-permute-start | bytes 4792328 | tf_op jit(solution)/shard_map/ppermute | solution.py:13
  79.2 2.1 %collective-permute-start.4 = (bf16[1040,768]{1,0:T(8,128)(2,1)}, bf16[1040,768]{1,0:T(8,128)(2,1)}, u32[]{:S(2)}, u32[]{:S(2)}) collective-permute-start(bf16[1040,768]{1,0:T(8,128)(2,1)} %collective-permute-done.1), channel_id=1, source_target_pairs={{0,1},{1,2},{2,3},{3,4},{4,5},{5,6},{6,7},{7,8},{8,9},{9,10},{10,1... | collective-permute-start | bytes 4792328 | tf_op jit(solution)/shard_map/ppermute | solution.py:13
  81.3 1.4 fusion.16
  84.7 3.6 %conditional.8 = (f32[1024]{0:T(1024)S(1)}, f32[1024]{0:T(1024)S(1)}) conditional(s32[]{:T(128)} %convert_element_type.76, () %tuple.127, (s32[4]{0:T(128)S(1)}, s32[4]{0:T(128)S(1)}, bf16[1024,768]{1,0:T(8,128)(2,1)S(1)}, bf16[1040,768]{1,0:T(8,128)(2,1)}) %tuple.128), branch_computations={%region_3.4_spmd, %region_4.7_spmd} | conditional | flops 1641101312 | bytes 3227892 | solution.py:72
  84.7 0.1 broadcast_bitcast_fusion
  84.8 3.5 %fusion.29 = (f32[1040]{0:T(1024)S(1)}, f32[1024]{0:T(1024)S(1)}) fusion(bf16[1024,768]{1,0:T(8,128)(2,1)S(1)} %get-tuple-element.279, bf16[1040,768]{1,0:T(8,128)(2,1)} %get-tuple-element.280, s32[1024]{0:T(1024)S(1)} %bitcast.116, s32[1040]{0:T(1024)S(1)} %concatenate.48), kind=kOutput, calls=%fused_computation.77 | convolution fusion | flops 1641101312 | bytes 3186816 | tf_op jit(solution)/shard_map/cond/branch_1_fun/dot_general | solution.py:62
  88.3 4.4 %conditional.9 = (f32[1024]{0:T(1024)S(1)}, f32[1024]{0:T(1024)S(1)}) conditional(s32[]{:T(128)} %convert_element_type.77, () %tuple.129, (s32[4]{0:T(128)S(1)}, s32[4]{0:T(128)S(1)}, bf16[1040,768]{1,0:T(8,128)(2,1)}, bf16[1040,768]{1,0:T(8,128)(2,1)}) %tuple.130), branch_computations={%region_8.9_spmd, %region_9.0_spmd} | conditional | flops 1666743552 | bytes 3269048 | solution.py:72
  88.3 0.1 broadcast_bitcast_fusion.2
  88.4 4.3 %fusion.30 = (f32[1040]{0:T(1024)S(1)}, f32[1040]{0:T(1024)S(1)}) fusion(bf16[1040,768]{1,0:T(8,128)(2,1)} %get-tuple-element.283, bf16[1040,768]{1,0:T(8,128)(2,1)} %get-tuple-element.284, s32[1040]{0:T(1024)S(1)} %concatenate.50, s32[1040]{0:T(1024)S(1)} %concatenate.49), kind=kOutput, calls=%fused_computation.78 | convolution fusion | flops 1666743552 | bytes 3211520 | tf_op jit(solution)/shard_map/cond/branch_1_fun/dot_general | solution.py:62
  92.8 23.6 %collective-permute-done.3 = bf16[1040,768]{1,0:T(8,128)(2,1)} collective-permute-done((bf16[1040,768]{1,0:T(8,128)(2,1)}, bf16[1040,768]{1,0:T(8,128)(2,1)}, u32[]{:S(2)}, u32[]{:S(2)}) %collective-permute-start.3) | collective-permute-done | bytes 1597472 | tf_op jit(solution)/shard_map/ppermute | solution.py:13
  116.4 2.2 %collective-permute-done.4 = bf16[1040,768]{1,0:T(8,128)(2,1)} collective-permute-done((bf16[1040,768]{1,0:T(8,128)(2,1)}, bf16[1040,768]{1,0:T(8,128)(2,1)}, u32[]{:S(2)}, u32[]{:S(2)}) %collective-permute-start.4) | collective-permute-done | bytes 1597472 | tf_op jit(solution)/shard_map/ppermute | solution.py:13
  118.6 0.7 slice.166
  119.3 1.2 slice.165
  120.5 1.2 concatenate.65
  121.7 0.1 collective-permute-start.7
  121.8 0.1 pad_maximum_fusion
  121.9 6.0 %collective-permute-start.6 = (bf16[528,768]{1,0:T(8,128)(2,1)S(1)}, bf16[528,768]{1,0:T(8,128)(2,1)}, u32[]{:S(2)}, u32[]{:S(2)}) collective-permute-start(bf16[528,768]{1,0:T(8,128)(2,1)S(1)} %pad_maximum_fusion), channel_id=1, source_target_pairs={{1,0},{2,1},{3,2},{4,3},{5,4},{6,5},{7,6},{8,7},{9,8},{10,9},{11,1... | collective-permute-start | bytes 2433032 | tf_op jit(solution)/shard_map/ppermute | solution.py:13
  127.9 1.3 fusion.19
  129.9 1.3 fusion.24
  132.4 1.9 %collective-permute-start.5 = (f32[1024]{0:T(1024)S(1)}, f32[1024]{0:T(1024)S(1)}, u32[]{:S(2)}, u32[]{:S(2)}) collective-permute-start(f32[1024]{0:T(1024)S(1)} %max.71), channel_id=1, source_target_pairs={{0,1},{1,2},{2,3},{3,4},{4,5},{5,6},{6,7},{7,8},{8,9},{9,10},{10,1... | collective-permute-start | bytes 12296 | tf_op jit(solution)/shard_map/ppermute | solution.py:13
  134.4 0.2 conditional.11
  134.6 0.0 copy-start.2
  134.7 8.4 %collective-permute-done.7 = bf16[528,768]{1,0:T(8,128)(2,1)S(1)} collective-permute-done((bf16[528,768]{1,0:T(8,128)(2,1)S(1)}, bf16[528,768]{1,0:T(8,128)(2,1)S(1)}, u32[]{:S(2)}, u32[]{:S(2)}) %collective-permute-start.7) | collective-permute-done | bytes 811040 | tf_op jit(solution)/shard_map/ppermute | solution.py:13
  143.1 1.2 collective-permute-done.6
  144.3 0.7 fusion.21
  145.6 1.3 convert_subtract_fusion
  147.6 1.9 %collective-permute-start.10 = (f32[1024]{0:T(1024)S(1)}, f32[1024]{0:T(1024)S(1)}, u32[]{:S(2)}, u32[]{:S(2)}) collective-permute-start(f32[1024]{0:T(1024)S(1)} %max.79), channel_id=1, source_target_pairs={{0,2},{1,3},{2,4},{3,5},{4,6},{5,7},{6,8},{7,9},{8,10},{9,11},{10,... | collective-permute-start | bytes 12296 | tf_op jit(solution)/shard_map/ppermute | solution.py:13
  149.6 8.2 %collective-permute-start.11 = (f32[1024]{0:T(1024)S(1)}, f32[1024]{0:T(1024)S(1)}, u32[]{:S(2)}, u32[]{:S(2)}) collective-permute-start(f32[1024]{0:T(1024)S(1)} %maximum_maximum_fusion), channel_id=1, source_target_pairs={{0,30},{1,31},{2,0},{3,1},{4,2},{5,3},{6,4},{7,5},{8,6},{9,7},{10,... | collective-permute-start | bytes 12296 | tf_op jit(solution)/shard_map/ppermute | solution.py:13
  157.9 0.2 collective-permute-start.9
  158.1 2.5 %collective-permute-start.8 = (f32[1024]{0:T(1024)S(1)}, f32[1024]{0:T(1024)S(1)}, u32[]{:S(2)}, u32[]{:S(2)}) collective-permute-start(f32[1024]{0:T(1024)S(1)} %maximum_maximum_fusion.3), channel_id=1, source_target_pairs={{0,31},{1,0},{2,1},{3,2},{4,3},{5,4},{6,5},{7,6},{8,7},{9,8},{10,9... | collective-permute-start | bytes 12296 | tf_op jit(solution)/shard_map/ppermute | solution.py:13
  160.6 0.0 collective-permute-done.5
  160.6 1.9 %collective-permute-start.12 = (f32[512]{0:T(512)S(1)}, f32[512]{0:T(512)S(1)}, u32[]{:S(2)}, u32[]{:S(2)}) collective-permute-start(f32[512]{0:T(512)S(1)} %get-tuple-element.379), channel_id=1, source_target_pairs={{0,3},{1,4},{2,5},{3,6},{4,7},{5,8},{6,9},{7,10},{8,11},{9,12},{10... | collective-permute-start | bytes 6152 | tf_op jit(solution)/shard_map/ppermute | solution.py:13
  162.6 6.0 %collective-permute-start.13 = (f32[512]{0:T(512)S(1)}, f32[512]{0:T(512)S(1)}, u32[]{:S(2)}, u32[]{:S(2)}) collective-permute-start(f32[512]{0:T(512)S(1)} %get-tuple-element.380), channel_id=1, source_target_pairs={{0,29},{1,30},{2,31},{3,0},{4,1},{5,2},{6,3},{7,4},{8,5},{9,6},{10... | collective-permute-start | bytes 6152 | tf_op jit(solution)/shard_map/ppermute | solution.py:13
  168.5 0.0 collective-permute-done.11
  168.6 0.0 collective-permute-done.9
  168.6 1.4 collective-permute-done.12
  170.0 0.6 broadcast_add_fusion
  (47 shorter events, 0.3 us)
Async XLA Ops:
  0.0 1.9 %copy-start = (bf16[1024,768]{1,0:T(8,128)(2,1)S(1)}, bf16[1024,768]{1,0:T(8,128)(2,1)}, u32[]{:S(2)}) copy-start(bf16[1024,768]{1,0:T(8,128)(2,1)} %param.64) | copy-start | bytes 4718596
  1.9 0.7 copy-start.1
  2.7 74.6 %collective-permute-start.1 = (bf16[1040,768]{1,0:T(8,128)(2,1)S(1)}, bf16[1040,768]{1,0:T(8,128)(2,1)}, u32[]{:S(2)}, u32[]{:S(2)}) collective-permute-start(bf16[1040,768]{1,0:T(8,128)(2,1)S(1)} %fusion.13), channel_id=1, source_target_pairs={{0,1},{1,2},{2,3},{3,4},{4,5},{5,6},{6,7},{7,8},{8,9},{9,10},{10,1... | collective-permute-start | bytes 4792328 | tf_op jit(solution)/shard_map/ppermute | solution.py:13
  4.7 72.6 %collective-permute-start = (bf16[1040,768]{1,0:T(8,128)(2,1)S(1)}, bf16[1040,768]{1,0:T(8,128)(2,1)}, u32[]{:S(2)}, u32[]{:S(2)}) collective-permute-start(bf16[1040,768]{1,0:T(8,128)(2,1)S(1)} %fusion.13), channel_id=1, source_target_pairs={{1,0},{2,1},{3,2},{4,3},{5,4},{6,5},{7,6},{8,7},{9,8},{10,9},{11,1... | collective-permute-start | bytes 4792328 | tf_op jit(solution)/shard_map/ppermute | solution.py:13
  10.5 66.8 %collective-permute-start.2 = (bf16[1024,768]{1,0:T(8,128)(2,1)S(1)}, bf16[1024,768]{1,0:T(8,128)(2,1)}, u32[]{:S(2)}, u32[]{:S(2)}) collective-permute-start(bf16[1024,768]{1,0:T(8,128)(2,1)S(1)} %fusion.12), channel_id=1, source_target_pairs={{0,8},{1,9},{2,10},{3,11},{4,12},{5,13},{6,14},{7,15},{8,16},{9,17... | collective-permute-start | bytes 4718600 | tf_op jit(solution)/shard_map/ppermute | solution.py:13
  77.3 39.0 %collective-permute-start.3 = (bf16[1040,768]{1,0:T(8,128)(2,1)}, bf16[1040,768]{1,0:T(8,128)(2,1)}, u32[]{:S(2)}, u32[]{:S(2)}) collective-permute-start(bf16[1040,768]{1,0:T(8,128)(2,1)} %collective-permute-done), channel_id=1, source_target_pairs={{1,0},{2,1},{3,2},{4,3},{5,4},{6,5},{7,6},{8,7},{9,8},{10,9},{11,1... | collective-permute-start | bytes 4792328 | tf_op jit(solution)/shard_map/ppermute | solution.py:13
  79.2 39.3 %collective-permute-start.4 = (bf16[1040,768]{1,0:T(8,128)(2,1)}, bf16[1040,768]{1,0:T(8,128)(2,1)}, u32[]{:S(2)}, u32[]{:S(2)}) collective-permute-start(bf16[1040,768]{1,0:T(8,128)(2,1)} %collective-permute-done.1), channel_id=1, source_target_pairs={{0,1},{1,2},{2,3},{3,4},{4,5},{5,6},{6,7},{7,8},{8,9},{9,10},{10,1... | collective-permute-start | bytes 4792328 | tf_op jit(solution)/shard_map/ppermute | solution.py:13
  121.7 21.4 %collective-permute-start.7 = (bf16[528,768]{1,0:T(8,128)(2,1)S(1)}, bf16[528,768]{1,0:T(8,128)(2,1)S(1)}, u32[]{:S(2)}, u32[]{:S(2)}) collective-permute-start(bf16[528,768]{1,0:T(8,128)(2,1)S(1)} %concatenate.65), channel_id=1, source_target_pairs={{0,1},{1,2},{2,3},{3,4},{4,5},{5,6},{6,7},{7,8},{8,9},{9,10},{10,1... | collective-permute-start | bytes 2433032 | tf_op jit(solution)/shard_map/ppermute | solution.py:13
  121.9 22.4 %collective-permute-start.6 = (bf16[528,768]{1,0:T(8,128)(2,1)S(1)}, bf16[528,768]{1,0:T(8,128)(2,1)}, u32[]{:S(2)}, u32[]{:S(2)}) collective-permute-start(bf16[528,768]{1,0:T(8,128)(2,1)S(1)} %pad_maximum_fusion), channel_id=1, source_target_pairs={{1,0},{2,1},{3,2},{4,3},{5,4},{6,5},{7,6},{8,7},{9,8},{10,9},{11,1... | collective-permute-start | bytes 2433032 | tf_op jit(solution)/shard_map/ppermute | solution.py:13
  132.4 28.2 %collective-permute-start.5 = (f32[1024]{0:T(1024)S(1)}, f32[1024]{0:T(1024)S(1)}, u32[]{:S(2)}, u32[]{:S(2)}) collective-permute-start(f32[1024]{0:T(1024)S(1)} %max.71), channel_id=1, source_target_pairs={{0,1},{1,2},{2,3},{3,4},{4,5},{5,6},{6,7},{7,8},{8,9},{9,10},{10,1... | collective-permute-start | bytes 12296 | tf_op jit(solution)/shard_map/ppermute | solution.py:13
  134.6 9.6 %copy-start.2 = (s32[1,2]{1,0:T(1,128)S(1)}, s32[1,2]{1,0:T(1,128)}, u32[]{:S(2)}) copy-start(s32[1,2]{1,0:T(1,128)} %constant.408) | copy-start | bytes 28
  147.6 14.9 %collective-permute-start.10 = (f32[1024]{0:T(1024)S(1)}, f32[1024]{0:T(1024)S(1)}, u32[]{:S(2)}, u32[]{:S(2)}) collective-permute-start(f32[1024]{0:T(1024)S(1)} %max.79), channel_id=1, source_target_pairs={{0,2},{1,3},{2,4},{3,5},{4,6},{5,7},{6,8},{7,9},{8,10},{9,11},{10,... | collective-permute-start | bytes 12296 | tf_op jit(solution)/shard_map/ppermute | solution.py:13
  149.6 19.0 %collective-permute-start.11 = (f32[1024]{0:T(1024)S(1)}, f32[1024]{0:T(1024)S(1)}, u32[]{:S(2)}, u32[]{:S(2)}) collective-permute-start(f32[1024]{0:T(1024)S(1)} %maximum_maximum_fusion), channel_id=1, source_target_pairs={{0,30},{1,31},{2,0},{3,1},{4,2},{5,3},{6,4},{7,5},{8,6},{9,7},{10,... | collective-permute-start | bytes 12296 | tf_op jit(solution)/shard_map/ppermute | solution.py:13
  157.9 10.7 %collective-permute-start.9 = (f32[1024]{0:T(1024)S(1)}, f32[1024]{0:T(1024)S(1)}, u32[]{:S(2)}, u32[]{:S(2)}) collective-permute-start(f32[1024]{0:T(1024)S(1)} %maximum_maximum_fusion.2), channel_id=1, source_target_pairs={{0,24},{1,25},{2,26},{3,27},{4,28},{5,29},{6,30},{7,31},{8,0},{9,1... | collective-permute-start | bytes 12296 | tf_op jit(solution)/shard_map/ppermute | solution.py:13
  158.1 10.5 %collective-permute-start.8 = (f32[1024]{0:T(1024)S(1)}, f32[1024]{0:T(1024)S(1)}, u32[]{:S(2)}, u32[]{:S(2)}) collective-permute-start(f32[1024]{0:T(1024)S(1)} %maximum_maximum_fusion.3), channel_id=1, source_target_pairs={{0,31},{1,0},{2,1},{3,2},{4,3},{5,4},{6,5},{7,6},{8,7},{9,8},{10,9... | collective-permute-start | bytes 12296 | tf_op jit(solution)/shard_map/ppermute | solution.py:13
  160.6 9.4 %collective-permute-start.12 = (f32[512]{0:T(512)S(1)}, f32[512]{0:T(512)S(1)}, u32[]{:S(2)}, u32[]{:S(2)}) collective-permute-start(f32[512]{0:T(512)S(1)} %get-tuple-element.379), channel_id=1, source_target_pairs={{0,3},{1,4},{2,5},{3,6},{4,7},{5,8},{6,9},{7,10},{8,11},{9,12},{10... | collective-permute-start | bytes 6152 | tf_op jit(solution)/shard_map/ppermute | solution.py:13
  162.6 7.5 %collective-permute-start.13 = (f32[512]{0:T(512)S(1)}, f32[512]{0:T(512)S(1)}, u32[]{:S(2)}, u32[]{:S(2)}) collective-permute-start(f32[512]{0:T(512)S(1)} %get-tuple-element.380), channel_id=1, source_target_pairs={{0,29},{1,30},{2,31},{3,0},{4,1},{5,2},{6,3},{7,4},{8,5},{9,6},{10... | collective-permute-start | bytes 6152 | tf_op jit(solution)/shard_map/ppermute | solution.py:13
where the time goes:
time: 173 us; the launch traced here: 171 us
  waiting for transfers between devices  99.9 us (58%)
  starting transfers between devices  42.3 us (24%)
  matrix products  9.82 us (6%)
  other arithmetic  9.1 us (5%)
  between operations  5.38 us (3%)
  local copies, waits for them, and re-layouts  3.71 us (2%)
    ppermute x14, waiting for transfers between devices, shift(): return lax.ppermute(value, axis, pairs)  99.9 us
    ppermute x14, starting transfers between devices, shift(): return lax.ppermute(value, axis, pairs)  42.3 us
    dot_general x2, matrix products, compute(): sims = jnp.dot(a, b.T, preferred_element_type=jnp.float32)  7.77 us
    sub x4, other arithmetic, tile(): block_reach = k * blocks + jnp.array(b_blocks, jnp.int32) - lags  4.76 us
  transfers between devices with their start and end apart: 14, of which 6 were waited for; matrix products, arithmetic and copies ran while one was open for 10% of the time, Pallas kernels for 0%

commit v1 on v0

--- a/solution.py
+++ b/solution.py
@@ -108,9 +108,15 @@
     hops = 3
     plan = plan_of()
     for hop in range(1, hops + 1):
-        if hop < hops:
-            a_next = shift(ahead[-1], "dev", -1)
-            b_next = shift(behind[-1], "dev", 1, cyclic=True)
+        if hop == 1:
+            a_next = shift(packet, "dev", -1)
+            b_next = shift(packet, "dev", 1, cyclic=True)
+            first_ahead, first_behind = a_next, b_next
+        elif hop < hops:
+            source_a = first_ahead if hop == 2 else ahead[-1]
+            source_b = first_behind if hop == 2 else behind[-1]
+            a_next = shift(source_a, "dev", -1)
+            b_next = shift(source_b, "dev", 1, cyclic=True)
         else:
             a_next = shift(part(ahead[-1], low), "dev", -1)
             b_next = shift(part(behind[-1], high), "dev", 1, cyclic=True)

time: 173 us -> 182 us (1.052)
  the two profiles are of different devices: /device:TPU:4 before, /device:TPU:36 now
where the time goes in v1:
time: 182 us
  starting transfers between devices  79.8 us (44%)
  waiting for transfers between devices  66.9 us (37%)
  matrix products  16.7 us (9%)
  other arithmetic  9.1 us (5%)
  between operations  5.41 us (3%)
  local copies, waits for them, and re-layouts  3.96 us (2%)
    ppermute x14, starting transfers between devices, shift(): return lax.ppermute(value, axis, pairs)  79.8 us
    ppermute x14, waiting for transfers between devices, shift(): return lax.ppermute(value, axis, pairs)  66.9 us
    dot_general x4, matrix products, compute(): sims = jnp.dot(a, b.T, preferred_element_type=jnp.float32)  14.7 us
    sub x4, other arithmetic, tile(): block_reach = k * blocks + jnp.array(b_blocks, jnp.int32) - lags  4.76 us
  transfers between devices with their start and end apart: 14, of which 7 were waited for; matrix products, arithmetic and copies ran while one was open for 13% of the time, Pallas kernels for 0%

profile of v1, /device:TPU:36, one launch (start us, length us, event | category | flops | bytes accessed | tf_op | source)
XLA Modules:
  0.0 182.2 jit_solution(13119638679067272971)
XLA Ops:
  0.0 1.9 %fusion.11 = f32[1024]{0:T(1024)S(1)} fusion(bf16[1024,768]{1,0:T(8,128)(2,1)} %param.64), kind=kLoop, calls=%fused_computation.40 | loop fusion | flops 2358272 | bytes 1576960 | tf_op jit(solution)/shard_map/reduce_sum | solution.py:18
  1.9 0.3 fusion.12
  2.3 0.3 copy-done.1
  2.6 0.1 fusion.13
  2.7 2.0 %collective-permute-start = (bf16[1040,768]{1,0:T(8,128)(2,1)S(1)}, bf16[1040,768]{1,0:T(8,128)(2,1)}, u32[]{:S(2)}, u32[]{:S(2)}) collective-permute-start(bf16[1040,768]{1,0:T(8,128)(2,1)S(1)} %fusion.13), channel_id=1, source_target_pairs={{1,0},{2,1},{3,2},{4,3},{5,4},{6,5},{7,6},{8,7},{9,8},{10,9},{11,1... | collective-permute-start | bytes 4792328 | tf_op jit(solution)/shard_map/ppermute | solution.py:13
  4.7 2.0 %collective-permute-start.1 = (bf16[1040,768]{1,0:T(8,128)(2,1)S(1)}, bf16[1040,768]{1,0:T(8,128)(2,1)}, u32[]{:S(2)}, u32[]{:S(2)}) collective-permute-start(bf16[1040,768]{1,0:T(8,128)(2,1)S(1)} %fusion.13), channel_id=1, source_target_pairs={{0,1},{1,2},{2,3},{3,4},{4,5},{5,6},{6,7},{7,8},{8,9},{9,10},{10,1... | collective-permute-start | bytes 4792328 | tf_op jit(solution)/shard_map/ppermute | solution.py:13
  6.7 1.2 collective-permute-start.2
  7.9 33.6 %collective-permute-done = bf16[1040,768]{1,0:T(8,128)(2,1)} collective-permute-done((bf16[1040,768]{1,0:T(8,128)(2,1)S(1)}, bf16[1040,768]{1,0:T(8,128)(2,1)}, u32[]{:S(2)}, u32[]{:S(2)}) %collective-permute-start) | collective-permute-done | bytes 1597472 | tf_op jit(solution)/shard_map/ppermute | solution.py:13
  41.5 5.1 %collective-permute-start.3 = (bf16[1040,768]{1,0:T(8,128)(2,1)}, bf16[1040,768]{1,0:T(8,128)(2,1)}, u32[]{:S(2)}, u32[]{:S(2)}) collective-permute-start(bf16[1040,768]{1,0:T(8,128)(2,1)} %collective-permute-done), channel_id=1, source_target_pairs={{1,0},{2,1},{3,2},{4,3},{5,4},{6,5},{7,6},{8,7},{9,8},{10,9},{11,1... | collective-permute-start | bytes 4792328 | tf_op jit(solution)/shard_map/ppermute | solution.py:13
  46.6 0.1 collective-permute-start.4
  46.7 0.1 broadcast_bitcast_fusion.16
  46.8 2.1 %select_reduce_fusion = f32[1024]{0:T(1024)S(1)} fusion(s32[1024]{0:T(1024)S(1)} %bitcast.117, bf16[1024,768]{1,0:T(8,128)(2,1)S(1)} %fusion.12), kind=kOutput, calls=%fused_computation.33 | convolution fusion | flops 1616903168 | bytes 1581056 | tf_op jit(solution)/shard_map/dot_general | solution.py:35
  48.9 1.4 fusion.16
  52.3 4.4 %conditional.9 = (f32[1024]{0:T(1024)S(1)}, f32[1024]{0:T(1024)S(1)}) conditional(s32[]{:T(128)} %convert_element_type.77, () %tuple.129, (s32[4]{0:T(128)S(1)}, s32[4]{0:T(128)S(1)}, bf16[1040,768]{1,0:T(8,128)(2,1)}, bf16[1040,768]{1,0:T(8,128)(2,1)}) %tuple.130), branch_computations={%region_8.9_spmd, %region_9.0_spmd} | conditional | flops 1666743552 | bytes 3269048 | solution.py:72
  52.3 0.1 broadcast_bitcast_fusion.2
  52.4 4.3 %fusion.30 = (f32[1040]{0:T(1024)S(1)}, f32[1040]{0:T(1024)S(1)}) fusion(bf16[1040,768]{1,0:T(8,128)(2,1)} %get-tuple-element.283, bf16[1040,768]{1,0:T(8,128)(2,1)} %get-tuple-element.284, s32[1040]{0:T(1024)S(1)} %concatenate.50, s32[1040]{0:T(1024)S(1)} %concatenate.49), kind=kOutput, calls=%fused_computation.78 | convolution fusion | flops 1666743552 | bytes 3211520 | tf_op jit(solution)/shard_map/cond/branch_1_fun/dot_general | solution.py:62
  56.7 3.6 %conditional.8 = (f32[1024]{0:T(1024)S(1)}, f32[1024]{0:T(1024)S(1)}) conditional(s32[]{:T(128)} %convert_element_type.76, () %tuple.127, (s32[4]{0:T(128)S(1)}, s32[4]{0:T(128)S(1)}, bf16[1024,768]{1,0:T(8,128)(2,1)S(1)}, bf16[1040,768]{1,0:T(8,128)(2,1)}) %tuple.128), branch_computations={%region_3.4_spmd, %region_4.7_spmd} | conditional | flops 1641101312 | bytes 3227892 | solution.py:72
  56.7 0.1 broadcast_bitcast_fusion
  56.8 3.5 %fusion.29 = (f32[1040]{0:T(1024)S(1)}, f32[1024]{0:T(1024)S(1)}) fusion(bf16[1024,768]{1,0:T(8,128)(2,1)S(1)} %get-tuple-element.279, bf16[1040,768]{1,0:T(8,128)(2,1)} %get-tuple-element.280, s32[1024]{0:T(1024)S(1)} %bitcast.119, s32[1040]{0:T(1024)S(1)} %concatenate.48), kind=kOutput, calls=%fused_computation.77 | convolution fusion | flops 1641101312 | bytes 3186816 | tf_op jit(solution)/shard_map/cond/branch_1_fun/dot_general | solution.py:62
  60.3 19.9 %collective-permute-done.3 = bf16[1040,768]{1,0:T(8,128)(2,1)} collective-permute-done((bf16[1040,768]{1,0:T(8,128)(2,1)}, bf16[1040,768]{1,0:T(8,128)(2,1)}, u32[]{:S(2)}, u32[]{:S(2)}) %collective-permute-start.3) | collective-permute-done | bytes 1597472 | tf_op jit(solution)/shard_map/ppermute | solution.py:13
  80.2 5.3 %collective-permute-done.4 = bf16[1040,768]{1,0:T(8,128)(2,1)} collective-permute-done((bf16[1040,768]{1,0:T(8,128)(2,1)}, bf16[1040,768]{1,0:T(8,128)(2,1)}, u32[]{:S(2)}, u32[]{:S(2)}) %collective-permute-start.4) | collective-permute-done | bytes 1597472 | tf_op jit(solution)/shard_map/ppermute | solution.py:13
  85.5 1.2 slice.165
  86.7 0.7 slice.166
  87.5 38.6 %collective-permute-start.6 = (bf16[528,768]{1,0:T(8,128)(2,1)S(1)}, bf16[528,768]{1,0:T(8,128)(2,1)}, u32[]{:S(2)}, u32[]{:S(2)}) collective-permute-start(bf16[528,768]{1,0:T(8,128)(2,1)S(1)} %pad_maximum_fusion), channel_id=1, source_target_pairs={{1,0},{2,1},{3,2},{4,3},{5,4},{6,5},{7,6},{8,7},{9,8},{10,9},{11,1... | collective-permute-start | bytes 2433032 | tf_op jit(solution)/shard_map/ppermute | solution.py:13
  126.1 1.2 concatenate.65
  127.3 0.1 collective-permute-start.7
  127.4 1.9 %collective-permute-start.5 = (f32[1024]{0:T(1024)S(1)}, f32[1024]{0:T(1024)S(1)}, u32[]{:S(2)}, u32[]{:S(2)}) collective-permute-start(f32[1024]{0:T(1024)S(1)} %max.71), channel_id=1, source_target_pairs={{0,1},{1,2},{2,3},{3,4},{4,5},{5,6},{6,7},{7,8},{8,9},{9,10},{10,1... | collective-permute-start | bytes 12296 | tf_op jit(solution)/shard_map/ppermute | solution.py:13
  129.3 1.3 fusion.19
  131.3 1.3 fusion.24
  133.8 0.2 conditional.13
  134.1 4.4 %conditional.11 = (f32[1024]{0:T(1024)S(1)}, f32[1024]{0:T(1024)S(1)}) conditional(s32[]{:T(128)} %convert_element_type.83, () %tuple.134, (s32[4]{0:T(128)S(1)}, s32[4]{0:T(128)S(1)}, bf16[1040,768]{1,0:T(8,128)(2,1)}, bf16[1040,768]{1,0:T(8,128)(2,1)}) %tuple.135), branch_computations={%region_18.19_spmd, %region_19.22_spmd} | conditional | flops 1666743552 | bytes 3269048 | solution.py:72
  134.1 0.1 broadcast_bitcast_fusion.6
  134.2 4.3 %fusion.32 = (f32[1040]{0:T(1024)S(1)}, f32[1040]{0:T(1024)S(1)}) fusion(bf16[1040,768]{1,0:T(8,128)(2,1)} %get-tuple-element.291, bf16[1040,768]{1,0:T(8,128)(2,1)} %get-tuple-element.292, s32[1040]{0:T(1024)S(1)} %concatenate.53, s32[1040]{0:T(1024)S(1)} %concatenate.52), kind=kOutput, calls=%fused_computation.80 | convolution fusion | flops 1666743552 | bytes 3211520 | tf_op jit(solution)/shard_map/cond/branch_1_fun/dot_general | solution.py:62
  138.5 0.2 collective-permute-done.6
  138.7 3.5 %collective-permute-done.7 = bf16[528,768]{1,0:T(8,128)(2,1)S(1)} collective-permute-done((bf16[528,768]{1,0:T(8,128)(2,1)S(1)}, bf16[528,768]{1,0:T(8,128)(2,1)S(1)}, u32[]{:S(2)}, u32[]{:S(2)}) %collective-permute-start.7) | collective-permute-done | bytes 811040 | tf_op jit(solution)/shard_map/ppermute | solution.py:13
  142.3 2.4 %collective-permute-start.8 = (f32[1024]{0:T(1024)S(1)}, f32[1024]{0:T(1024)S(1)}, u32[]{:S(2)}, u32[]{:S(2)}) collective-permute-start(f32[1024]{0:T(1024)S(1)} %maximum_maximum_fusion.3), channel_id=1, source_target_pairs={{0,31},{1,0},{2,1},{3,2},{4,3},{5,4},{6,5},{7,6},{8,7},{9,8},{10,9... | collective-permute-start | bytes 12296 | tf_op jit(solution)/shard_map/ppermute | solution.py:13
  144.7 0.7 fusion.21
  146.0 2.8 %conditional.14 = (f32[1024]{0:T(1024)S(1)}, f32[512]{0:T(512)S(1)}) conditional(s32[]{:T(128)} %convert_element_type.90, () %tuple.141, (s32[2]{0:T(128)S(1)}, s32[4]{0:T(128)S(1)}, bf16[1024,768]{1,0:T(8,128)(2,1)}, bf16[528,768]{1,0:T(8,128)(2,1)S(1)}) %tuple.142), branch_computations={%region_33.34_spmd, %region_34.37_spmd} | conditional | flops 833174016 | bytes 2423020 | solution.py:72
  146.2 2.6 %fusion.6 = (f32[528]{0:T(1024)S(1)}, f32[1024]{0:T(1024)S(1)}) fusion(s32[1024]{0:T(1024)S(1)} %bitcast.116, s32[528]{0:T(1024)S(1)} %concatenate.57, bf16[1024,768]{1,0:T(8,128)(2,1)} %get-tuple-element.303, bf16[528,768]{1,0:T(8,128)(2,1)S(1)} %get-tuple-element.304), kind=kOutput, calls=%fused_computation.25 | convolution fusion | flops 833174016 | bytes 2396288 | tf_op jit(solution)/shard_map/cond/branch_1_fun/dot_general | solution.py:62
  148.8 11.5 %collective-permute-start.9 = (f32[1024]{0:T(1024)S(1)}, f32[1024]{0:T(1024)S(1)}, u32[]{:S(2)}, u32[]{:S(2)}) collective-permute-start(f32[1024]{0:T(1024)S(1)} %maximum_maximum_fusion.2), channel_id=1, source_target_pairs={{0,24},{1,25},{2,26},{3,27},{4,28},{5,29},{6,30},{7,31},{8,0},{9,1... | collective-permute-start | bytes 12296 | tf_op jit(solution)/shard_map/ppermute | solution.py:13
  160.3 1.9 %collective-permute-start.10 = (f32[1024]{0:T(1024)S(1)}, f32[1024]{0:T(1024)S(1)}, u32[]{:S(2)}, u32[]{:S(2)}) collective-permute-start(f32[1024]{0:T(1024)S(1)} %max.79), channel_id=1, source_target_pairs={{0,2},{1,3},{2,4},{3,5},{4,6},{5,7},{6,8},{7,9},{8,10},{9,11},{10,... | collective-permute-start | bytes 12296 | tf_op jit(solution)/shard_map/ppermute | solution.py:13
  162.2 1.3 convert_subtract_fusion
  164.2 5.1 %collective-permute-start.11 = (f32[1024]{0:T(1024)S(1)}, f32[1024]{0:T(1024)S(1)}, u32[]{:S(2)}, u32[]{:S(2)}) collective-permute-start(f32[1024]{0:T(1024)S(1)} %maximum_maximum_fusion), channel_id=1, source_target_pairs={{0,30},{1,31},{2,0},{3,1},{4,2},{5,3},{6,4},{7,5},{8,6},{9,7},{10,... | collective-permute-start | bytes 12296 | tf_op jit(solution)/shard_map/ppermute | solution.py:13
  169.3 5.6 %collective-permute-start.12 = (f32[512]{0:T(512)S(1)}, f32[512]{0:T(512)S(1)}, u32[]{:S(2)}, u32[]{:S(2)}) collective-permute-start(f32[512]{0:T(512)S(1)} %get-tuple-element.379), channel_id=1, source_target_pairs={{0,3},{1,4},{2,5},{3,6},{4,7},{5,8},{6,9},{7,10},{8,11},{9,12},{10... | collective-permute-start | bytes 6152 | tf_op jit(solution)/shard_map/ppermute | solution.py:13
  174.9 2.3 %collective-permute-start.13 = (f32[512]{0:T(512)S(1)}, f32[512]{0:T(512)S(1)}, u32[]{:S(2)}, u32[]{:S(2)}) collective-permute-start(f32[512]{0:T(512)S(1)} %get-tuple-element.380), channel_id=1, source_target_pairs={{0,29},{1,30},{2,31},{3,0},{4,1},{5,2},{6,3},{7,4},{8,5},{9,6},{10... | collective-permute-start | bytes 6152 | tf_op jit(solution)/shard_map/ppermute | solution.py:13
  177.3 1.4 collective-permute-done.12
  178.7 2.9 %collective-permute-done.13 = f32[512]{0:T(512)S(1)} collective-permute-done((f32[512]{0:T(512)S(1)}, f32[512]{0:T(512)S(1)}, u32[]{:S(2)}, u32[]{:S(2)}) %collective-permute-start.13) | collective-permute-done | bytes 2080 | tf_op jit(solution)/shard_map/ppermute | solution.py:13
  181.6 0.6 broadcast_add_fusion
  (58 shorter events, 0.5 us)
Async XLA Ops:
  0.0 1.9 %copy-start = (bf16[1024,768]{1,0:T(8,128)(2,1)S(1)}, bf16[1024,768]{1,0:T(8,128)(2,1)}, u32[]{:S(2)}) copy-start(bf16[1024,768]{1,0:T(8,128)(2,1)} %param.64) | copy-start | bytes 4718596
  1.9 0.7 copy-start.1
  2.7 38.8 %collective-permute-start = (bf16[1040,768]{1,0:T(8,128)(2,1)S(1)}, bf16[1040,768]{1,0:T(8,128)(2,1)}, u32[]{:S(2)}, u32[]{:S(2)}) collective-permute-start(bf16[1040,768]{1,0:T(8,128)(2,1)S(1)} %fusion.13), channel_id=1, source_target_pairs={{1,0},{2,1},{3,2},{4,3},{5,4},{6,5},{7,6},{8,7},{9,8},{10,9},{11,1... | collective-permute-start | bytes 4792328 | tf_op jit(solution)/shard_map/ppermute | solution.py:13
  4.7 41.9 %collective-permute-start.1 = (bf16[1040,768]{1,0:T(8,128)(2,1)S(1)}, bf16[1040,768]{1,0:T(8,128)(2,1)}, u32[]{:S(2)}, u32[]{:S(2)}) collective-permute-start(bf16[1040,768]{1,0:T(8,128)(2,1)S(1)} %fusion.13), channel_id=1, source_target_pairs={{0,1},{1,2},{2,3},{3,4},{4,5},{5,6},{6,7},{7,8},{8,9},{9,10},{10,1... | collective-permute-start | bytes 4792328 | tf_op jit(solution)/shard_map/ppermute | solution.py:13
  6.7 42.1 %collective-permute-start.2 = (bf16[1024,768]{1,0:T(8,128)(2,1)S(1)}, bf16[1024,768]{1,0:T(8,128)(2,1)}, u32[]{:S(2)}, u32[]{:S(2)}) collective-permute-start(bf16[1024,768]{1,0:T(8,128)(2,1)S(1)} %fusion.12), channel_id=1, source_target_pairs={{0,8},{1,9},{2,10},{3,11},{4,12},{5,13},{6,14},{7,15},{8,16},{9,17... | collective-permute-start | bytes 4718600 | tf_op jit(solution)/shard_map/ppermute | solution.py:13
  41.5 38.7 %collective-permute-start.3 = (bf16[1040,768]{1,0:T(8,128)(2,1)}, bf16[1040,768]{1,0:T(8,128)(2,1)}, u32[]{:S(2)}, u32[]{:S(2)}) collective-permute-start(bf16[1040,768]{1,0:T(8,128)(2,1)} %collective-permute-done), channel_id=1, source_target_pairs={{1,0},{2,1},{3,2},{4,3},{5,4},{6,5},{7,6},{8,7},{9,8},{10,9},{11,1... | collective-permute-start | bytes 4792328 | tf_op jit(solution)/shard_map/ppermute | solution.py:13
  46.6 38.9 %collective-permute-start.4 = (bf16[1040,768]{1,0:T(8,128)(2,1)}, bf16[1040,768]{1,0:T(8,128)(2,1)}, u32[]{:S(2)}, u32[]{:S(2)}) collective-permute-start(bf16[1040,768]{1,0:T(8,128)(2,1)} %collective-permute-done.1), channel_id=1, source_target_pairs={{0,1},{1,2},{2,3},{3,4},{4,5},{5,6},{6,7},{7,8},{8,9},{9,10},{10,1... | collective-permute-start | bytes 4792328 | tf_op jit(solution)/shard_map/ppermute | solution.py:13
  87.5 51.2 %collective-permute-start.6 = (bf16[528,768]{1,0:T(8,128)(2,1)S(1)}, bf16[528,768]{1,0:T(8,128)(2,1)}, u32[]{:S(2)}, u32[]{:S(2)}) collective-permute-start(bf16[528,768]{1,0:T(8,128)(2,1)S(1)} %pad_maximum_fusion), channel_id=1, source_target_pairs={{1,0},{2,1},{3,2},{4,3},{5,4},{6,5},{7,6},{8,7},{9,8},{10,9},{11,1... | collective-permute-start | bytes 2433032 | tf_op jit(solution)/shard_map/ppermute | solution.py:13
  127.3 15.0 %collective-permute-start.7 = (bf16[528,768]{1,0:T(8,128)(2,1)S(1)}, bf16[528,768]{1,0:T(8,128)(2,1)S(1)}, u32[]{:S(2)}, u32[]{:S(2)}) collective-permute-start(bf16[528,768]{1,0:T(8,128)(2,1)S(1)} %concatenate.65), channel_id=1, source_target_pairs={{0,1},{1,2},{2,3},{3,4},{4,5},{5,6},{6,7},{7,8},{8,9},{9,10},{10,1... | collective-permute-start | bytes 2433032 | tf_op jit(solution)/shard_map/ppermute | solution.py:13
  127.4 41.9 %collective-permute-start.5 = (f32[1024]{0:T(1024)S(1)}, f32[1024]{0:T(1024)S(1)}, u32[]{:S(2)}, u32[]{:S(2)}) collective-permute-start(f32[1024]{0:T(1024)S(1)} %max.71), channel_id=1, source_target_pairs={{0,1},{1,2},{2,3},{3,4},{4,5},{5,6},{6,7},{7,8},{8,9},{9,10},{10,1... | collective-permute-start | bytes 12296 | tf_op jit(solution)/shard_map/ppermute | solution.py:13
  134.1 10.6 %copy-start.2 = (s32[1,2]{1,0:T(1,128)S(1)}, s32[1,2]{1,0:T(1,128)}, u32[]{:S(2)}) copy-start(s32[1,2]{1,0:T(1,128)} %constant.408) | copy-start | bytes 28
  142.3 32.7 %collective-permute-start.8 = (f32[1024]{0:T(1024)S(1)}, f32[1024]{0:T(1024)S(1)}, u32[]{:S(2)}, u32[]{:S(2)}) collective-permute-start(f32[1024]{0:T(1024)S(1)} %maximum_maximum_fusion.3), channel_id=1, source_target_pairs={{0,31},{1,0},{2,1},{3,2},{4,3},{5,4},{6,5},{7,6},{8,7},{9,8},{10,9... | collective-permute-start | bytes 12296 | tf_op jit(solution)/shard_map/ppermute | solution.py:13
  148.8 28.4 %collective-permute-start.9 = (f32[1024]{0:T(1024)S(1)}, f32[1024]{0:T(1024)S(1)}, u32[]{:S(2)}, u32[]{:S(2)}) collective-permute-start(f32[1024]{0:T(1024)S(1)} %maximum_maximum_fusion.2), channel_id=1, source_target_pairs={{0,24},{1,25},{2,26},{3,27},{4,28},{5,29},{6,30},{7,31},{8,0},{9,1... | collective-permute-start | bytes 12296 | tf_op jit(solution)/shard_map/ppermute | solution.py:13
  160.3 17.0 %collective-permute-start.10 = (f32[1024]{0:T(1024)S(1)}, f32[1024]{0:T(1024)S(1)}, u32[]{:S(2)}, u32[]{:S(2)}) collective-permute-start(f32[1024]{0:T(1024)S(1)} %max.79), channel_id=1, source_target_pairs={{0,2},{1,3},{2,4},{3,5},{4,6},{5,7},{6,8},{7,9},{8,10},{9,11},{10,... | collective-permute-start | bytes 12296 | tf_op jit(solution)/shard_map/ppermute | solution.py:13
  164.2 13.0 %collective-permute-start.11 = (f32[1024]{0:T(1024)S(1)}, f32[1024]{0:T(1024)S(1)}, u32[]{:S(2)}, u32[]{:S(2)}) collective-permute-start(f32[1024]{0:T(1024)S(1)} %maximum_maximum_fusion), channel_id=1, source_target_pairs={{0,30},{1,31},{2,0},{3,1},{4,2},{5,3},{6,4},{7,5},{8,6},{9,7},{10,... | collective-permute-start | bytes 12296 | tf_op jit(solution)/shard_map/ppermute | solution.py:13
  169.3 9.4 %collective-permute-start.12 = (f32[512]{0:T(512)S(1)}, f32[512]{0:T(512)S(1)}, u32[]{:S(2)}, u32[]{:S(2)}) collective-permute-start(f32[512]{0:T(512)S(1)} %get-tuple-element.379), channel_id=1, source_target_pairs={{0,3},{1,4},{2,5},{3,6},{4,7},{5,8},{6,9},{7,10},{8,11},{9,12},{10... | collective-permute-start | bytes 6152 | tf_op jit(solution)/shard_map/ppermute | solution.py:13
  174.9 6.7 %collective-permute-start.13 = (f32[512]{0:T(512)S(1)}, f32[512]{0:T(512)S(1)}, u32[]{:S(2)}, u32[]{:S(2)}) collective-permute-start(f32[512]{0:T(512)S(1)} %get-tuple-element.380), channel_id=1, source_target_pairs={{0,29},{1,30},{2,31},{3,0},{4,1},{5,2},{6,3},{7,4},{8,5},{9,6},{10... | collective-permute-start | bytes 6152 | tf_op jit(solution)/shard_map/ppermute | solution.py:13

commit v2 on v0

--- a/solution.py
+++ b/solution.py
@@ -71,7 +71,8 @@
 
         return lax.cond(matched, compute, skipped, 0)
 
-    far = shift(unit, "dev", stride, cyclic=True)
+    far = jnp.concatenate([shift(unit[:half * width], "dev", stride, cyclic=True),
+                           shift(unit[half * width:], "dev", stride, cyclic=True)], axis=0)
     far_ok = [(place >= stride) | (place < m) for m in range(4)]
     ahead = [packet]
     behind = [packet]

time: 173 us -> 175 us (1.012)
  waiting for transfers between devices: 99.9 us -> 95.5 us
  matrix products: 9.82 us -> 14.1 us
    ppermute x14 -> x15, waiting for transfers between devices: 99.9 us -> 95.5 us  [shift(): return lax.ppermute(value, axis, pairs)]
    dot_general x2 -> x3, matrix products: 7.77 us -> 12 us  [compute(): sims = jnp.dot(a, b.T, preferred_element_type=jnp.float32)]
    ppermute x14 -> x15, starting transfers between devices: 42.3 us -> 42.4 us  [shift(): return lax.ppermute(value, axis, pairs)]
  transfers between devices with their start and end apart: 14 -> 15, of which waited for: 6 -> 7; matrix products, arithmetic and copies ran while one was open for 10% -> 13% of each run, Pallas kernels for 0% -> 0%
where the time goes in v2:
time: 175 us; the launch traced here: 172 us
  waiting for transfers between devices  95.5 us (55%)
  starting transfers between devices  42.4 us (24%)
  matrix products  14.1 us (8%)
  other arithmetic  10.8 us (6%)
  between operations  5.45 us (3%)
  local copies, waits for them, and re-layouts  3.9 us (2%)
    ppermute x15, waiting for transfers between devices, shift(): return lax.ppermute(value, axis, pairs)  95.5 us
    ppermute x15, starting transfers between devices, shift(): return lax.ppermute(value, axis, pairs)  42.4 us
    dot_general x3, matrix products, compute(): sims = jnp.dot(a, b.T, preferred_element_type=jnp.float32)  12 us
    sub x4, other arithmetic, tile(): block_reach = k * blocks + jnp.array(b_blocks, jnp.int32) - lags  5.34 us
  transfers between devices with their start and end apart: 15, of which 7 were waited for; matrix products, arithmetic and copies ran while one was open for 13% of the time, Pallas kernels for 0%

profile of v2, /device:TPU:4, one launch (start us, length us, event | category | flops | bytes accessed | tf_op | source)
XLA Modules:
  0.0 172.4 jit_solution(6724228373101821927)
XLA Ops:
  0.0 1.9 %fusion.11 = f32[1024]{0:T(1024)S(1)} fusion(bf16[1024,768]{1,0:T(8,128)(2,1)} %param.64), kind=kLoop, calls=%fused_computation.40 | loop fusion | flops 2358272 | bytes 1576960 | tf_op jit(solution)/shard_map/reduce_sum | solution.py:18
  1.9 0.3 fusion.12
  2.3 0.3 copy-done.1
  2.6 0.1 fusion.13
  2.7 2.0 %collective-permute-start.1 = (bf16[1040,768]{1,0:T(8,128)(2,1)S(1)}, bf16[1040,768]{1,0:T(8,128)(2,1)}, u32[]{:S(2)}, u32[]{:S(2)}) collective-permute-start(bf16[1040,768]{1,0:T(8,128)(2,1)S(1)} %fusion.13), channel_id=1, source_target_pairs={{0,1},{1,2},{2,3},{3,4},{4,5},{5,6},{6,7},{7,8},{8,9},{9,10},{10,1... | collective-permute-start | bytes 4792328 | tf_op jit(solution)/shard_map/ppermute | solution.py:13
  4.7 5.8 %collective-permute-start = (bf16[1040,768]{1,0:T(8,128)(2,1)S(1)}, bf16[1040,768]{1,0:T(8,128)(2,1)}, u32[]{:S(2)}, u32[]{:S(2)}) collective-permute-start(bf16[1040,768]{1,0:T(8,128)(2,1)S(1)} %fusion.13), channel_id=1, source_target_pairs={{1,0},{2,1},{3,2},{4,3},{5,4},{6,5},{7,6},{8,7},{9,8},{10,9},{11,1... | collective-permute-start | bytes 4792328 | tf_op jit(solution)/shard_map/ppermute | solution.py:13
  10.5 0.1 fusion.36
  10.6 1.6 collective-permute-start.2
  12.2 0.1 collective-permute-start.3
  12.3 0.1 broadcast_bitcast_fusion.16
  12.4 2.1 %select_reduce_fusion = f32[1024]{0:T(1024)S(1)} fusion(s32[1024]{0:T(1024)S(1)} %bitcast.120, bf16[1024,768]{1,0:T(8,128)(2,1)S(1)} %fusion.12), kind=kOutput, calls=%fused_computation.33 | convolution fusion | flops 1616903168 | bytes 1581056 | tf_op jit(solution)/shard_map/dot_general | solution.py:35
  14.4 46.0 %collective-permute-done.2 = bf16[512,768]{1,0:T(8,128)(2,1)S(1)} collective-permute-done((bf16[512,768]{1,0:T(8,128)(2,1)S(1)}, bf16[512,768]{1,0:T(8,128)(2,1)S(1)}, u32[]{:S(2)}, u32[]{:S(2)}) %collective-permute-start.2) | collective-permute-done | bytes 786464 | tf_op jit(solution)/shard_map/ppermute | solution.py:13
  60.5 16.8 %collective-permute-done.3 = bf16[512,768]{1,0:T(8,128)(2,1)S(1)} collective-permute-done((bf16[512,768]{1,0:T(8,128)(2,1)S(1)}, bf16[512,768]{1,0:T(8,128)(2,1)S(1)}, u32[]{:S(2)}, u32[]{:S(2)}) %collective-permute-start.3) | collective-permute-done | bytes 786464 | tf_op jit(solution)/shard_map/ppermute | solution.py:13
  77.2 0.1 pad_maximum_fusion
  77.3 1.9 %collective-permute-start.4 = (bf16[1040,768]{1,0:T(8,128)(2,1)}, bf16[1040,768]{1,0:T(8,128)(2,1)}, u32[]{:S(2)}, u32[]{:S(2)}) collective-permute-start(bf16[1040,768]{1,0:T(8,128)(2,1)} %collective-permute-done), channel_id=1, source_target_pairs={{1,0},{2,1},{3,2},{4,3},{5,4},{6,5},{7,6},{8,7},{9,8},{10,9},{11,1... | collective-permute-start | bytes 4792328 | tf_op jit(solution)/shard_map/ppermute | solution.py:13
  79.3 2.1 %collective-permute-start.5 = (bf16[1040,768]{1,0:T(8,128)(2,1)}, bf16[1040,768]{1,0:T(8,128)(2,1)}, u32[]{:S(2)}, u32[]{:S(2)}) collective-permute-start(bf16[1040,768]{1,0:T(8,128)(2,1)} %collective-permute-done.1), channel_id=1, source_target_pairs={{0,1},{1,2},{2,3},{3,4},{4,5},{5,6},{6,7},{7,8},{8,9},{9,10},{10,1... | collective-permute-start | bytes 4792328 | tf_op jit(solution)/shard_map/ppermute | solution.py:13
  81.4 1.3 fusion.16
  84.6 3.6 %conditional.8 = (f32[1024]{0:T(1024)S(1)}, f32[1024]{0:T(1024)S(1)}) conditional(s32[]{:T(128)} %convert_element_type.76, () %tuple.127, (s32[4]{0:T(128)S(1)}, s32[4]{0:T(128)S(1)}, bf16[1024,768]{1,0:T(8,128)(2,1)S(1)}, bf16[1040,768]{1,0:T(8,128)(2,1)}) %tuple.128), branch_computations={%region_3.4_spmd, %region_4.7_spmd} | conditional | flops 1641101312 | bytes 3227892 | solution.py:72
  84.6 0.1 broadcast_bitcast_fusion
  84.7 3.5 %fusion.29 = (f32[1040]{0:T(1024)S(1)}, f32[1024]{0:T(1024)S(1)}) fusion(bf16[1024,768]{1,0:T(8,128)(2,1)S(1)} %get-tuple-element.279, bf16[1040,768]{1,0:T(8,128)(2,1)} %get-tuple-element.280, s32[1024]{0:T(1024)S(1)} %bitcast.116, s32[1040]{0:T(1024)S(1)} %concatenate.50), kind=kOutput, calls=%fused_computation.78 | convolution fusion | flops 1641101312 | bytes 3186816 | tf_op jit(solution)/shard_map/cond/branch_1_fun/dot_general | solution.py:62
  88.2 4.4 %conditional.9 = (f32[1024]{0:T(1024)S(1)}, f32[1024]{0:T(1024)S(1)}) conditional(s32[]{:T(128)} %convert_element_type.77, () %tuple.129, (s32[4]{0:T(128)S(1)}, s32[4]{0:T(128)S(1)}, bf16[1040,768]{1,0:T(8,128)(2,1)}, bf16[1040,768]{1,0:T(8,128)(2,1)}) %tuple.130), branch_computations={%region_8.9_spmd, %region_9.0_spmd} | conditional | flops 1666743552 | bytes 3269048 | solution.py:72
  88.2 0.1 broadcast_bitcast_fusion.2
  88.3 4.3 %fusion.30 = (f32[1040]{0:T(1024)S(1)}, f32[1040]{0:T(1024)S(1)}) fusion(bf16[1040,768]{1,0:T(8,128)(2,1)} %get-tuple-element.283, bf16[1040,768]{1,0:T(8,128)(2,1)} %get-tuple-element.284, s32[1040]{0:T(1024)S(1)} %concatenate.52, s32[1040]{0:T(1024)S(1)} %concatenate.51), kind=kOutput, calls=%fused_computation.79 | convolution fusion | flops 1666743552 | bytes 3211520 | tf_op jit(solution)/shard_map/cond/branch_1_fun/dot_general | solution.py:62
  92.6 23.8 %collective-permute-done.4 = bf16[1040,768]{1,0:T(8,128)(2,1)} collective-permute-done((bf16[1040,768]{1,0:T(8,128)(2,1)}, bf16[1040,768]{1,0:T(8,128)(2,1)}, u32[]{:S(2)}, u32[]{:S(2)}) %collective-permute-start.4) | collective-permute-done | bytes 1597472 | tf_op jit(solution)/shard_map/ppermute | solution.py:13
  116.4 2.2 %collective-permute-done.5 = bf16[1040,768]{1,0:T(8,128)(2,1)} collective-permute-done((bf16[1040,768]{1,0:T(8,128)(2,1)}, bf16[1040,768]{1,0:T(8,128)(2,1)}, u32[]{:S(2)}, u32[]{:S(2)}) %collective-permute-start.5) | collective-permute-done | bytes 1597472 | tf_op jit(solution)/shard_map/ppermute | solution.py:13
  118.6 0.7 slice.174
  119.4 1.2 slice.173
  120.5 1.2 concatenate.69
  121.7 0.1 collective-permute-start.8
  121.8 1.0 pad_maximum_fusion.1
  122.8 6.2 %collective-permute-start.7 = (bf16[528,768]{1,0:T(8,128)(2,1)}, bf16[528,768]{1,0:T(8,128)(2,1)}, u32[]{:S(2)}, u32[]{:S(2)}) collective-permute-start(bf16[528,768]{1,0:T(8,128)(2,1)} %pad_maximum_fusion.1), channel_id=1, source_target_pairs={{1,0},{2,1},{3,2},{4,3},{5,4},{6,5},{7,6},{8,7},{9,8},{10,9},{11,1... | collective-permute-start | bytes 2433032 | tf_op jit(solution)/shard_map/ppermute | solution.py:13
  129.0 1.3 fusion.19
  131.0 1.4 fusion.24
  133.7 1.9 %collective-permute-start.6 = (f32[1024]{0:T(1024)S(1)}, f32[1024]{0:T(1024)S(1)}, u32[]{:S(2)}, u32[]{:S(2)}) collective-permute-start(f32[1024]{0:T(1024)S(1)} %max.71), channel_id=1, source_target_pairs={{0,1},{1,2},{2,3},{3,4},{4,5},{5,6},{6,7},{7,8},{8,9},{9,10},{10,1... | collective-permute-start | bytes 12296 | tf_op jit(solution)/shard_map/ppermute | solution.py:13
  135.7 4.4 %conditional.11 = (f32[1024]{0:T(1024)S(1)}, f32[1024]{0:T(1024)S(1)}) conditional(s32[]{:T(128)} %convert_element_type.83, () %tuple.134, (s32[4]{0:T(128)S(1)}, s32[4]{0:T(128)S(1)}, bf16[1040,768]{1,0:T(8,128)(2,1)}, bf16[1040,768]{1,0:T(8,128)(2,1)}) %tuple.135), branch_computations={%region_18.19_spmd, %region_19.22_spmd} | conditional | flops 1666743552 | bytes 3269048 | solution.py:72
  135.7 0.1 broadcast_bitcast_fusion.6
  135.8 4.3 %fusion.32 = (f32[1040]{0:T(1024)S(1)}, f32[1040]{0:T(1024)S(1)}) fusion(bf16[1040,768]{1,0:T(8,128)(2,1)} %get-tuple-element.291, bf16[1040,768]{1,0:T(8,128)(2,1)} %get-tuple-element.292, s32[1040]{0:T(1024)S(1)} %concatenate.55, s32[1040]{0:T(1024)S(1)} %concatenate.54), kind=kOutput, calls=%fused_computation.81 | convolution fusion | flops 1666743552 | bytes 3211520 | tf_op jit(solution)/shard_map/cond/branch_1_fun/dot_general | solution.py:62
  140.2 3.0 %collective-permute-done.8 = bf16[528,768]{1,0:T(8,128)(2,1)} collective-permute-done((bf16[528,768]{1,0:T(8,128)(2,1)S(1)}, bf16[528,768]{1,0:T(8,128)(2,1)}, u32[]{:S(2)}, u32[]{:S(2)}) %collective-permute-start.8) | collective-permute-done | bytes 811040 | tf_op jit(solution)/shard_map/ppermute | solution.py:13
  143.2 2.3 %collective-permute-done.7 = bf16[528,768]{1,0:T(8,128)(2,1)} collective-permute-done((bf16[528,768]{1,0:T(8,128)(2,1)}, bf16[528,768]{1,0:T(8,128)(2,1)}, u32[]{:S(2)}, u32[]{:S(2)}) %collective-permute-start.7) | collective-permute-done | bytes 811040 | tf_op jit(solution)/shard_map/ppermute | solution.py:13
  145.5 1.4 fusion.21
  147.5 1.3 convert_subtract_fusion
  149.5 1.9 %collective-permute-start.11 = (f32[1024]{0:T(1024)S(1)}, f32[1024]{0:T(1024)S(1)}, u32[]{:S(2)}, u32[]{:S(2)}) collective-permute-start(f32[1024]{0:T(1024)S(1)} %max.79), channel_id=1, source_target_pairs={{0,2},{1,3},{2,4},{3,5},{4,6},{5,7},{6,8},{7,9},{8,10},{9,11},{10,... | collective-permute-start | bytes 12296 | tf_op jit(solution)/shard_map/ppermute | solution.py:13
  151.5 5.1 %collective-permute-start.12 = (f32[1024]{0:T(1024)S(1)}, f32[1024]{0:T(1024)S(1)}, u32[]{:S(2)}, u32[]{:S(2)}) collective-permute-start(f32[1024]{0:T(1024)S(1)} %maximum_maximum_fusion), channel_id=1, source_target_pairs={{0,30},{1,31},{2,0},{3,1},{4,2},{5,3},{6,4},{7,5},{8,6},{9,7},{10,... | collective-permute-start | bytes 12296 | tf_op jit(solution)/shard_map/ppermute | solution.py:13
  156.6 5.8 %collective-permute-start.10 = (f32[1024]{0:T(1024)S(1)}, f32[1024]{0:T(1024)S(1)}, u32[]{:S(2)}, u32[]{:S(2)}) collective-permute-start(f32[1024]{0:T(1024)S(1)} %maximum_maximum_fusion.2), channel_id=1, source_target_pairs={{0,24},{1,25},{2,26},{3,27},{4,28},{5,29},{6,30},{7,31},{8,0},{9,1... | collective-permute-start | bytes 12296 | tf_op jit(solution)/shard_map/ppermute | solution.py:13
  162.4 1.9 %collective-permute-start.13 = (f32[512]{0:T(512)S(1)}, f32[512]{0:T(512)S(1)}, u32[]{:S(2)}, u32[]{:S(2)}) collective-permute-start(f32[512]{0:T(512)S(1)} %get-tuple-element.379), channel_id=1, source_target_pairs={{0,3},{1,4},{2,5},{3,6},{4,7},{5,8},{6,9},{7,10},{8,11},{9,12},{10... | collective-permute-start | bytes 6152 | tf_op jit(solution)/shard_map/ppermute | solution.py:13
  164.4 6.0 %collective-permute-start.14 = (f32[512]{0:T(512)S(1)}, f32[512]{0:T(512)S(1)}, u32[]{:S(2)}, u32[]{:S(2)}) collective-permute-start(f32[512]{0:T(512)S(1)} %get-tuple-element.380), channel_id=1, source_target_pairs={{0,29},{1,30},{2,31},{3,0},{4,1},{5,2},{6,3},{7,4},{8,5},{9,6},{10... | collective-permute-start | bytes 6152 | tf_op jit(solution)/shard_map/ppermute | solution.py:13
  170.4 1.4 collective-permute-done.13
  171.8 0.6 broadcast_add_fusion
  (57 shorter events, 0.3 us)
Async XLA Ops:
  0.0 1.9 %copy-start = (bf16[1024,768]{1,0:T(8,128)(2,1)S(1)}, bf16[1024,768]{1,0:T(8,128)(2,1)}, u32[]{:S(2)}) copy-start(bf16[1024,768]{1,0:T(8,128)(2,1)} %param.64) | copy-start | bytes 4718596
  1.9 0.7 copy-start.1
  2.7 74.6 %collective-permute-start.1 = (bf16[1040,768]{1,0:T(8,128)(2,1)S(1)}, bf16[1040,768]{1,0:T(8,128)(2,1)}, u32[]{:S(2)}, u32[]{:S(2)}) collective-permute-start(bf16[1040,768]{1,0:T(8,128)(2,1)S(1)} %fusion.13), channel_id=1, source_target_pairs={{0,1},{1,2},{2,3},{3,4},{4,5},{5,6},{6,7},{7,8},{8,9},{9,10},{10,1... | collective-permute-start | bytes 4792328 | tf_op jit(solution)/shard_map/ppermute | solution.py:13
  4.7 72.7 %collective-permute-start = (bf16[1040,768]{1,0:T(8,128)(2,1)S(1)}, bf16[1040,768]{1,0:T(8,128)(2,1)}, u32[]{:S(2)}, u32[]{:S(2)}) collective-permute-start(bf16[1040,768]{1,0:T(8,128)(2,1)S(1)} %fusion.13), channel_id=1, source_target_pairs={{1,0},{2,1},{3,2},{4,3},{5,4},{6,5},{7,6},{8,7},{9,8},{10,9},{11,1... | collective-permute-start | bytes 4792328 | tf_op jit(solution)/shard_map/ppermute | solution.py:13
  10.6 49.8 %collective-permute-start.2 = (bf16[512,768]{1,0:T(8,128)(2,1)S(1)}, bf16[512,768]{1,0:T(8,128)(2,1)S(1)}, u32[]{:S(2)}, u32[]{:S(2)}) collective-permute-start(bf16[512,768]{1,0:T(8,128)(2,1)S(1)} %get-tuple-element.421), channel_id=1, source_target_pairs={{0,8},{1,9},{2,10},{3,11},{4,12},{5,13},{6,14},{7,15},{8,16},{9,17... | collective-permute-start | bytes 2359304 | tf_op jit(solution)/shard_map/ppermute | solution.py:13
  12.2 65.0 %collective-permute-start.3 = (bf16[512,768]{1,0:T(8,128)(2,1)S(1)}, bf16[512,768]{1,0:T(8,128)(2,1)S(1)}, u32[]{:S(2)}, u32[]{:S(2)}) collective-permute-start(bf16[512,768]{1,0:T(8,128)(2,1)S(1)} %get-tuple-element.422), channel_id=1, source_target_pairs={{0,8},{1,9},{2,10},{3,11},{4,12},{5,13},{6,14},{7,15},{8,16},{9,17... | collective-permute-start | bytes 2359304 | tf_op jit(solution)/shard_map/ppermute | solution.py:13
  77.3 39.1 %collective-permute-start.4 = (bf16[1040,768]{1,0:T(8,128)(2,1)}, bf16[1040,768]{1,0:T(8,128)(2,1)}, u32[]{:S(2)}, u32[]{:S(2)}) collective-permute-start(bf16[1040,768]{1,0:T(8,128)(2,1)} %collective-permute-done), channel_id=1, source_target_pairs={{1,0},{2,1},{3,2},{4,3},{5,4},{6,5},{7,6},{8,7},{9,8},{10,9},{11,1... | collective-permute-start | bytes 4792328 | tf_op jit(solution)/shard_map/ppermute | solution.py:13
  79.3 39.3 %collective-permute-start.5 = (bf16[1040,768]{1,0:T(8,128)(2,1)}, bf16[1040,768]{1,0:T(8,128)(2,1)}, u32[]{:S(2)}, u32[]{:S(2)}) collective-permute-start(bf16[1040,768]{1,0:T(8,128)(2,1)} %collective-permute-done.1), channel_id=1, source_target_pairs={{0,1},{1,2},{2,3},{3,4},{4,5},{5,6},{6,7},{7,8},{8,9},{9,10},{10,1... | collective-permute-start | bytes 4792328 | tf_op jit(solution)/shard_map/ppermute | solution.py:13
  121.7 21.5 %collective-permute-start.8 = (bf16[528,768]{1,0:T(8,128)(2,1)S(1)}, bf16[528,768]{1,0:T(8,128)(2,1)}, u32[]{:S(2)}, u32[]{:S(2)}) collective-permute-start(bf16[528,768]{1,0:T(8,128)(2,1)S(1)} %concatenate.69), channel_id=1, source_target_pairs={{0,1},{1,2},{2,3},{3,4},{4,5},{5,6},{6,7},{7,8},{8,9},{9,10},{10,1... | collective-permute-start | bytes 2433032 | tf_op jit(solution)/shard_map/ppermute | solution.py:13
  122.8 22.7 %collective-permute-start.7 = (bf16[528,768]{1,0:T(8,128)(2,1)}, bf16[528,768]{1,0:T(8,128)(2,1)}, u32[]{:S(2)}, u32[]{:S(2)}) collective-permute-start(bf16[528,768]{1,0:T(8,128)(2,1)} %pad_maximum_fusion.1), channel_id=1, source_target_pairs={{1,0},{2,1},{3,2},{4,3},{5,4},{6,5},{7,6},{8,7},{9,8},{10,9},{11,1... | collective-permute-start | bytes 2433032 | tf_op jit(solution)/shard_map/ppermute | solution.py:13
  133.7 28.7 %collective-permute-start.6 = (f32[1024]{0:T(1024)S(1)}, f32[1024]{0:T(1024)S(1)}, u32[]{:S(2)}, u32[]{:S(2)}) collective-permute-start(f32[1024]{0:T(1024)S(1)} %max.71), channel_id=1, source_target_pairs={{0,1},{1,2},{2,3},{3,4},{4,5},{5,6},{6,7},{7,8},{8,9},{9,10},{10,1... | collective-permute-start | bytes 12296 | tf_op jit(solution)/shard_map/ppermute | solution.py:13
  140.1 5.4 %copy-start.2 = (s32[1,2]{1,0:T(1,128)S(1)}, s32[1,2]{1,0:T(1,128)}, u32[]{:S(2)}) copy-start(s32[1,2]{1,0:T(1,128)} %constant.408) | copy-start | bytes 28
  149.5 14.8 %collective-permute-start.11 = (f32[1024]{0:T(1024)S(1)}, f32[1024]{0:T(1024)S(1)}, u32[]{:S(2)}, u32[]{:S(2)}) collective-permute-start(f32[1024]{0:T(1024)S(1)} %max.79), channel_id=1, source_target_pairs={{0,2},{1,3},{2,4},{3,5},{4,6},{5,7},{6,8},{7,9},{8,10},{9,11},{10,... | collective-permute-start | bytes 12296 | tf_op jit(solution)/shard_map/ppermute | solution.py:13
  151.5 18.8 %collective-permute-start.12 = (f32[1024]{0:T(1024)S(1)}, f32[1024]{0:T(1024)S(1)}, u32[]{:S(2)}, u32[]{:S(2)}) collective-permute-start(f32[1024]{0:T(1024)S(1)} %maximum_maximum_fusion), channel_id=1, source_target_pairs={{0,30},{1,31},{2,0},{3,1},{4,2},{5,3},{6,4},{7,5},{8,6},{9,7},{10,... | collective-permute-start | bytes 12296 | tf_op jit(solution)/shard_map/ppermute | solution.py:13
  156.6 13.7 %collective-permute-start.10 = (f32[1024]{0:T(1024)S(1)}, f32[1024]{0:T(1024)S(1)}, u32[]{:S(2)}, u32[]{:S(2)}) collective-permute-start(f32[1024]{0:T(1024)S(1)} %maximum_maximum_fusion.2), channel_id=1, source_target_pairs={{0,24},{1,25},{2,26},{3,27},{4,28},{5,29},{6,30},{7,31},{8,0},{9,1... | collective-permute-start | bytes 12296 | tf_op jit(solution)/shard_map/ppermute | solution.py:13
  162.4 8.0 %collective-permute-start.9 = (f32[1024]{0:T(1024)S(1)}, f32[1024]{0:T(1024)S(1)}, u32[]{:S(2)}, u32[]{:S(2)}) collective-permute-start(f32[1024]{0:T(1024)S(1)} %maximum_maximum_fusion.3), channel_id=1, source_target_pairs={{0,31},{1,0},{2,1},{3,2},{4,3},{5,4},{6,5},{7,6},{8,7},{9,8},{10,9... | collective-permute-start | bytes 12296 | tf_op jit(solution)/shard_map/ppermute | solution.py:13
  162.4 9.4 %collective-permute-start.13 = (f32[512]{0:T(512)S(1)}, f32[512]{0:T(512)S(1)}, u32[]{:S(2)}, u32[]{:S(2)}) collective-permute-start(f32[512]{0:T(512)S(1)} %get-tuple-element.379), channel_id=1, source_target_pairs={{0,3},{1,4},{2,5},{3,6},{4,7},{5,8},{6,9},{7,10},{8,11},{9,12},{10... | collective-permute-start | bytes 6152 | tf_op jit(solution)/shard_map/ppermute | solution.py:13
  164.4 7.5 %collective-permute-start.14 = (f32[512]{0:T(512)S(1)}, f32[512]{0:T(512)S(1)}, u32[]{:S(2)}, u32[]{:S(2)}) collective-permute-start(f32[512]{0:T(512)S(1)} %get-tuple-element.380), channel_id=1, source_target_pairs={{0,29},{1,30},{2,31},{3,0},{4,1},{5,2},{6,3},{7,4},{8,5},{9,6},{10... | collective-permute-start | bytes 6152 | tf_op jit(solution)/shard_map/ppermute | solution.py:13

commit v3 on v0

--- a/solution.py
+++ b/solution.py
@@ -71,7 +71,8 @@
 
         return lax.cond(matched, compute, skipped, 0)
 
-    far = shift(unit, "dev", stride, cyclic=True)
+    far = jnp.concatenate([shift(unit[b * width:(b + 1) * width], "dev", stride, cyclic=True)
+                           for b in everything], axis=0)
     far_ok = [(place >= stride) | (place < m) for m in range(4)]
     ahead = [packet]
     behind = [packet]

time: 173 us -> 174 us (level)
  the two profiles are of different devices: /device:TPU:4 before, /device:TPU:22 now
where the time goes in v3:
time: 174 us; the launch traced here: 173 us
  waiting for transfers between devices  100 us (57%)
  starting transfers between devices  46.6 us (27%)
  other arithmetic  10.8 us (6%)
  matrix products  5.53 us (3%)
  between operations  5.45 us (3%)
  local copies, waits for them, and re-layouts  3.72 us (2%)
    ppermute x17, waiting for transfers between devices, shift(): return lax.ppermute(value, axis, pairs)  100 us
    ppermute x17, starting transfers between devices, shift(): return lax.ppermute(value, axis, pairs)  46.6 us
    sub x4, other arithmetic, tile(): block_reach = k * blocks + jnp.array(b_blocks, jnp.int32) - lags  5.34 us
  transfers between devices with their start and end apart: 17, of which 9 were waited for; matrix products, arithmetic and copies ran while one was open for 8% of the time, Pallas kernels for 0%

profile of v3, /device:TPU:22, one launch (start us, length us, event | category | flops | bytes accessed | tf_op | source)
XLA Modules:
  0.0 172.8 jit_solution(17846158091176327226)
XLA Ops:
  0.0 1.9 %fusion.11 = f32[1024]{0:T(1024)S(1)} fusion(bf16[1024,768]{1,0:T(8,128)(2,1)} %param.64), kind=kLoop, calls=%fused_computation.40 | loop fusion | flops 2358272 | bytes 1576960 | tf_op jit(solution)/shard_map/reduce_sum | solution.py:18
  1.9 0.3 fusion.12
  2.3 0.3 copy-done.1
  2.6 0.1 fusion.13
  2.7 2.0 %collective-permute-start.1 = (bf16[1040,768]{1,0:T(8,128)(2,1)S(1)}, bf16[1040,768]{1,0:T(8,128)(2,1)}, u32[]{:S(2)}, u32[]{:S(2)}) collective-permute-start(bf16[1040,768]{1,0:T(8,128)(2,1)S(1)} %fusion.13), channel_id=1, source_target_pairs={{0,1},{1,2},{2,3},{3,4},{4,5},{5,6},{6,7},{7,8},{8,9},{9,10},{10,1... | collective-permute-start | bytes 4792328 | tf_op jit(solution)/shard_map/ppermute | solution.py:13
  4.7 6.1 %collective-permute-start = (bf16[1040,768]{1,0:T(8,128)(2,1)S(1)}, bf16[1040,768]{1,0:T(8,128)(2,1)}, u32[]{:S(2)}, u32[]{:S(2)}) collective-permute-start(bf16[1040,768]{1,0:T(8,128)(2,1)S(1)} %fusion.13), channel_id=1, source_target_pairs={{1,0},{2,1},{3,2},{4,3},{5,4},{6,5},{7,6},{8,7},{9,8},{10,9},{11,1... | collective-permute-start | bytes 4792328 | tf_op jit(solution)/shard_map/ppermute | solution.py:13
  10.8 0.1 fusion.36
  10.9 0.1 collective-permute-start.2
  11.0 1.7 collective-permute-start.5
  12.7 1.5 collective-permute-start.4
  14.2 0.1 broadcast_bitcast_fusion.16
  14.2 38.1 %collective-permute-done.2 = bf16[256,768]{1,0:T(8,128)(2,1)S(1)} collective-permute-done((bf16[256,768]{1,0:T(8,128)(2,1)S(1)}, bf16[256,768]{1,0:T(8,128)(2,1)S(1)}, u32[]{:S(2)}, u32[]{:S(2)}) %collective-permute-start.2) | collective-permute-done | bytes 393248 | tf_op jit(solution)/shard_map/ppermute | solution.py:13
  52.3 2.4 %collective-permute-start.3 = (bf16[256,768]{1,0:T(8,128)(2,1)S(1)}, bf16[256,768]{1,0:T(8,128)(2,1)S(1)}, u32[]{:S(2)}, u32[]{:S(2)}) collective-permute-start(bf16[256,768]{1,0:T(8,128)(2,1)S(1)} %get-tuple-element.424), channel_id=1, source_target_pairs={{0,8},{1,9},{2,10},{3,11},{4,12},{5,13},{6,14},{7,15},{8,16},{9,17... | collective-permute-start | bytes 1179656 | tf_op jit(solution)/shard_map/ppermute | solution.py:13
  54.7 2.1 %select_reduce_fusion = f32[1024]{0:T(1024)S(1)} fusion(s32[1024]{0:T(1024)S(1)} %bitcast.116, bf16[1024,768]{1,0:T(8,128)(2,1)S(1)} %fusion.12), kind=kOutput, calls=%fused_computation.33 | convolution fusion | flops 1616903168 | bytes 1581056 | tf_op jit(solution)/shard_map/dot_general | solution.py:35
  56.8 4.0 %collective-permute-done.5 = bf16[256,768]{1,0:T(8,128)(2,1)S(1)} collective-permute-done((bf16[256,768]{1,0:T(8,128)(2,1)S(1)}, bf16[256,768]{1,0:T(8,128)(2,1)S(1)}, u32[]{:S(2)}, u32[]{:S(2)}) %collective-permute-start.5) | collective-permute-done | bytes 393248 | tf_op jit(solution)/shard_map/ppermute | solution.py:13
  60.7 8.4 %collective-permute-done.4 = bf16[256,768]{1,0:T(8,128)(2,1)S(1)} collective-permute-done((bf16[256,768]{1,0:T(8,128)(2,1)S(1)}, bf16[256,768]{1,0:T(8,128)(2,1)S(1)}, u32[]{:S(2)}, u32[]{:S(2)}) %collective-permute-start.4) | collective-permute-done | bytes 393248 | tf_op jit(solution)/shard_map/ppermute | solution.py:13
  69.2 8.3 %collective-permute-done.3 = bf16[256,768]{1,0:T(8,128)(2,1)S(1)} collective-permute-done((bf16[256,768]{1,0:T(8,128)(2,1)S(1)}, bf16[256,768]{1,0:T(8,128)(2,1)S(1)}, u32[]{:S(2)}, u32[]{:S(2)}) %collective-permute-start.3) | collective-permute-done | bytes 393248 | tf_op jit(solution)/shard_map/ppermute | solution.py:13
  77.5 0.1 pad_maximum_fusion
  77.6 1.9 %collective-permute-start.6 = (bf16[1040,768]{1,0:T(8,128)(2,1)}, bf16[1040,768]{1,0:T(8,128)(2,1)}, u32[]{:S(2)}, u32[]{:S(2)}) collective-permute-start(bf16[1040,768]{1,0:T(8,128)(2,1)} %collective-permute-done), channel_id=1, source_target_pairs={{1,0},{2,1},{3,2},{4,3},{5,4},{6,5},{7,6},{8,7},{9,8},{10,9},{11,1... | collective-permute-start | bytes 4792328 | tf_op jit(solution)/shard_map/ppermute | solution.py:13
  79.6 2.1 %collective-permute-start.7 = (bf16[1040,768]{1,0:T(8,128)(2,1)}, bf16[1040,768]{1,0:T(8,128)(2,1)}, u32[]{:S(2)}, u32[]{:S(2)}) collective-permute-start(bf16[1040,768]{1,0:T(8,128)(2,1)} %collective-permute-done.1), channel_id=1, source_target_pairs={{0,1},{1,2},{2,3},{3,4},{4,5},{5,6},{6,7},{7,8},{8,9},{9,10},{10,1... | collective-permute-start | bytes 4792328 | tf_op jit(solution)/shard_map/ppermute | solution.py:13
  81.7 1.3 fusion.16
  84.8 3.6 %conditional.8 = (f32[1024]{0:T(1024)S(1)}, f32[1024]{0:T(1024)S(1)}) conditional(s32[]{:T(128)} %convert_element_type.76, () %tuple.127, (s32[4]{0:T(128)S(1)}, s32[4]{0:T(128)S(1)}, bf16[1024,768]{1,0:T(8,128)(2,1)S(1)}, bf16[1040,768]{1,0:T(8,128)(2,1)}) %tuple.128), branch_computations={%region_3.4_spmd, %region_4.7_spmd} | conditional | flops 1641101312 | bytes 3227892 | solution.py:72
  84.9 0.1 broadcast_bitcast_fusion
  85.0 3.5 %fusion.29 = (f32[1040]{0:T(1024)S(1)}, f32[1024]{0:T(1024)S(1)}) fusion(bf16[1024,768]{1,0:T(8,128)(2,1)S(1)} %get-tuple-element.279, bf16[1040,768]{1,0:T(8,128)(2,1)} %get-tuple-element.280, s32[1024]{0:T(1024)S(1)} %bitcast.117, s32[1040]{0:T(1024)S(1)} %concatenate.50), kind=kOutput, calls=%fused_computation.78 | convolution fusion | flops 1641101312 | bytes 3186816 | tf_op jit(solution)/shard_map/cond/branch_1_fun/dot_general | solution.py:62
  88.5 0.2 conditional.10
  88.7 28.0 %collective-permute-done.6 = bf16[1040,768]{1,0:T(8,128)(2,1)} collective-permute-done((bf16[1040,768]{1,0:T(8,128)(2,1)}, bf16[1040,768]{1,0:T(8,128)(2,1)}, u32[]{:S(2)}, u32[]{:S(2)}) %collective-permute-start.6) | collective-permute-done | bytes 1597472 | tf_op jit(solution)/shard_map/ppermute | solution.py:13
  116.7 2.2 %collective-permute-done.7 = bf16[1040,768]{1,0:T(8,128)(2,1)} collective-permute-done((bf16[1040,768]{1,0:T(8,128)(2,1)}, bf16[1040,768]{1,0:T(8,128)(2,1)}, u32[]{:S(2)}, u32[]{:S(2)}) %collective-permute-start.7) | collective-permute-done | bytes 1597472 | tf_op jit(solution)/shard_map/ppermute | solution.py:13
  118.9 0.7 slice.182
  119.7 1.2 slice.181
  120.8 1.2 concatenate.69
  122.0 0.1 collective-permute-start.10
  122.1 1.0 pad_maximum_fusion.1
  123.1 6.0 %collective-permute-start.9 = (bf16[528,768]{1,0:T(8,128)(2,1)}, bf16[528,768]{1,0:T(8,128)(2,1)}, u32[]{:S(2)}, u32[]{:S(2)}) collective-permute-start(bf16[528,768]{1,0:T(8,128)(2,1)} %pad_maximum_fusion.1), channel_id=1, source_target_pairs={{1,0},{2,1},{3,2},{4,3},{5,4},{6,5},{7,6},{8,7},{9,8},{10,9},{11,1... | collective-permute-start | bytes 2433032 | tf_op jit(solution)/shard_map/ppermute | solution.py:13
  129.1 1.3 fusion.19
  131.1 1.4 fusion.24
  133.9 1.9 %collective-permute-start.8 = (f32[1024]{0:T(1024)S(1)}, f32[1024]{0:T(1024)S(1)}, u32[]{:S(2)}, u32[]{:S(2)}) collective-permute-start(f32[1024]{0:T(1024)S(1)} %max.71), channel_id=1, source_target_pairs={{0,1},{1,2},{2,3},{3,4},{4,5},{5,6},{6,7},{7,8},{8,9},{9,10},{10,1... | collective-permute-start | bytes 12296 | tf_op jit(solution)/shard_map/ppermute | solution.py:13
  135.9 7.6 %collective-permute-done.10 = bf16[528,768]{1,0:T(8,128)(2,1)} collective-permute-done((bf16[528,768]{1,0:T(8,128)(2,1)S(1)}, bf16[528,768]{1,0:T(8,128)(2,1)}, u32[]{:S(2)}, u32[]{:S(2)}) %collective-permute-start.10) | collective-permute-done | bytes 811040 | tf_op jit(solution)/shard_map/ppermute | solution.py:13
  143.5 2.3 %collective-permute-done.9 = bf16[528,768]{1,0:T(8,128)(2,1)} collective-permute-done((bf16[528,768]{1,0:T(8,128)(2,1)}, bf16[528,768]{1,0:T(8,128)(2,1)}, u32[]{:S(2)}, u32[]{:S(2)}) %collective-permute-start.9) | collective-permute-done | bytes 811040 | tf_op jit(solution)/shard_map/ppermute | solution.py:13
  145.8 1.4 fusion.21
  147.8 1.3 convert_subtract_fusion
  149.8 1.9 %collective-permute-start.13 = (f32[1024]{0:T(1024)S(1)}, f32[1024]{0:T(1024)S(1)}, u32[]{:S(2)}, u32[]{:S(2)}) collective-permute-start(f32[1024]{0:T(1024)S(1)} %max.79), channel_id=1, source_target_pairs={{0,2},{1,3},{2,4},{3,5},{4,6},{5,7},{6,8},{7,9},{8,10},{9,11},{10,... | collective-permute-start | bytes 12296 | tf_op jit(solution)/shard_map/ppermute | solution.py:13
  151.8 5.1 %collective-permute-start.14 = (f32[1024]{0:T(1024)S(1)}, f32[1024]{0:T(1024)S(1)}, u32[]{:S(2)}, u32[]{:S(2)}) collective-permute-start(f32[1024]{0:T(1024)S(1)} %maximum_maximum_fusion), channel_id=1, source_target_pairs={{0,30},{1,31},{2,0},{3,1},{4,2},{5,3},{6,4},{7,5},{8,6},{9,7},{10,... | collective-permute-start | bytes 12296 | tf_op jit(solution)/shard_map/ppermute | solution.py:13
  156.9 0.6 collective-permute-start.12
  157.5 5.3 %collective-permute-start.11 = (f32[1024]{0:T(1024)S(1)}, f32[1024]{0:T(1024)S(1)}, u32[]{:S(2)}, u32[]{:S(2)}) collective-permute-start(f32[1024]{0:T(1024)S(1)} %maximum_maximum_fusion.3), channel_id=1, source_target_pairs={{0,31},{1,0},{2,1},{3,2},{4,3},{5,4},{6,5},{7,6},{8,7},{9,8},{10,9... | collective-permute-start | bytes 12296 | tf_op jit(solution)/shard_map/ppermute | solution.py:13
  162.8 1.9 %collective-permute-start.15 = (f32[512]{0:T(512)S(1)}, f32[512]{0:T(512)S(1)}, u32[]{:S(2)}, u32[]{:S(2)}) collective-permute-start(f32[512]{0:T(512)S(1)} %get-tuple-element.379), channel_id=1, source_target_pairs={{0,3},{1,4},{2,5},{3,6},{4,7},{5,8},{6,9},{7,10},{8,11},{9,12},{10... | collective-permute-start | bytes 6152 | tf_op jit(solution)/shard_map/ppermute | solution.py:13
  164.7 6.0 %collective-permute-start.16 = (f32[512]{0:T(512)S(1)}, f32[512]{0:T(512)S(1)}, u32[]{:S(2)}, u32[]{:S(2)}) collective-permute-start(f32[512]{0:T(512)S(1)} %get-tuple-element.380), channel_id=1, source_target_pairs={{0,29},{1,30},{2,31},{3,0},{4,1},{5,2},{6,3},{7,4},{8,5},{9,6},{10... | collective-permute-start | bytes 6152 | tf_op jit(solution)/shard_map/ppermute | solution.py:13
  170.7 1.4 collective-permute-done.15
  172.2 0.6 broadcast_add_fusion
  (49 shorter events, 0.3 us)
Async XLA Ops:
  0.0 1.9 %copy-start = (bf16[1024,768]{1,0:T(8,128)(2,1)S(1)}, bf16[1024,768]{1,0:T(8,128)(2,1)}, u32[]{:S(2)}) copy-start(bf16[1024,768]{1,0:T(8,128)(2,1)} %param.64) | copy-start | bytes 4718596
  1.9 0.7 copy-start.1
  2.7 74.9 %collective-permute-start.1 = (bf16[1040,768]{1,0:T(8,128)(2,1)S(1)}, bf16[1040,768]{1,0:T(8,128)(2,1)}, u32[]{:S(2)}, u32[]{:S(2)}) collective-permute-start(bf16[1040,768]{1,0:T(8,128)(2,1)S(1)} %fusion.13), channel_id=1, source_target_pairs={{0,1},{1,2},{2,3},{3,4},{4,5},{5,6},{6,7},{7,8},{8,9},{9,10},{10,1... | collective-permute-start | bytes 4792328 | tf_op jit(solution)/shard_map/ppermute | solution.py:13
  4.7 73.0 %collective-permute-start = (bf16[1040,768]{1,0:T(8,128)(2,1)S(1)}, bf16[1040,768]{1,0:T(8,128)(2,1)}, u32[]{:S(2)}, u32[]{:S(2)}) collective-permute-start(bf16[1040,768]{1,0:T(8,128)(2,1)S(1)} %fusion.13), channel_id=1, source_target_pairs={{1,0},{2,1},{3,2},{4,3},{5,4},{6,5},{7,6},{8,7},{9,8},{10,9},{11,1... | collective-permute-start | bytes 4792328 | tf_op jit(solution)/shard_map/ppermute | solution.py:13
  10.9 41.4 %collective-permute-start.2 = (bf16[256,768]{1,0:T(8,128)(2,1)S(1)}, bf16[256,768]{1,0:T(8,128)(2,1)S(1)}, u32[]{:S(2)}, u32[]{:S(2)}) collective-permute-start(bf16[256,768]{1,0:T(8,128)(2,1)S(1)} %get-tuple-element.421), channel_id=1, source_target_pairs={{0,8},{1,9},{2,10},{3,11},{4,12},{5,13},{6,14},{7,15},{8,16},{9,17... | collective-permute-start | bytes 1179656 | tf_op jit(solution)/shard_map/ppermute | solution.py:13
  11.0 49.7 %collective-permute-start.5 = (bf16[256,768]{1,0:T(8,128)(2,1)S(1)}, bf16[256,768]{1,0:T(8,128)(2,1)S(1)}, u32[]{:S(2)}, u32[]{:S(2)}) collective-permute-start(bf16[256,768]{1,0:T(8,128)(2,1)S(1)} %get-tuple-element.422), channel_id=1, source_target_pairs={{0,8},{1,9},{2,10},{3,11},{4,12},{5,13},{6,14},{7,15},{8,16},{9,17... | collective-permute-start | bytes 1179656 | tf_op jit(solution)/shard_map/ppermute | solution.py:13
  12.7 56.5 %collective-permute-start.4 = (bf16[256,768]{1,0:T(8,128)(2,1)S(1)}, bf16[256,768]{1,0:T(8,128)(2,1)S(1)}, u32[]{:S(2)}, u32[]{:S(2)}) collective-permute-start(bf16[256,768]{1,0:T(8,128)(2,1)S(1)} %get-tuple-element.423), channel_id=1, source_target_pairs={{0,8},{1,9},{2,10},{3,11},{4,12},{5,13},{6,14},{7,15},{8,16},{9,17... | collective-permute-start | bytes 1179656 | tf_op jit(solution)/shard_map/ppermute | solution.py:13
  52.3 25.2 %collective-permute-start.3 = (bf16[256,768]{1,0:T(8,128)(2,1)S(1)}, bf16[256,768]{1,0:T(8,128)(2,1)S(1)}, u32[]{:S(2)}, u32[]{:S(2)}) collective-permute-start(bf16[256,768]{1,0:T(8,128)(2,1)S(1)} %get-tuple-element.424), channel_id=1, source_target_pairs={{0,8},{1,9},{2,10},{3,11},{4,12},{5,13},{6,14},{7,15},{8,16},{9,17... | collective-permute-start | bytes 1179656 | tf_op jit(solution)/shard_map/ppermute | solution.py:13
  77.6 39.1 %collective-permute-start.6 = (bf16[1040,768]{1,0:T(8,128)(2,1)}, bf16[1040,768]{1,0:T(8,128)(2,1)}, u32[]{:S(2)}, u32[]{:S(2)}) collective-permute-start(bf16[1040,768]{1,0:T(8,128)(2,1)} %collective-permute-done), channel_id=1, source_target_pairs={{1,0},{2,1},{3,2},{4,3},{5,4},{6,5},{7,6},{8,7},{9,8},{10,9},{11,1... | collective-permute-start | bytes 4792328 | tf_op jit(solution)/shard_map/ppermute | solution.py:13
  79.6 39.3 %collective-permute-start.7 = (bf16[1040,768]{1,0:T(8,128)(2,1)}, bf16[1040,768]{1,0:T(8,128)(2,1)}, u32[]{:S(2)}, u32[]{:S(2)}) collective-permute-start(bf16[1040,768]{1,0:T(8,128)(2,1)} %collective-permute-done.1), channel_id=1, source_target_pairs={{0,1},{1,2},{2,3},{3,4},{4,5},{5,6},{6,7},{7,8},{8,9},{9,10},{10,1... | collective-permute-start | bytes 4792328 | tf_op jit(solution)/shard_map/ppermute | solution.py:13
  122.0 21.5 %collective-permute-start.10 = (bf16[528,768]{1,0:T(8,128)(2,1)S(1)}, bf16[528,768]{1,0:T(8,128)(2,1)}, u32[]{:S(2)}, u32[]{:S(2)}) collective-permute-start(bf16[528,768]{1,0:T(8,128)(2,1)S(1)} %concatenate.69), channel_id=1, source_target_pairs={{0,1},{1,2},{2,3},{3,4},{4,5},{5,6},{6,7},{7,8},{8,9},{9,10},{10,1... | collective-permute-start | bytes 2433032 | tf_op jit(solution)/shard_map/ppermute | solution.py:13
  123.1 22.7 %collective-permute-start.9 = (bf16[528,768]{1,0:T(8,128)(2,1)}, bf16[528,768]{1,0:T(8,128)(2,1)}, u32[]{:S(2)}, u32[]{:S(2)}) collective-permute-start(bf16[528,768]{1,0:T(8,128)(2,1)} %pad_maximum_fusion.1), channel_id=1, source_target_pairs={{1,0},{2,1},{3,2},{4,3},{5,4},{6,5},{7,6},{8,7},{9,8},{10,9},{11,1... | collective-permute-start | bytes 2433032 | tf_op jit(solution)/shard_map/ppermute | solution.py:13
  133.9 28.9 %collective-permute-start.8 = (f32[1024]{0:T(1024)S(1)}, f32[1024]{0:T(1024)S(1)}, u32[]{:S(2)}, u32[]{:S(2)}) collective-permute-start(f32[1024]{0:T(1024)S(1)} %max.71), channel_id=1, source_target_pairs={{0,1},{1,2},{2,3},{3,4},{4,5},{5,6},{6,7},{7,8},{8,9},{9,10},{10,1... | collective-permute-start | bytes 12296 | tf_op jit(solution)/shard_map/ppermute | solution.py:13
  135.9 9.9 %copy-start.2 = (s32[1,2]{1,0:T(1,128)S(1)}, s32[1,2]{1,0:T(1,128)}, u32[]{:S(2)}) copy-start(s32[1,2]{1,0:T(1,128)} %constant.408) | copy-start | bytes 28
  149.8 14.9 %collective-permute-start.13 = (f32[1024]{0:T(1024)S(1)}, f32[1024]{0:T(1024)S(1)}, u32[]{:S(2)}, u32[]{:S(2)}) collective-permute-start(f32[1024]{0:T(1024)S(1)} %max.79), channel_id=1, source_target_pairs={{0,2},{1,3},{2,4},{3,5},{4,6},{5,7},{6,8},{7,9},{8,10},{9,11},{10,... | collective-permute-start | bytes 12296 | tf_op jit(solution)/shard_map/ppermute | solution.py:13
  151.8 18.9 %collective-permute-start.14 = (f32[1024]{0:T(1024)S(1)}, f32[1024]{0:T(1024)S(1)}, u32[]{:S(2)}, u32[]{:S(2)}) collective-permute-start(f32[1024]{0:T(1024)S(1)} %maximum_maximum_fusion), channel_id=1, source_target_pairs={{0,30},{1,31},{2,0},{3,1},{4,2},{5,3},{6,4},{7,5},{8,6},{9,7},{10,... | collective-permute-start | bytes 12296 | tf_op jit(solution)/shard_map/ppermute | solution.py:13
  156.9 13.8 %collective-permute-start.12 = (f32[1024]{0:T(1024)S(1)}, f32[1024]{0:T(1024)S(1)}, u32[]{:S(2)}, u32[]{:S(2)}) collective-permute-start(f32[1024]{0:T(1024)S(1)} %maximum_maximum_fusion.2), channel_id=1, source_target_pairs={{0,24},{1,25},{2,26},{3,27},{4,28},{5,29},{6,30},{7,31},{8,0},{9,1... | collective-permute-start | bytes 12296 | tf_op jit(solution)/shard_map/ppermute | solution.py:13
  157.5 13.2 %collective-permute-start.11 = (f32[1024]{0:T(1024)S(1)}, f32[1024]{0:T(1024)S(1)}, u32[]{:S(2)}, u32[]{:S(2)}) collective-permute-start(f32[1024]{0:T(1024)S(1)} %maximum_maximum_fusion.3), channel_id=1, source_target_pairs={{0,31},{1,0},{2,1},{3,2},{4,3},{5,4},{6,5},{7,6},{8,7},{9,8},{10,9... | collective-permute-start | bytes 12296 | tf_op jit(solution)/shard_map/ppermute | solution.py:13
  162.8 9.4 %collective-permute-start.15 = (f32[512]{0:T(512)S(1)}, f32[512]{0:T(512)S(1)}, u32[]{:S(2)}, u32[]{:S(2)}) collective-permute-start(f32[512]{0:T(512)S(1)} %get-tuple-element.379), channel_id=1, source_target_pairs={{0,3},{1,4},{2,5},{3,6},{4,7},{5,8},{6,9},{7,10},{8,11},{9,12},{10... | collective-permute-start | bytes 6152 | tf_op jit(solution)/shard_map/ppermute | solution.py:13
  164.7 7.5 %collective-permute-start.16 = (f32[512]{0:T(512)S(1)}, f32[512]{0:T(512)S(1)}, u32[]{:S(2)}, u32[]{:S(2)}) collective-permute-start(f32[512]{0:T(512)S(1)} %get-tuple-element.380), channel_id=1, source_target_pairs={{0,29},{1,30},{2,31},{3,0},{4,1},{5,2},{6,3},{7,4},{8,5},{9,6},{10... | collective-permute-start | bytes 6152 | tf_op jit(solution)/shard_map/ppermute | solution.py:13

commit v4 on v2

--- a/solution.py
+++ b/solution.py
@@ -106,8 +106,16 @@
         else:
             sends[dest] = (chosen, value)
 
+    def deliver(dest, value):
+        if dest[0] == "ahead":
+            return shift(value, "dev", dest[1])
+        if dest[0] == "behind":
+            return shift(value, "dev", -dest[1], cyclic=True)
+        return shift(value, "dev", -stride, cyclic=True)
+
     hops = 3
     plan = plan_of()
+    last_dests = {e[7] for e in plan if e[0] == hops} | {e[8] for e in plan if e[0] == hops}
     for hop in range(1, hops + 1):
         if hop < hops:
             a_next = shift(ahead[-1], "dev", -1)
@@ -119,8 +127,22 @@
         pieces = [tile(fetch(e[1]), e[2], fetch(e[3]), e[4], e[5], e[6]) for e in ready]
         if hop == 1:
             a_next, b_next, far, best = lax.optimization_barrier((a_next, b_next, far, best))
+        elif hop < hops:
+            a_next, b_next, pieces = lax.optimization_barrier((a_next, b_next, pieces))
         else:
-            a_next, b_next, pieces = lax.optimization_barrier((a_next, b_next, pieces))
+            for e, (row_part, column_part) in zip(ready, pieces):
+                gather(e[7], e[2], row_part)
+                gather(e[8], e[4], column_part)
+            ready = []
+            done = [dest for dest in sends if dest not in last_dests]
+            arrivals = [deliver(dest, sends[dest][1]) for dest in done]
+            kept = [dest for dest in sends if dest in last_dests]
+            a_next, b_next, arrivals, held, best = lax.optimization_barrier(
+                (a_next, b_next, arrivals, [sends[dest][1] for dest in kept], best))
+            for dest, arrived in zip(done, arrivals):
+                chosen = sends[dest][0]
+                best = best.at[chosen[0] * width:(chosen[-1] + 1) * width].max(arrived)
+            sends = {dest: (sends[dest][0], value) for dest, value in zip(kept, held)}
         for e, (row_part, column_part) in zip(ready, pieces):
             gather(e[7], e[2], row_part)
             gather(e[8], e[4], column_part)
@@ -133,13 +155,7 @@
         gather(e[8], e[4], column_part)
 
     for dest, (chosen, value) in sends.items():
-        if dest[0] == "ahead":
-            arrived = shift(value, "dev", dest[1])
-        elif dest[0] == "behind":
-            arrived = shift(value, "dev", -dest[1], cyclic=True)
-        else:
-            arrived = shift(value, "dev", -stride, cyclic=True)
-        best = best.at[chosen[0] * width:(chosen[-1] + 1) * width].max(arrived)
+        best = best.at[chosen[0] * width:(chosen[-1] + 1) * width].max(deliver(dest, value))
     return best - 2.0
 
 

time: 175 us -> 175 us (level)
  the two profiles are of different devices: /device:TPU:4 before, /device:TPU:14 now
where the time goes in v4:
time: 175 us
  waiting for transfers between devices  96.3 us (55%)
  starting transfers between devices  53.5 us (31%)
  other arithmetic  10.8 us (6%)
  matrix products  5.54 us (3%)
  between operations  5.44 us (3%)
  local copies, waits for them, and re-layouts  3.72 us (2%)
    ppermute x15, waiting for transfers between devices, shift(): return lax.ppermute(value, axis, pairs)  96.3 us
    ppermute x15, starting transfers between devices, shift(): return lax.ppermute(value, axis, pairs)  53.5 us
    sub x4, other arithmetic, tile(): block_reach = k * blocks + jnp.array(b_blocks, jnp.int32) - lags  5.35 us
  transfers between devices with their start and end apart: 15, of which 6 were waited for; matrix products, arithmetic and copies ran while one was open for 6% of the time, Pallas kernels for 0%

profile of v4, /device:TPU:14, one launch (start us, length us, event | category | flops | bytes accessed | tf_op | source)
XLA Modules:
  0.0 175.4 jit_solution(14254778917567994056)
XLA Ops:
  0.0 1.9 %fusion.11 = f32[1024]{0:T(1024)S(1)} fusion(bf16[1024,768]{1,0:T(8,128)(2,1)} %param.64), kind=kLoop, calls=%fused_computation.40 | loop fusion | flops 2358272 | bytes 1576960 | tf_op jit(solution)/shard_map/reduce_sum | solution.py:18
  1.9 0.0 copy-start.1
  1.9 0.3 fusion.12
  2.3 0.3 copy-done.1
  2.6 0.1 fusion.13
  2.7 2.0 %collective-permute-start.1 = (bf16[1040,768]{1,0:T(8,128)(2,1)S(1)}, bf16[1040,768]{1,0:T(8,128)(2,1)}, u32[]{:S(2)}, u32[]{:S(2)}) collective-permute-start(bf16[1040,768]{1,0:T(8,128)(2,1)S(1)} %fusion.13), channel_id=1, source_target_pairs={{0,1},{1,2},{2,3},{3,4},{4,5},{5,6},{6,7},{7,8},{8,9},{9,10},{10,1... | collective-permute-start | bytes 4792328 | tf_op jit(solution)/shard_map/ppermute | solution.py:13
  4.7 6.1 %collective-permute-start = (bf16[1040,768]{1,0:T(8,128)(2,1)S(1)}, bf16[1040,768]{1,0:T(8,128)(2,1)}, u32[]{:S(2)}, u32[]{:S(2)}) collective-permute-start(bf16[1040,768]{1,0:T(8,128)(2,1)S(1)} %fusion.13), channel_id=1, source_target_pairs={{1,0},{2,1},{3,2},{4,3},{5,4},{6,5},{7,6},{8,7},{9,8},{10,9},{11,1... | collective-permute-start | bytes 4792328 | tf_op jit(solution)/shard_map/ppermute | solution.py:13
  10.8 0.1 fusion.36
  10.9 0.1 collective-permute-start.2
  11.0 1.7 collective-permute-start.3
  12.7 0.1 broadcast_bitcast_fusion.16
  12.8 2.1 %select_reduce_fusion = f32[1024]{0:T(1024)S(1)} fusion(s32[1024]{0:T(1024)S(1)} %bitcast.120, bf16[1024,768]{1,0:T(8,128)(2,1)S(1)} %fusion.12), kind=kOutput, calls=%fused_computation.33 | convolution fusion | flops 1616903168 | bytes 1581056 | tf_op jit(solution)/shard_map/dot_general | solution.py:35
  14.8 45.9 %collective-permute-done.2 = bf16[512,768]{1,0:T(8,128)(2,1)S(1)} collective-permute-done((bf16[512,768]{1,0:T(8,128)(2,1)S(1)}, bf16[512,768]{1,0:T(8,128)(2,1)S(1)}, u32[]{:S(2)}, u32[]{:S(2)}) %collective-permute-start.2) | collective-permute-done | bytes 786464 | tf_op jit(solution)/shard_map/ppermute | solution.py:13
  60.7 16.8 %collective-permute-done.3 = bf16[512,768]{1,0:T(8,128)(2,1)S(1)} collective-permute-done((bf16[512,768]{1,0:T(8,128)(2,1)S(1)}, bf16[512,768]{1,0:T(8,128)(2,1)S(1)}, u32[]{:S(2)}, u32[]{:S(2)}) %collective-permute-start.3) | collective-permute-done | bytes 786464 | tf_op jit(solution)/shard_map/ppermute | solution.py:13
  77.5 0.1 pad_maximum_fusion
  77.6 0.0 collective-permute-done.1
  77.6 0.0 collective-permute-done
  77.6 1.9 %collective-permute-start.4 = (bf16[1040,768]{1,0:T(8,128)(2,1)}, bf16[1040,768]{1,0:T(8,128)(2,1)}, u32[]{:S(2)}, u32[]{:S(2)}) collective-permute-start(bf16[1040,768]{1,0:T(8,128)(2,1)} %collective-permute-done), channel_id=1, source_target_pairs={{1,0},{2,1},{3,2},{4,3},{5,4},{6,5},{7,6},{8,7},{9,8},{10,9},{11,1... | collective-permute-start | bytes 4792328 | tf_op jit(solution)/shard_map/ppermute | solution.py:13
  79.6 2.1 %collective-permute-start.5 = (bf16[1040,768]{1,0:T(8,128)(2,1)}, bf16[1040,768]{1,0:T(8,128)(2,1)}, u32[]{:S(2)}, u32[]{:S(2)}) collective-permute-start(bf16[1040,768]{1,0:T(8,128)(2,1)} %collective-permute-done.1), channel_id=1, source_target_pairs={{0,1},{1,2},{2,3},{3,4},{4,5},{5,6},{6,7},{7,8},{8,9},{9,10},{10,1... | collective-permute-start | bytes 4792328 | tf_op jit(solution)/shard_map/ppermute | solution.py:13
  81.7 1.3 fusion.16
  84.8 3.6 %conditional.8 = (f32[1024]{0:T(1024)S(1)}, f32[1024]{0:T(1024)S(1)}) conditional(s32[]{:T(128)} %convert_element_type.76, () %tuple.127, (s32[4]{0:T(128)S(1)}, s32[4]{0:T(128)S(1)}, bf16[1024,768]{1,0:T(8,128)(2,1)S(1)}, bf16[1040,768]{1,0:T(8,128)(2,1)}) %tuple.128), branch_computations={%region_3.4_spmd, %region_4.7_spmd} | conditional | flops 1641101312 | bytes 3227892 | solution.py:72
  84.9 0.1 broadcast_bitcast_fusion
  85.0 3.5 %fusion.29 = (f32[1040]{0:T(1024)S(1)}, f32[1024]{0:T(1024)S(1)}) fusion(bf16[1024,768]{1,0:T(8,128)(2,1)S(1)} %get-tuple-element.279, bf16[1040,768]{1,0:T(8,128)(2,1)} %get-tuple-element.280, s32[1024]{0:T(1024)S(1)} %bitcast.116, s32[1040]{0:T(1024)S(1)} %concatenate.50), kind=kOutput, calls=%fused_computation.76 | convolution fusion | flops 1641101312 | bytes 3186816 | tf_op jit(solution)/shard_map/cond/branch_1_fun/dot_general | solution.py:62
  88.5 28.2 %collective-permute-done.4 = bf16[1040,768]{1,0:T(8,128)(2,1)} collective-permute-done((bf16[1040,768]{1,0:T(8,128)(2,1)}, bf16[1040,768]{1,0:T(8,128)(2,1)}, u32[]{:S(2)}, u32[]{:S(2)}) %collective-permute-start.4) | collective-permute-done | bytes 1597472 | tf_op jit(solution)/shard_map/ppermute | solution.py:13
  116.7 2.2 %collective-permute-done.5 = bf16[1040,768]{1,0:T(8,128)(2,1)} collective-permute-done((bf16[1040,768]{1,0:T(8,128)(2,1)}, bf16[1040,768]{1,0:T(8,128)(2,1)}, u32[]{:S(2)}, u32[]{:S(2)}) %collective-permute-start.5) | collective-permute-done | bytes 1597472 | tf_op jit(solution)/shard_map/ppermute | solution.py:13
  118.9 0.7 slice.174
  119.7 1.2 slice.173
  120.8 1.2 concatenate.69
  122.0 0.1 collective-permute-start.7
  122.1 1.0 pad_maximum_fusion.1
  123.1 6.2 %collective-permute-start.6 = (bf16[528,768]{1,0:T(8,128)(2,1)}, bf16[528,768]{1,0:T(8,128)(2,1)}, u32[]{:S(2)}, u32[]{:S(2)}) collective-permute-start(bf16[528,768]{1,0:T(8,128)(2,1)} %pad_maximum_fusion.1), channel_id=1, source_target_pairs={{1,0},{2,1},{3,2},{4,3},{5,4},{6,5},{7,6},{8,7},{9,8},{10,9},{11,1... | collective-permute-start | bytes 2433032 | tf_op jit(solution)/shard_map/ppermute | solution.py:13
  129.3 1.4 fusion.24
  132.1 3.5 %collective-permute-start.10 = (f32[1024]{0:T(1024)S(1)}, f32[1024]{0:T(1024)S(1)}, u32[]{:S(2)}, u32[]{:S(2)}) collective-permute-start(f32[1024]{0:T(1024)S(1)} %max.73), channel_id=1, source_target_pairs={{0,2},{1,3},{2,4},{3,5},{4,6},{5,7},{6,8},{7,9},{8,10},{9,11},{10,... | collective-permute-start | bytes 12296 | tf_op jit(solution)/shard_map/ppermute | solution.py:13
  135.6 0.1 collective-permute-start.9
  135.7 6.3 %collective-permute-start.8 = (f32[1024]{0:T(1024)S(1)}, f32[1024]{0:T(1024)S(1)}, u32[]{:S(2)}, u32[]{:S(2)}) collective-permute-start(f32[1024]{0:T(1024)S(1)} %max.70), channel_id=1, source_target_pairs={{0,1},{1,2},{2,3},{3,4},{4,5},{5,6},{6,7},{7,8},{8,9},{9,10},{10,1... | collective-permute-start | bytes 12296 | tf_op jit(solution)/shard_map/ppermute | solution.py:13
  142.0 1.3 fusion.19
  144.0 0.0 copy-start.2
  144.1 0.0 collective-permute-done.10
  144.1 1.7 collective-permute-done.9
  145.8 0.0 collective-permute-done.7
  145.9 1.4 fusion.21
  147.9 1.3 convert_subtract_fusion
  149.9 2.2 %collective-permute-start.12 = (f32[1024]{0:T(1024)S(1)}, f32[1024]{0:T(1024)S(1)}, u32[]{:S(2)}, u32[]{:S(2)}) collective-permute-start(f32[1024]{0:T(1024)S(1)} %max.82), channel_id=1, source_target_pairs={{0,30},{1,31},{2,0},{3,1},{4,2},{5,3},{6,4},{7,5},{8,6},{9,7},{10,... | collective-permute-start | bytes 12296 | tf_op jit(solution)/shard_map/ppermute | solution.py:13
  152.2 13.2 %collective-permute-start.11 = (f32[1024]{0:T(1024)S(1)}, f32[1024]{0:T(1024)S(1)}, u32[]{:S(2)}, u32[]{:S(2)}) collective-permute-start(f32[1024]{0:T(1024)S(1)} %max.80), channel_id=1, source_target_pairs={{0,24},{1,25},{2,26},{3,27},{4,28},{5,29},{6,30},{7,31},{8,0},{9,1... | collective-permute-start | bytes 12296 | tf_op jit(solution)/shard_map/ppermute | solution.py:13
  165.4 1.9 %collective-permute-start.13 = (f32[512]{0:T(512)S(1)}, f32[512]{0:T(512)S(1)}, u32[]{:S(2)}, u32[]{:S(2)}) collective-permute-start(f32[512]{0:T(512)S(1)} %get-tuple-element.379), channel_id=1, source_target_pairs={{0,3},{1,4},{2,5},{3,6},{4,7},{5,8},{6,9},{7,10},{8,11},{9,12},{10... | collective-permute-start | bytes 6152 | tf_op jit(solution)/shard_map/ppermute | solution.py:13
  167.3 6.0 %collective-permute-start.14 = (f32[512]{0:T(512)S(1)}, f32[512]{0:T(512)S(1)}, u32[]{:S(2)}, u32[]{:S(2)}) collective-permute-start(f32[512]{0:T(512)S(1)} %get-tuple-element.380), channel_id=1, source_target_pairs={{0,29},{1,30},{2,31},{3,0},{4,1},{5,2},{6,3},{7,4},{8,5},{9,6},{10... | collective-permute-start | bytes 6152 | tf_op jit(solution)/shard_map/ppermute | solution.py:13
  173.3 1.4 collective-permute-done.13
  174.8 0.6 broadcast_add_fusion
  (48 shorter events, 0.4 us)
Async XLA Ops:
  0.0 1.9 %copy-start = (bf16[1024,768]{1,0:T(8,128)(2,1)S(1)}, bf16[1024,768]{1,0:T(8,128)(2,1)}, u32[]{:S(2)}) copy-start(bf16[1024,768]{1,0:T(8,128)(2,1)} %param.64) | copy-start | bytes 4718596
  1.9 0.7 copy-start.1
  2.7 74.9 %collective-permute-start.1 = (bf16[1040,768]{1,0:T(8,128)(2,1)S(1)}, bf16[1040,768]{1,0:T(8,128)(2,1)}, u32[]{:S(2)}, u32[]{:S(2)}) collective-permute-start(bf16[1040,768]{1,0:T(8,128)(2,1)S(1)} %fusion.13), channel_id=1, source_target_pairs={{0,1},{1,2},{2,3},{3,4},{4,5},{5,6},{6,7},{7,8},{8,9},{9,10},{10,1... | collective-permute-start | bytes 4792328 | tf_op jit(solution)/shard_map/ppermute | solution.py:13
  4.7 73.0 %collective-permute-start = (bf16[1040,768]{1,0:T(8,128)(2,1)S(1)}, bf16[1040,768]{1,0:T(8,128)(2,1)}, u32[]{:S(2)}, u32[]{:S(2)}) collective-permute-start(bf16[1040,768]{1,0:T(8,128)(2,1)S(1)} %fusion.13), channel_id=1, source_target_pairs={{1,0},{2,1},{3,2},{4,3},{5,4},{6,5},{7,6},{8,7},{9,8},{10,9},{11,1... | collective-permute-start | bytes 4792328 | tf_op jit(solution)/shard_map/ppermute | solution.py:13
  10.9 49.8 %collective-permute-start.2 = (bf16[512,768]{1,0:T(8,128)(2,1)S(1)}, bf16[512,768]{1,0:T(8,128)(2,1)S(1)}, u32[]{:S(2)}, u32[]{:S(2)}) collective-permute-start(bf16[512,768]{1,0:T(8,128)(2,1)S(1)} %get-tuple-element.421), channel_id=1, source_target_pairs={{0,8},{1,9},{2,10},{3,11},{4,12},{5,13},{6,14},{7,15},{8,16},{9,17... | collective-permute-start | bytes 2359304 | tf_op jit(solution)/shard_map/ppermute | solution.py:13
  11.0 66.5 %collective-permute-start.3 = (bf16[512,768]{1,0:T(8,128)(2,1)S(1)}, bf16[512,768]{1,0:T(8,128)(2,1)S(1)}, u32[]{:S(2)}, u32[]{:S(2)}) collective-permute-start(bf16[512,768]{1,0:T(8,128)(2,1)S(1)} %get-tuple-element.422), channel_id=1, source_target_pairs={{0,8},{1,9},{2,10},{3,11},{4,12},{5,13},{6,14},{7,15},{8,16},{9,17... | collective-permute-start | bytes 2359304 | tf_op jit(solution)/shard_map/ppermute | solution.py:13
  77.6 39.1 %collective-permute-start.4 = (bf16[1040,768]{1,0:T(8,128)(2,1)}, bf16[1040,768]{1,0:T(8,128)(2,1)}, u32[]{:S(2)}, u32[]{:S(2)}) collective-permute-start(bf16[1040,768]{1,0:T(8,128)(2,1)} %collective-permute-done), channel_id=1, source_target_pairs={{1,0},{2,1},{3,2},{4,3},{5,4},{6,5},{7,6},{8,7},{9,8},{10,9},{11,1... | collective-permute-start | bytes 4792328 | tf_op jit(solution)/shard_map/ppermute | solution.py:13
  79.6 39.3 %collective-permute-start.5 = (bf16[1040,768]{1,0:T(8,128)(2,1)}, bf16[1040,768]{1,0:T(8,128)(2,1)}, u32[]{:S(2)}, u32[]{:S(2)}) collective-permute-start(bf16[1040,768]{1,0:T(8,128)(2,1)} %collective-permute-done.1), channel_id=1, source_target_pairs={{0,1},{1,2},{2,3},{3,4},{4,5},{5,6},{6,7},{7,8},{8,9},{9,10},{10,1... | collective-permute-start | bytes 4792328 | tf_op jit(solution)/shard_map/ppermute | solution.py:13
  122.0 23.8 %collective-permute-start.7 = (bf16[528,768]{1,0:T(8,128)(2,1)S(1)}, bf16[528,768]{1,0:T(8,128)(2,1)}, u32[]{:S(2)}, u32[]{:S(2)}) collective-permute-start(bf16[528,768]{1,0:T(8,128)(2,1)S(1)} %concatenate.69), channel_id=1, source_target_pairs={{0,1},{1,2},{2,3},{3,4},{4,5},{5,6},{6,7},{7,8},{8,9},{9,10},{10,1... | collective-permute-start | bytes 2433032 | tf_op jit(solution)/shard_map/ppermute | solution.py:13
  123.1 22.7 %collective-permute-start.6 = (bf16[528,768]{1,0:T(8,128)(2,1)}, bf16[528,768]{1,0:T(8,128)(2,1)}, u32[]{:S(2)}, u32[]{:S(2)}) collective-permute-start(bf16[528,768]{1,0:T(8,128)(2,1)} %pad_maximum_fusion.1), channel_id=1, source_target_pairs={{1,0},{2,1},{3,2},{4,3},{5,4},{6,5},{7,6},{8,7},{9,8},{10,9},{11,1... | collective-permute-start | bytes 2433032 | tf_op jit(solution)/shard_map/ppermute | solution.py:13
  132.1 12.0 %collective-permute-start.10 = (f32[1024]{0:T(1024)S(1)}, f32[1024]{0:T(1024)S(1)}, u32[]{:S(2)}, u32[]{:S(2)}) collective-permute-start(f32[1024]{0:T(1024)S(1)} %max.73), channel_id=1, source_target_pairs={{0,2},{1,3},{2,4},{3,5},{4,6},{5,7},{6,8},{7,9},{8,10},{9,11},{10,... | collective-permute-start | bytes 12296 | tf_op jit(solution)/shard_map/ppermute | solution.py:13
  135.6 10.2 %collective-permute-start.9 = (f32[1024]{0:T(1024)S(1)}, f32[1024]{0:T(1024)S(1)}, u32[]{:S(2)}, u32[]{:S(2)}) collective-permute-start(f32[1024]{0:T(1024)S(1)} %maximum_maximum_fusion.1), channel_id=1, source_target_pairs={{0,31},{1,0},{2,1},{3,2},{4,3},{5,4},{6,5},{7,6},{8,7},{9,8},{10,9... | collective-permute-start | bytes 12296 | tf_op jit(solution)/shard_map/ppermute | solution.py:13
  135.7 10.1 %collective-permute-start.8 = (f32[1024]{0:T(1024)S(1)}, f32[1024]{0:T(1024)S(1)}, u32[]{:S(2)}, u32[]{:S(2)}) collective-permute-start(f32[1024]{0:T(1024)S(1)} %max.70), channel_id=1, source_target_pairs={{0,1},{1,2},{2,3},{3,4},{4,5},{5,6},{6,7},{7,8},{8,9},{9,10},{10,1... | collective-permute-start | bytes 12296 | tf_op jit(solution)/shard_map/ppermute | solution.py:13
  144.0 1.8 %copy-start.2 = (s32[1,2]{1,0:T(1,128)S(1)}, s32[1,2]{1,0:T(1,128)}, u32[]{:S(2)}) copy-start(s32[1,2]{1,0:T(1,128)} %constant.408) | copy-start | bytes 28
  149.9 23.4 %collective-permute-start.12 = (f32[1024]{0:T(1024)S(1)}, f32[1024]{0:T(1024)S(1)}, u32[]{:S(2)}, u32[]{:S(2)}) collective-permute-start(f32[1024]{0:T(1024)S(1)} %max.82), channel_id=1, source_target_pairs={{0,30},{1,31},{2,0},{3,1},{4,2},{5,3},{6,4},{7,5},{8,6},{9,7},{10,... | collective-permute-start | bytes 12296 | tf_op jit(solution)/shard_map/ppermute | solution.py:13
  152.2 21.1 %collective-permute-start.11 = (f32[1024]{0:T(1024)S(1)}, f32[1024]{0:T(1024)S(1)}, u32[]{:S(2)}, u32[]{:S(2)}) collective-permute-start(f32[1024]{0:T(1024)S(1)} %max.80), channel_id=1, source_target_pairs={{0,24},{1,25},{2,26},{3,27},{4,28},{5,29},{6,30},{7,31},{8,0},{9,1... | collective-permute-start | bytes 12296 | tf_op jit(solution)/shard_map/ppermute | solution.py:13
  165.4 9.4 %collective-permute-start.13 = (f32[512]{0:T(512)S(1)}, f32[512]{0:T(512)S(1)}, u32[]{:S(2)}, u32[]{:S(2)}) collective-permute-start(f32[512]{0:T(512)S(1)} %get-tuple-element.379), channel_id=1, source_target_pairs={{0,3},{1,4},{2,5},{3,6},{4,7},{5,8},{6,9},{7,10},{8,11},{9,12},{10... | collective-permute-start | bytes 6152 | tf_op jit(solution)/shard_map/ppermute | solution.py:13
  167.3 7.5 %collective-permute-start.14 = (f32[512]{0:T(512)S(1)}, f32[512]{0:T(512)S(1)}, u32[]{:S(2)}, u32[]{:S(2)}) collective-permute-start(f32[512]{0:T(512)S(1)} %get-tuple-element.380), channel_id=1, source_target_pairs={{0,29},{1,30},{2,31},{3,0},{4,1},{5,2},{6,3},{7,4},{8,5},{9,6},{10... | collective-permute-start | bytes 6152 | tf_op jit(solution)/shard_map/ppermute | solution.py:13

commit v5 on v4

--- a/solution.py
+++ b/solution.py
@@ -39,43 +39,65 @@
     lag = first_block + jnp.arange(blocks, dtype=jnp.int32) - cluster_ids
     meta = jnp.zeros((16, dim), jnp.bfloat16).at[0, :blocks].set(lag.astype(jnp.bfloat16))
     extra = meta.shape[0]
-    packet = jnp.concatenate([unit, meta], axis=0)
     everything = tuple(range(blocks))
     low, high = everything[:half], everything[half:]
+    packet = jnp.concatenate([unit[: half * width], meta, unit[half * width:]], axis=0)
+    packet_layout = low + ("lags",) + high
+    plain_layout = everything
+
+    def length(segment):
+        return extra if segment == "lags" else width
 
     def part(pk, chosen):
-        return jnp.concatenate([pk[chosen[0] * width:(chosen[-1] + 1) * width], pk[-extra:]], axis=0)
+        if chosen == low:
+            return pk[: half * width + extra], low + ("lags",)
+        return pk[half * width:], ("lags",) + high
 
-    def tile(a, a_blocks, b, b_blocks, k, valid):
-        nb = len(b_blocks)
-        lags = b[nb * width, b_blocks[0]:b_blocks[-1] + 1].astype(jnp.int32)
+    def tile(a, a_layout, b, b_layout, k, valid):
+        a_blocks = tuple(x for x in a_layout if x != "lags")
+        b_blocks = tuple(x for x in b_layout if x != "lags")
+        where = 0
+        for segment in b_layout:
+            if segment == "lags":
+                break
+            where += length(segment)
+        lags = b[where, b_blocks[0]:b_blocks[-1] + 1].astype(jnp.int32)
         block_reach = k * blocks + jnp.array(b_blocks, jnp.int32) - lags
         a_rows = jnp.concatenate([
-            jnp.repeat(jnp.array(a_blocks, jnp.int32), width),
-            jnp.full((a.shape[0] - len(a_blocks) * width,), -4 * rows, jnp.int32)])
+            jnp.full((extra,), -4 * rows, jnp.int32) if segment == "lags"
+            else jnp.full((width,), segment, jnp.int32) for segment in a_layout])
         b_rows = jnp.concatenate([
-            jnp.repeat(block_reach, width),
-            jnp.full((b.shape[0] - nb * width,), 4 * rows, jnp.int32)])
+            jnp.full((extra,), 4 * rows, jnp.int32) if segment == "lags"
+            else jnp.full((width,), 0, jnp.int32) + block_reach[b_blocks.index(segment)]
+            for segment in b_layout])
         matched = (jnp.min(block_reach) <= max(a_blocks)) & valid
+
+        def drop_lags(values, layout):
+            kept, start = [], 0
+            for segment in layout:
+                if segment != "lags":
+                    kept.append(values[start:start + width])
+                start += length(segment)
+            return jnp.concatenate(kept)
 
         def compute(unused):
             sims = jnp.dot(a, b.T, preferred_element_type=jnp.float32)
             same = b_rows[None, :] <= a_rows[:, None]
             shifted = jnp.where(same, sims + 2.0, jnp.zeros_like(sims))
-            return (jnp.max(shifted, axis=1)[: len(a_blocks) * width],
-                    jnp.max(shifted, axis=0)[: nb * width])
+            return (drop_lags(jnp.max(shifted, axis=1), a_layout),
+                    drop_lags(jnp.max(shifted, axis=0), b_layout))
 
         def skipped(unused):
             return (jnp.zeros((len(a_blocks) * width,), jnp.float32),
-                    jnp.zeros((nb * width,), jnp.float32))
+                    jnp.zeros((len(b_blocks) * width,), jnp.float32))
 
         return lax.cond(matched, compute, skipped, 0)
 
     far = jnp.concatenate([shift(unit[:half * width], "dev", stride, cyclic=True),
                            shift(unit[half * width:], "dev", stride, cyclic=True)], axis=0)
     far_ok = [(place >= stride) | (place < m) for m in range(4)]
-    ahead = [packet]
-    behind = [packet]
+    ahead = [(packet, packet_layout)]
+    behind = [(packet, packet_layout)]
     def plan_of():
         return [
             (1, ("own",), everything, ("ahead", 1), everything, 1, True, ("best",), ("ahead", 1)),
@@ -90,9 +112,9 @@
 
     def fetch(where):
         if where[0] == "own":
-            return unit
+            return unit, plain_layout
         if where[0] == "far":
-            return far
+            return far, plain_layout
         return (ahead if where[0] == "ahead" else behind)[where[1]]
 
     sends = {}
@@ -118,13 +140,15 @@
     last_dests = {e[7] for e in plan if e[0] == hops} | {e[8] for e in plan if e[0] == hops}
     for hop in range(1, hops + 1):
         if hop < hops:
-            a_next = shift(ahead[-1], "dev", -1)
-            b_next = shift(behind[-1], "dev", 1, cyclic=True)
+            a_send, a_layout = ahead[-1]
+            b_send, b_layout = behind[-1]
         else:
-            a_next = shift(part(ahead[-1], low), "dev", -1)
-            b_next = shift(part(behind[-1], high), "dev", 1, cyclic=True)
+            a_send, a_layout = part(ahead[-1][0], low)
+            b_send, b_layout = part(behind[-1][0], high)
+        a_next = shift(a_send, "dev", -1)
+        b_next = shift(b_send, "dev", 1, cyclic=True)
         ready = [entry for entry in plan if entry[0] == hop - 1]
-        pieces = [tile(fetch(e[1]), e[2], fetch(e[3]), e[4], e[5], e[6]) for e in ready]
+        pieces = [tile(*fetch(e[1]), *fetch(e[3]), e[5], e[6]) for e in ready]
         if hop == 1:
             a_next, b_next, far, best = lax.optimization_barrier((a_next, b_next, far, best))
         elif hop < hops:
@@ -146,11 +170,11 @@
         for e, (row_part, column_part) in zip(ready, pieces):
             gather(e[7], e[2], row_part)
             gather(e[8], e[4], column_part)
-        ahead.append(a_next)
-        behind.append(b_next)
+        ahead.append((a_next, a_layout))
+        behind.append((b_next, b_layout))
     ready = [entry for entry in plan if entry[0] == hops]
     for e in ready:
-        row_part, column_part = tile(fetch(e[1]), e[2], fetch(e[3]), e[4], e[5], e[6])
+        row_part, column_part = tile(*fetch(e[1]), *fetch(e[3]), e[5], e[6])
         gather(e[7], e[2], row_part)
         gather(e[8], e[4], column_part)
 

time: 175 us -> 184 us (1.051)
  the two profiles are of different devices: /device:TPU:14 before, /device:TPU:54 now
where the time goes in v5:
time: 184 us; the launch traced here: 182 us
  starting transfers between devices  80.1 us (44%)
  waiting for transfers between devices  49.4 us (27%)
  local copies, waits for them, and re-layouts  27.2 us (15%)
  other arithmetic  9.87 us (5%)
  matrix products  9.82 us (5%)
  between operations  5.64 us (3%)
    ppermute x15, starting transfers between devices, shift(): return lax.ppermute(value, axis, pairs)  80.1 us
    ppermute x15, waiting for transfers between devices, shift(): return lax.ppermute(value, axis, pairs)  49.4 us
    add x28, local copies, waits for them, and re-layouts, tile(): jnp.full((width,), 0, jnp.int32) + block_reach[b_blocks.index(segment)]  17.8 us
    dot_general x2, matrix products, compute(): sims = jnp.dot(a, b.T, preferred_element_type=jnp.float32)  7.78 us
    sub x4, other arithmetic, tile(): block_reach = k * blocks + jnp.array(b_blocks, jnp.int32) - lags  5.33 us
    slice x8, local copies, waits for them, and re-layouts, tile(): block_reach[b_blocks.index(segment)]  5.1 us
  transfers between devices with their start and end apart: 15, of which 6 were waited for; matrix products, arithmetic and copies ran while one was open for 19% of the time, Pallas kernels for 0%

profile of v5, /device:TPU:54, one launch (start us, length us, event | category | flops | bytes accessed | tf_op | source)
XLA Modules:
  0.0 182.2 jit_solution(2895807030897014438)
XLA Ops:
  0.0 1.9 %fusion.12 = f32[1024]{0:T(1024)S(1)} fusion(bf16[1024,768]{1,0:T(8,128)(2,1)} %param.56), kind=kLoop, calls=%fused_computation.36 | loop fusion | flops 2358272 | bytes 1576960 | tf_op jit(solution)/shard_map/reduce_sum | solution.py:18
  3.0 2.0 %collective-permute-start.1 = (bf16[1040,768]{1,0:T(8,128)(2,1)S(1)}, bf16[1040,768]{1,0:T(8,128)(2,1)}, u32[]{:S(2)}, u32[]{:S(2)}) collective-permute-start(bf16[1040,768]{1,0:T(8,128)(2,1)S(1)} %fusion.15), channel_id=1, source_target_pairs={{0,1},{1,2},{2,3},{3,4},{4,5},{5,6},{6,7},{7,8},{8,9},{9,10},{10,1... | collective-permute-start | bytes 4792328 | tf_op jit(solution)/shard_map/ppermute | solution.py:13
  5.0 2.0 %collective-permute-start = (bf16[1040,768]{1,0:T(8,128)(2,1)S(1)}, bf16[1040,768]{1,0:T(8,128)(2,1)}, u32[]{:S(2)}, u32[]{:S(2)}) collective-permute-start(bf16[1040,768]{1,0:T(8,128)(2,1)S(1)} %fusion.15), channel_id=1, source_target_pairs={{1,0},{2,1},{3,2},{4,3},{5,4},{6,5},{7,6},{8,7},{9,8},{10,9},{11,1... | collective-permute-start | bytes 4792328 | tf_op jit(solution)/shard_map/ppermute | solution.py:13
  7.6 1.5 collective-permute-start.3
  9.2 2.0 %select_reduce_fusion = f32[1024]{0:T(1024)S(1)} fusion(s32[1024]{0:T(1024)S(1)} %bitcast.82, bf16[1024,768]{1,0:T(8,128)(2,1)S(1)} %fusion.13), kind=kOutput, calls=%fused_computation.29 | convolution fusion | flops 1616903168 | bytes 1581056 | tf_op jit(solution)/shard_map/dot_general | solution.py:35
  11.2 16.3 %collective-permute-done.2 = bf16[512,768]{1,0:T(8,128)(2,1)S(1)} collective-permute-done((bf16[512,768]{1,0:T(8,128)(2,1)S(1)}, bf16[512,768]{1,0:T(8,128)(2,1)S(1)}, u32[]{:S(2)}, u32[]{:S(2)}) %collective-permute-start.2) | collective-permute-done | bytes 786464 | tf_op jit(solution)/shard_map/ppermute | solution.py:13
  27.5 15.3 %collective-permute-done.3 = bf16[512,768]{1,0:T(8,128)(2,1)S(1)} collective-permute-done((bf16[512,768]{1,0:T(8,128)(2,1)S(1)}, bf16[512,768]{1,0:T(8,128)(2,1)S(1)}, u32[]{:S(2)}, u32[]{:S(2)}) %collective-permute-start.3) | collective-permute-done | bytes 786464 | tf_op jit(solution)/shard_map/ppermute | solution.py:13
  43.6 36.4 %collective-permute-start.4 = (bf16[1040,768]{1,0:T(8,128)(2,1)}, bf16[1040,768]{1,0:T(8,128)(2,1)}, u32[]{:S(2)}, u32[]{:S(2)}) collective-permute-start(bf16[1040,768]{1,0:T(8,128)(2,1)} %collective-permute-done), channel_id=1, source_target_pairs={{1,0},{2,1},{3,2},{4,3},{5,4},{6,5},{7,6},{8,7},{9,8},{10,9},{11,1... | collective-permute-start | bytes 4792328 | tf_op jit(solution)/shard_map/ppermute | solution.py:13
  80.1 1.3 fusion.20
  83.3 0.7 fusion.54
  84.0 0.6 add.201
  85.2 0.6 add.199
  86.6 0.7 fusion.55
  87.3 0.6 add.196
  88.5 0.6 add.194
  89.9 0.7 fusion.53
  90.6 0.6 add.206
  91.8 0.6 add.204
  93.2 4.4 %conditional.9 = (f32[1024]{0:T(1024)S(1)}, f32[1024]{0:T(1024)S(1)}) conditional(s32[]{:T(128)} %convert_element_type.77, () %tuple.129, (s32[1040]{0:T(1024)S(1)}, bf16[1040,768]{1,0:T(8,128)(2,1)}, bf16[1040,768]{1,0:T(8,128)(2,1)}) %tuple.130), branch_computations={%region_8.9_spmd, %region_9.0_spmd} | conditional | flops 1666745600 | bytes 3244304 | solution.py:94
  93.2 4.3 %fusion.31 = (f32[1040]{0:T(1024)S(1)}, f32[1040]{0:T(1024)S(1)}) fusion(bf16[1040,768]{1,0:T(8,128)(2,1)} %get-tuple-element.213, bf16[1040,768]{1,0:T(8,128)(2,1)} %get-tuple-element.214, s32[1040]{0:T(1024)} %constant.333.clone, s32[1040]{0:T(1024)S(1)} %get-tuple-element.212), kind=kOutput, calls=%fused_computation.74 | convolution fusion | flops 1666743552 | bytes 3211520 | tf_op jit(solution)/shard_map/cond/branch_1_fun/dot_general | solution.py:84
  97.6 3.6 %conditional.8 = (f32[1024]{0:T(1024)S(1)}, f32[1024]{0:T(1024)S(1)}) conditional(s32[]{:T(128)} %convert_element_type.76, () %tuple.127, (s32[1040]{0:T(1024)S(1)}, bf16[1024,768]{1,0:T(8,128)(2,1)S(1)}, bf16[1040,768]{1,0:T(8,128)(2,1)}) %tuple.128), branch_computations={%region_3.4_spmd, %region_4.7_spmd} | conditional | flops 1641102336 | bytes 3203216 | solution.py:94
  97.6 3.5 %fusion.30 = (f32[1040]{0:T(1024)S(1)}, f32[1024]{0:T(1024)S(1)}) fusion(bf16[1024,768]{1,0:T(8,128)(2,1)S(1)} %get-tuple-element.210, bf16[1040,768]{1,0:T(8,128)(2,1)} %get-tuple-element.211, s32[1024]{0:T(1024)} %constant.328.clone, s32[1040]{0:T(1024)S(1)} %get-tuple-element.209), kind=kOutput, calls=%fused_computation.73 | convolution fusion | flops 1641101312 | bytes 3186816 | tf_op jit(solution)/shard_map/cond/branch_1_fun/dot_general | solution.py:84
  101.2 13.4 %collective-permute-done.4 = bf16[1040,768]{1,0:T(8,128)(2,1)} collective-permute-done((bf16[1040,768]{1,0:T(8,128)(2,1)}, bf16[1040,768]{1,0:T(8,128)(2,1)}, u32[]{:S(2)}, u32[]{:S(2)}) %collective-permute-start.4) | collective-permute-done | bytes 1597472 | tf_op jit(solution)/shard_map/ppermute | solution.py:13
  114.7 2.3 %collective-permute-done.5 = bf16[1040,768]{1,0:T(8,128)(2,1)} collective-permute-done((bf16[1040,768]{1,0:T(8,128)(2,1)}, bf16[1040,768]{1,0:T(8,128)(2,1)}, u32[]{:S(2)}, u32[]{:S(2)}) %collective-permute-start.5) | collective-permute-done | bytes 1597472 | tf_op jit(solution)/shard_map/ppermute | solution.py:13
  117.0 1.2 slice.358
  118.2 1.2 slice.359
  119.9 4.0 %collective-permute-start.6 = (bf16[528,768]{1,0:T(8,128)(2,1)S(1)}, bf16[528,768]{1,0:T(8,128)(2,1)}, u32[]{:S(2)}, u32[]{:S(2)}) collective-permute-start(bf16[528,768]{1,0:T(8,128)(2,1)S(1)} %slice.358), channel_id=1, source_target_pairs={{1,0},{2,1},{3,2},{4,3},{5,4},{6,5},{7,6},{8,7},{9,8},{10,9},{11,1... | collective-permute-start | bytes 2433032 | tf_op jit(solution)/shard_map/ppermute | solution.py:13
  124.0 1.3 fusion.29
  126.6 0.7 fusion.52
  127.9 0.6 add.210
  129.2 0.7 add.208
  130.0 0.7 fusion.51
  131.3 0.6 add.215
  132.5 0.7 add.213
  133.4 5.6 %collective-permute-start.10 = (f32[1024]{0:T(1024)S(1)}, f32[1024]{0:T(1024)S(1)}, u32[]{:S(2)}, u32[]{:S(2)}) collective-permute-start(f32[1024]{0:T(1024)S(1)} %max.73), channel_id=1, source_target_pairs={{0,2},{1,3},{2,4},{3,5},{4,6},{5,7},{6,8},{7,9},{8,10},{9,11},{10,... | collective-permute-start | bytes 12296 | tf_op jit(solution)/shard_map/ppermute | solution.py:13
  139.0 9.2 %collective-permute-start.9 = (f32[1024]{0:T(1024)S(1)}, f32[1024]{0:T(1024)S(1)}, u32[]{:S(2)}, u32[]{:S(2)}) collective-permute-start(f32[1024]{0:T(1024)S(1)} %maximum_maximum_fusion.1), channel_id=1, source_target_pairs={{0,31},{1,0},{2,1},{3,2},{4,3},{5,4},{6,5},{7,6},{8,7},{9,8},{10,9... | collective-permute-start | bytes 12296 | tf_op jit(solution)/shard_map/ppermute | solution.py:13
  148.3 1.9 %collective-permute-start.8 = (f32[1024]{0:T(1024)S(1)}, f32[1024]{0:T(1024)S(1)}, u32[]{:S(2)}, u32[]{:S(2)}) collective-permute-start(f32[1024]{0:T(1024)S(1)} %max.70), channel_id=1, source_target_pairs={{0,1},{1,2},{2,3},{3,4},{4,5},{5,6},{6,7},{7,8},{8,9},{9,10},{10,1... | collective-permute-start | bytes 12296 | tf_op jit(solution)/shard_map/ppermute | solution.py:13
  150.2 1.3 fusion.17
  151.5 0.6 fusion.50
  152.8 0.6 add.221
  154.6 0.7 add.218
  156.1 1.4 convert_subtract_fusion.1
  158.7 1.3 convert_subtract_fusion
  162.5 0.7 add.226
  163.9 8.2 %collective-permute-start.12 = (f32[1024]{0:T(1024)S(1)}, f32[1024]{0:T(1024)S(1)}, u32[]{:S(2)}, u32[]{:S(2)}) collective-permute-start(f32[1024]{0:T(1024)S(1)} %max.82), channel_id=1, source_target_pairs={{0,30},{1,31},{2,0},{3,1},{4,2},{5,3},{6,4},{7,5},{8,6},{9,7},{10,... | collective-permute-start | bytes 12296 | tf_op jit(solution)/shard_map/ppermute | solution.py:13
  172.2 1.9 %collective-permute-start.13 = (f32[512]{0:T(512)S(1)}, f32[512]{0:T(512)S(1)}, u32[]{:S(2)}, u32[]{:S(2)}) collective-permute-start(f32[512]{0:T(512)S(1)} %get-tuple-element.303), channel_id=1, source_target_pairs={{0,3},{1,4},{2,5},{3,6},{4,7},{5,8},{6,9},{7,10},{8,11},{9,12},{10... | collective-permute-start | bytes 6152 | tf_op jit(solution)/shard_map/ppermute | solution.py:13
  174.1 6.0 %collective-permute-start.14 = (f32[512]{0:T(512)S(1)}, f32[512]{0:T(512)S(1)}, u32[]{:S(2)}, u32[]{:S(2)}) collective-permute-start(f32[512]{0:T(512)S(1)} %get-tuple-element.304), channel_id=1, source_target_pairs={{0,29},{1,30},{2,31},{3,0},{4,1},{5,2},{6,3},{7,4},{8,5},{9,6},{10... | collective-permute-start | bytes 6152 | tf_op jit(solution)/shard_map/ppermute | solution.py:13
  180.1 1.4 collective-permute-done.13
  (88 shorter events, 15.6 us)
Async XLA Ops:
  0.0 1.9 %copy-start = (bf16[1024,768]{1,0:T(8,128)(2,1)S(1)}, bf16[1024,768]{1,0:T(8,128)(2,1)}, u32[]{:S(2)}) copy-start(bf16[1024,768]{1,0:T(8,128)(2,1)} %param.56) | copy-start | bytes 4718596
  2.3 0.7 copy-start.1
  3.0 40.0 %collective-permute-start.1 = (bf16[1040,768]{1,0:T(8,128)(2,1)S(1)}, bf16[1040,768]{1,0:T(8,128)(2,1)}, u32[]{:S(2)}, u32[]{:S(2)}) collective-permute-start(bf16[1040,768]{1,0:T(8,128)(2,1)S(1)} %fusion.15), channel_id=1, source_target_pairs={{0,1},{1,2},{2,3},{3,4},{4,5},{5,6},{6,7},{7,8},{8,9},{9,10},{10,1... | collective-permute-start | bytes 4792328 | tf_op jit(solution)/shard_map/ppermute | solution.py:13
  5.0 38.6 %collective-permute-start = (bf16[1040,768]{1,0:T(8,128)(2,1)S(1)}, bf16[1040,768]{1,0:T(8,128)(2,1)}, u32[]{:S(2)}, u32[]{:S(2)}) collective-permute-start(bf16[1040,768]{1,0:T(8,128)(2,1)S(1)} %fusion.15), channel_id=1, source_target_pairs={{1,0},{2,1},{3,2},{4,3},{5,4},{6,5},{7,6},{8,7},{9,8},{10,9},{11,1... | collective-permute-start | bytes 4792328 | tf_op jit(solution)/shard_map/ppermute | solution.py:13
  7.0 20.5 %collective-permute-start.2 = (bf16[512,768]{1,0:T(8,128)(2,1)S(1)}, bf16[512,768]{1,0:T(8,128)(2,1)S(1)}, u32[]{:S(2)}, u32[]{:S(2)}) collective-permute-start(bf16[512,768]{1,0:T(8,128)(2,1)S(1)} %get-tuple-element.359), channel_id=1, source_target_pairs={{0,8},{1,9},{2,10},{3,11},{4,12},{5,13},{6,14},{7,15},{8,16},{9,17... | collective-permute-start | bytes 2359304 | tf_op jit(solution)/shard_map/ppermute | solution.py:13
  7.6 35.3 %collective-permute-start.3 = (bf16[512,768]{1,0:T(8,128)(2,1)S(1)}, bf16[512,768]{1,0:T(8,128)(2,1)S(1)}, u32[]{:S(2)}, u32[]{:S(2)}) collective-permute-start(bf16[512,768]{1,0:T(8,128)(2,1)S(1)} %get-tuple-element.360), channel_id=1, source_target_pairs={{0,8},{1,9},{2,10},{3,11},{4,12},{5,13},{6,14},{7,15},{8,16},{9,17... | collective-permute-start | bytes 2359304 | tf_op jit(solution)/shard_map/ppermute | solution.py:13
  43.6 71.1 %collective-permute-start.4 = (bf16[1040,768]{1,0:T(8,128)(2,1)}, bf16[1040,768]{1,0:T(8,128)(2,1)}, u32[]{:S(2)}, u32[]{:S(2)}) collective-permute-start(bf16[1040,768]{1,0:T(8,128)(2,1)} %collective-permute-done), channel_id=1, source_target_pairs={{1,0},{2,1},{3,2},{4,3},{5,4},{6,5},{7,6},{8,7},{9,8},{10,9},{11,1... | collective-permute-start | bytes 4792328 | tf_op jit(solution)/shard_map/ppermute | solution.py:13
  80.0 37.0 %collective-permute-start.5 = (bf16[1040,768]{1,0:T(8,128)(2,1)}, bf16[1040,768]{1,0:T(8,128)(2,1)}, u32[]{:S(2)}, u32[]{:S(2)}) collective-permute-start(bf16[1040,768]{1,0:T(8,128)(2,1)} %collective-permute-done.1), channel_id=1, source_target_pairs={{0,1},{1,2},{2,3},{3,4},{4,5},{5,6},{6,7},{7,8},{8,9},{9,10},{10,1... | collective-permute-start | bytes 4792328 | tf_op jit(solution)/shard_map/ppermute | solution.py:13
  119.4 36.2 %collective-permute-start.7 = (bf16[528,768]{1,0:T(8,128)(2,1)S(1)}, bf16[528,768]{1,0:T(8,128)(2,1)}, u32[]{:S(2)}, u32[]{:S(2)}) collective-permute-start(bf16[528,768]{1,0:T(8,128)(2,1)S(1)} %slice.359), channel_id=1, source_target_pairs={{0,1},{1,2},{2,3},{3,4},{4,5},{5,6},{6,7},{7,8},{8,9},{9,10},{10,1... | collective-permute-start | bytes 2433032 | tf_op jit(solution)/shard_map/ppermute | solution.py:13
  119.9 35.6 %collective-permute-start.6 = (bf16[528,768]{1,0:T(8,128)(2,1)S(1)}, bf16[528,768]{1,0:T(8,128)(2,1)}, u32[]{:S(2)}, u32[]{:S(2)}) collective-permute-start(bf16[528,768]{1,0:T(8,128)(2,1)S(1)} %slice.358), channel_id=1, source_target_pairs={{1,0},{2,1},{3,2},{4,3},{5,4},{6,5},{7,6},{8,7},{9,8},{10,9},{11,1... | collective-permute-start | bytes 2433032 | tf_op jit(solution)/shard_map/ppermute | solution.py:13
  133.4 22.1 %collective-permute-start.10 = (f32[1024]{0:T(1024)S(1)}, f32[1024]{0:T(1024)S(1)}, u32[]{:S(2)}, u32[]{:S(2)}) collective-permute-start(f32[1024]{0:T(1024)S(1)} %max.73), channel_id=1, source_target_pairs={{0,2},{1,3},{2,4},{3,5},{4,6},{5,7},{6,8},{7,9},{8,10},{9,11},{10,... | collective-permute-start | bytes 12296 | tf_op jit(solution)/shard_map/ppermute | solution.py:13
  139.0 16.5 %collective-permute-start.9 = (f32[1024]{0:T(1024)S(1)}, f32[1024]{0:T(1024)S(1)}, u32[]{:S(2)}, u32[]{:S(2)}) collective-permute-start(f32[1024]{0:T(1024)S(1)} %maximum_maximum_fusion.1), channel_id=1, source_target_pairs={{0,31},{1,0},{2,1},{3,2},{4,3},{5,4},{6,5},{7,6},{8,7},{9,8},{10,9... | collective-permute-start | bytes 12296 | tf_op jit(solution)/shard_map/ppermute | solution.py:13
  148.3 7.3 %collective-permute-start.8 = (f32[1024]{0:T(1024)S(1)}, f32[1024]{0:T(1024)S(1)}, u32[]{:S(2)}, u32[]{:S(2)}) collective-permute-start(f32[1024]{0:T(1024)S(1)} %max.70), channel_id=1, source_target_pairs={{0,1},{1,2},{2,3},{3,4},{4,5},{5,6},{6,7},{7,8},{8,9},{9,10},{10,1... | collective-permute-start | bytes 12296 | tf_op jit(solution)/shard_map/ppermute | solution.py:13
  155.4 0.7 copy-start.2
  163.9 16.2 %collective-permute-start.12 = (f32[1024]{0:T(1024)S(1)}, f32[1024]{0:T(1024)S(1)}, u32[]{:S(2)}, u32[]{:S(2)}) collective-permute-start(f32[1024]{0:T(1024)S(1)} %max.82), channel_id=1, source_target_pairs={{0,30},{1,31},{2,0},{3,1},{4,2},{5,3},{6,4},{7,5},{8,6},{9,7},{10,... | collective-permute-start | bytes 12296 | tf_op jit(solution)/shard_map/ppermute | solution.py:13
  172.1 8.0 %collective-permute-start.11 = (f32[1024]{0:T(1024)S(1)}, f32[1024]{0:T(1024)S(1)}, u32[]{:S(2)}, u32[]{:S(2)}) collective-permute-start(f32[1024]{0:T(1024)S(1)} %max.80), channel_id=1, source_target_pairs={{0,24},{1,25},{2,26},{3,27},{4,28},{5,29},{6,30},{7,31},{8,0},{9,1... | collective-permute-start | bytes 12296 | tf_op jit(solution)/shard_map/ppermute | solution.py:13
  172.2 9.4 %collective-permute-start.13 = (f32[512]{0:T(512)S(1)}, f32[512]{0:T(512)S(1)}, u32[]{:S(2)}, u32[]{:S(2)}) collective-permute-start(f32[512]{0:T(512)S(1)} %get-tuple-element.303), channel_id=1, source_target_pairs={{0,3},{1,4},{2,5},{3,6},{4,7},{5,8},{6,9},{7,10},{8,11},{9,12},{10... | collective-permute-start | bytes 6152 | tf_op jit(solution)/shard_map/ppermute | solution.py:13
  174.1 7.5 %collective-permute-start.14 = (f32[512]{0:T(512)S(1)}, f32[512]{0:T(512)S(1)}, u32[]{:S(2)}, u32[]{:S(2)}) collective-permute-start(f32[512]{0:T(512)S(1)} %get-tuple-element.304), channel_id=1, source_target_pairs={{0,29},{1,30},{2,31},{3,0},{4,1},{5,2},{6,3},{7,4},{8,5},{9,6},{10... | collective-permute-start | bytes 6152 | tf_op jit(solution)/shard_map/ppermute | solution.py:13

commit v6 on v4

--- a/solution.py
+++ b/solution.py
@@ -74,8 +74,10 @@
     far = jnp.concatenate([shift(unit[:half * width], "dev", stride, cyclic=True),
                            shift(unit[half * width:], "dev", stride, cyclic=True)], axis=0)
     far_ok = [(place >= stride) | (place < m) for m in range(4)]
-    ahead = [packet]
-    behind = [packet]
+    halves = (part(packet, low), part(packet, high))
+    ahead = [halves]
+    behind = [halves]
+    joined = {}
     def plan_of():
         return [
             (1, ("own",), everything, ("ahead", 1), everything, 1, True, ("best",), ("ahead", 1)),
@@ -93,7 +95,12 @@
             return unit
         if where[0] == "far":
             return far
-        return (ahead if where[0] == "ahead" else behind)[where[1]]
+        held = (ahead if where[0] == "ahead" else behind)[where[1]]
+        if len(held) == 1:
+            return held[0]
+        if where not in joined:
+            joined[where] = jnp.concatenate([held[0][: half * width], held[1]], axis=0)
+        return joined[where]
 
     sends = {}
 
@@ -118,11 +125,11 @@
     last_dests = {e[7] for e in plan if e[0] == hops} | {e[8] for e in plan if e[0] == hops}
     for hop in range(1, hops + 1):
         if hop < hops:
-            a_next = shift(ahead[-1], "dev", -1)
-            b_next = shift(behind[-1], "dev", 1, cyclic=True)
+            a_next = tuple(shift(piece, "dev", -1) for piece in ahead[-1])
+            b_next = tuple(shift(piece, "dev", 1, cyclic=True) for piece in behind[-1])
         else:
-            a_next = shift(part(ahead[-1], low), "dev", -1)
-            b_next = shift(part(behind[-1], high), "dev", 1, cyclic=True)
+            a_next = (shift(ahead[-1][0], "dev", -1),)
+            b_next = (shift(behind[-1][1], "dev", 1, cyclic=True),)
         ready = [entry for entry in plan if entry[0] == hop - 1]
         pieces = [tile(fetch(e[1]), e[2], fetch(e[3]), e[4], e[5], e[6]) for e in ready]
         if hop == 1:

time: 175 us -> 174 us (level)
  the two profiles are of different devices: /device:TPU:14 before, /device:TPU:232 now
where the time goes in v6:
time: 174 us; the launch traced here: 172 us
  starting transfers between devices  85.2 us (49%)
  waiting for transfers between devices  40.5 us (23%)
  other arithmetic  19.6 us (11%)
  matrix products  11.7 us (7%)
  local copies, waits for them, and re-layouts  8.88 us (5%)
  between operations  5.63 us (3%)
    ppermute x19, starting transfers between devices, shift(): return lax.ppermute(value, axis, pairs)  85.2 us
    ppermute x19, waiting for transfers between devices, shift(): return lax.ppermute(value, axis, pairs)  40.5 us
    dot_general x3, matrix products, compute(): sims = jnp.dot(a, b.T, preferred_element_type=jnp.float32)  9.7 us
    concatenate x3, other arithmetic, fetch(): joined[where] = jnp.concatenate([held[0][:half * width], held[1]], axis=0)  7.15 us
    sub x4, other arithmetic, tile(): block_reach = k * blocks + jnp.array(b_blocks, jnp.int32) - lags  5.4 us
    slice x4, local copies, waits for them, and re-layouts, fetch(): joined[where] = jnp.concatenate([held[0][:half * width], held[1]], axis=0)  4.74 us
    unnamed x16, local copies, waits for them, and re-layouts  3.74 us
  transfers between devices with their start and end apart: 19, of which 6 were waited for; matrix products, arithmetic and copies ran while one was open for 18% of the time, Pallas kernels for 0%

profile of v6, /device:TPU:232, one launch (start us, length us, event | category | flops | bytes accessed | tf_op | source)
XLA Modules:
  0.0 172.1 jit_solution(7199288204498951381)
XLA Ops:
  0.0 1.9 %fusion.10 = f32[1024]{0:T(1024)S(1)} fusion(bf16[1024,768]{1,0:T(8,128)(2,1)} %param.64), kind=kLoop, calls=%fused_computation.38 | loop fusion | flops 2358272 | bytes 1576960 | tf_op jit(solution)/shard_map/reduce_sum | solution.py:18
  1.9 0.3 fusion.11
  2.4 1.6 collective-permute-start.4
  4.0 1.5 collective-permute-start.5
  5.6 2.9 %collective-permute-start = (bf16[528,768]{1,0:T(8,128)(2,1)S(1)}, bf16[528,768]{1,0:T(8,128)(2,1)}, u32[]{:S(2)}, u32[]{:S(2)}) collective-permute-start(bf16[528,768]{1,0:T(8,128)(2,1)S(1)} %get-tuple-element.436), channel_id=1, source_target_pairs={{1,0},{2,1},{3,2},{4,3},{5,4},{6,5},{7,6},{8,7},{9,8},{10,9},{11,1... | collective-permute-start | bytes 2433032 | tf_op jit(solution)/shard_map/ppermute | solution.py:13
  8.5 3.2 %collective-permute-start.2 = (bf16[528,768]{1,0:T(8,128)(2,1)S(1)}, bf16[528,768]{1,0:T(8,128)(2,1)}, u32[]{:S(2)}, u32[]{:S(2)}) collective-permute-start(bf16[528,768]{1,0:T(8,128)(2,1)S(1)} %get-tuple-element.436), channel_id=1, source_target_pairs={{0,1},{1,2},{2,3},{3,4},{4,5},{5,6},{6,7},{7,8},{8,9},{9,10},{10,1... | collective-permute-start | bytes 2433032 | tf_op jit(solution)/shard_map/ppermute | solution.py:13
  11.7 1.9 %collective-permute-start.1 = (bf16[528,768]{1,0:T(8,128)(2,1)S(1)}, bf16[528,768]{1,0:T(8,128)(2,1)}, u32[]{:S(2)}, u32[]{:S(2)}) collective-permute-start(bf16[528,768]{1,0:T(8,128)(2,1)S(1)} %get-tuple-element.435), channel_id=1, source_target_pairs={{1,0},{2,1},{3,2},{4,3},{5,4},{6,5},{7,6},{8,7},{9,8},{10,9},{11,1... | collective-permute-start | bytes 2433032 | tf_op jit(solution)/shard_map/ppermute | solution.py:13
  13.6 10.6 %collective-permute-done.4 = bf16[512,768]{1,0:T(8,128)(2,1)} collective-permute-done((bf16[512,768]{1,0:T(8,128)(2,1)S(1)}, bf16[512,768]{1,0:T(8,128)(2,1)}, u32[]{:S(2)}, u32[]{:S(2)}) %collective-permute-start.4) | collective-permute-done | bytes 786464 | tf_op jit(solution)/shard_map/ppermute | solution.py:13
  24.2 14.5 %collective-permute-start.3 = (bf16[528,768]{1,0:T(8,128)(2,1)S(1)}, bf16[528,768]{1,0:T(8,128)(2,1)}, u32[]{:S(2)}, u32[]{:S(2)}) collective-permute-start(bf16[528,768]{1,0:T(8,128)(2,1)S(1)} %get-tuple-element.435), channel_id=1, source_target_pairs={{0,1},{1,2},{2,3},{3,4},{4,5},{5,6},{6,7},{7,8},{8,9},{9,10},{10,1... | collective-permute-start | bytes 2433032 | tf_op jit(solution)/shard_map/ppermute | solution.py:13
  38.7 2.0 %select_reduce_fusion = f32[1024]{0:T(1024)S(1)} fusion(s32[1024]{0:T(1024)S(1)} %bitcast.120, bf16[1024,768]{1,0:T(8,128)(2,1)S(1)} %fusion.11), kind=kOutput, calls=%fused_computation.33 | convolution fusion | flops 1616903168 | bytes 1581056 | tf_op jit(solution)/shard_map/dot_general | solution.py:35
  40.8 2.6 %pad_maximum_fusion.4 = bf16[1024,768]{1,0:T(8,128)(2,1)} fusion(bf16[512,768]{1,0:T(8,128)(2,1)} %collective-permute-done.5, bf16[512,768]{1,0:T(8,128)(2,1)} %collective-permute-done.4), kind=kLoop, calls=%fused_computation.46 | loop fusion | flops 3145728 | bytes 3145728 | tf_op jit(solution)/shard_map/concatenate | solution.py:74
  43.4 2.9 %collective-permute-done.1 = bf16[528,768]{1,0:T(8,128)(2,1)} collective-permute-done((bf16[528,768]{1,0:T(8,128)(2,1)S(1)}, bf16[528,768]{1,0:T(8,128)(2,1)}, u32[]{:S(2)}, u32[]{:S(2)}) %collective-permute-start.1) | collective-permute-done | bytes 811040 | tf_op jit(solution)/shard_map/ppermute | solution.py:13
  46.3 7.7 %collective-permute-done.3 = bf16[528,768]{1,0:T(8,128)(2,1)} collective-permute-done((bf16[528,768]{1,0:T(8,128)(2,1)S(1)}, bf16[528,768]{1,0:T(8,128)(2,1)}, u32[]{:S(2)}, u32[]{:S(2)}) %collective-permute-start.3) | collective-permute-done | bytes 811040 | tf_op jit(solution)/shard_map/ppermute | solution.py:13
  54.0 1.9 %collective-permute-start.7 = (bf16[528,768]{1,0:T(8,128)(2,1)}, bf16[528,768]{1,0:T(8,128)(2,1)}, u32[]{:S(2)}, u32[]{:S(2)}) collective-permute-start(bf16[528,768]{1,0:T(8,128)(2,1)} %collective-permute-done.1), channel_id=1, source_target_pairs={{1,0},{2,1},{3,2},{4,3},{5,4},{6,5},{7,6},{8,7},{9,8},{10,9},{11,1... | collective-permute-start | bytes 2433032 | tf_op jit(solution)/shard_map/ppermute | solution.py:13
  56.0 20.5 %collective-permute-start.9 = (bf16[528,768]{1,0:T(8,128)(2,1)}, bf16[528,768]{1,0:T(8,128)(2,1)}, u32[]{:S(2)}, u32[]{:S(2)}) collective-permute-start(bf16[528,768]{1,0:T(8,128)(2,1)} %collective-permute-done.3), channel_id=1, source_target_pairs={{0,1},{1,2},{2,3},{3,4},{4,5},{5,6},{6,7},{7,8},{8,9},{9,10},{10,1... | collective-permute-start | bytes 2433032 | tf_op jit(solution)/shard_map/ppermute | solution.py:13
  76.4 1.9 %collective-permute-start.6 = (bf16[528,768]{1,0:T(8,128)(2,1)}, bf16[528,768]{1,0:T(8,128)(2,1)}, u32[]{:S(2)}, u32[]{:S(2)}) collective-permute-start(bf16[528,768]{1,0:T(8,128)(2,1)} %collective-permute-done), channel_id=1, source_target_pairs={{1,0},{2,1},{3,2},{4,3},{5,4},{6,5},{7,6},{8,7},{9,8},{10,9},{11,1... | collective-permute-start | bytes 2433032 | tf_op jit(solution)/shard_map/ppermute | solution.py:13
  78.3 4.2 %collective-permute-start.8 = (bf16[528,768]{1,0:T(8,128)(2,1)}, bf16[528,768]{1,0:T(8,128)(2,1)}, u32[]{:S(2)}, u32[]{:S(2)}) collective-permute-start(bf16[528,768]{1,0:T(8,128)(2,1)} %collective-permute-done.2), channel_id=1, source_target_pairs={{0,1},{1,2},{2,3},{3,4},{4,5},{5,6},{6,7},{7,8},{8,9},{9,10},{10,1... | collective-permute-start | bytes 2433032 | tf_op jit(solution)/shard_map/ppermute | solution.py:13
  82.5 1.2 slice.177
  83.7 1.2 slice.178
  84.9 1.4 fusion.17
  88.2 3.4 %pad_maximum_fusion = (bf16[1040,768]{1,0:T(8,128)(2,1)}, bf16[1040,768]{1,0:T(8,128)(2,1)}) fusion(bf16[528,768]{1,0:T(8,128)(2,1)} %collective-permute-done.1, bf16[512,768]{1,0:T(8,128)(2,1)S(1)} %slice.177, bf16[528,768]{1,0:T(8,128)(2,1)} %collective-permute-done.3, bf16[512,768]{1,0:T(8,128)(2,1)S(1)} %slice.178), kind=kLoop, calls=%fused_computation.42 | loop fusion | flops 6389760 | bytes 6389760 | tf_op jit(solution)/shard_map/concatenate | solution.py:102
  91.6 1.4 copy-done.1
  93.0 3.9 %conditional.9 = (f32[1024]{0:T(1024)S(1)}, f32[1024]{0:T(1024)S(1)}) conditional(s32[]{:T(128)} %convert_element_type.77, () %tuple.129, (s32[4]{0:T(128)S(1)}, s32[4]{0:T(128)S(1)}, bf16[1040,768]{1,0:T(8,128)(2,1)}, bf16[1040,768]{1,0:T(8,128)(2,1)S(1)}) %tuple.192), branch_computations={%region_8.9_spmd, %region_9.0_spmd} | conditional | flops 1666743552 | bytes 3269048 | solution.py:72
  93.1 3.8 %fusion.31 = (f32[1040]{0:T(1024)S(1)}, f32[1040]{0:T(1024)S(1)}) fusion(bf16[1040,768]{1,0:T(8,128)(2,1)} %get-tuple-element.283, bf16[1040,768]{1,0:T(8,128)(2,1)S(1)} %get-tuple-element.284, s32[1040]{0:T(1024)S(1)} %concatenate.58, s32[1040]{0:T(1024)S(1)} %concatenate.57), kind=kOutput, calls=%fused_computation.81 | convolution fusion | flops 1666743552 | bytes 3211520 | tf_op jit(solution)/shard_map/cond/branch_1_fun/dot_general | solution.py:62
  97.0 2.4 %conditional.8 = (f32[1024]{0:T(1024)S(1)}, f32[1024]{0:T(1024)S(1)}) conditional(s32[]{:T(128)} %convert_element_type.76, () %tuple.127, (s32[4]{0:T(128)S(1)}, s32[4]{0:T(128)S(1)}, bf16[1024,768]{1,0:T(8,128)(2,1)S(1)}, bf16[1040,768]{1,0:T(8,128)(2,1)S(1)}) %tuple.193), branch_computations={%region_3.4_spmd, %region_4.7_spmd} | conditional | flops 1641101312 | bytes 3227892 | solution.py:72
  97.2 2.1 %fusion.30 = (f32[1040]{0:T(1024)S(1)}, f32[1024]{0:T(1024)S(1)}) fusion(bf16[1024,768]{1,0:T(8,128)(2,1)S(1)} %get-tuple-element.279, bf16[1040,768]{1,0:T(8,128)(2,1)S(1)} %get-tuple-element.280, s32[1024]{0:T(1024)S(1)} %bitcast.118, s32[1040]{0:T(1024)S(1)} %concatenate.56), kind=kOutput, calls=%fused_computation.80 | convolution fusion | flops 1641101312 | bytes 3186816 | tf_op jit(solution)/shard_map/cond/branch_1_fun/dot_general | solution.py:62
  99.4 11.9 %collective-permute-done.6 = bf16[528,768]{1,0:T(8,128)(2,1)} collective-permute-done((bf16[528,768]{1,0:T(8,128)(2,1)}, bf16[528,768]{1,0:T(8,128)(2,1)}, u32[]{:S(2)}, u32[]{:S(2)}) %collective-permute-start.6) | collective-permute-done | bytes 811040 | tf_op jit(solution)/shard_map/ppermute | solution.py:13
  111.2 1.2 slice.181
  112.4 1.9 %collective-permute-start.10 = (bf16[528,768]{1,0:T(8,128)(2,1)}, bf16[528,768]{1,0:T(8,128)(2,1)}, u32[]{:S(2)}, u32[]{:S(2)}) collective-permute-start(bf16[528,768]{1,0:T(8,128)(2,1)} %collective-permute-done.6), channel_id=1, source_target_pairs={{1,0},{2,1},{3,2},{4,3},{5,4},{6,5},{7,6},{8,7},{9,8},{10,9},{11,1... | collective-permute-start | bytes 2433032 | tf_op jit(solution)/shard_map/ppermute | solution.py:13
  114.3 4.2 %collective-permute-start.11 = (bf16[528,768]{1,0:T(8,128)(2,1)}, bf16[528,768]{1,0:T(8,128)(2,1)}, u32[]{:S(2)}, u32[]{:S(2)}) collective-permute-start(bf16[528,768]{1,0:T(8,128)(2,1)} %collective-permute-done.9), channel_id=1, source_target_pairs={{0,1},{1,2},{2,3},{3,4},{4,5},{5,6},{6,7},{7,8},{8,9},{9,10},{10,1... | collective-permute-start | bytes 2433032 | tf_op jit(solution)/shard_map/ppermute | solution.py:13
  118.5 2.4 %pad_maximum_fusion.2 = bf16[1040,768]{1,0:T(8,128)(2,1)} fusion(bf16[528,768]{1,0:T(8,128)(2,1)} %collective-permute-done.7, bf16[512,768]{1,0:T(8,128)(2,1)S(1)} %slice.181), kind=kLoop, calls=%fused_computation.44 | loop fusion | flops 3194880 | bytes 3194880 | tf_op jit(solution)/shard_map/concatenate | solution.py:102
  121.0 1.4 fusion.25
  122.3 1.2 slice.182
  124.9 1.4 pad_maximum_fusion.3
  126.6 1.4 copy-done.3
  128.0 3.9 %conditional.11 = (f32[1024]{0:T(1024)S(1)}, f32[1024]{0:T(1024)S(1)}) conditional(s32[]{:T(128)} %convert_element_type.83, () %tuple.134, (s32[4]{0:T(128)S(1)}, s32[4]{0:T(128)S(1)}, bf16[1040,768]{1,0:T(8,128)(2,1)}, bf16[1040,768]{1,0:T(8,128)(2,1)S(1)}) %tuple.195), branch_computations={%region_18.19_spmd, %region_19.22_spmd} | conditional | flops 1666743552 | bytes 3269048 | solution.py:72
  128.1 3.8 %fusion.33 = (f32[1040]{0:T(1024)S(1)}, f32[1040]{0:T(1024)S(1)}) fusion(bf16[1040,768]{1,0:T(8,128)(2,1)} %get-tuple-element.291, bf16[1040,768]{1,0:T(8,128)(2,1)S(1)} %get-tuple-element.292, s32[1040]{0:T(1024)S(1)} %concatenate.61, s32[1040]{0:T(1024)S(1)} %concatenate.60), kind=kOutput, calls=%fused_computation.83 | convolution fusion | flops 1666743552 | bytes 3211520 | tf_op jit(solution)/shard_map/cond/branch_1_fun/dot_general | solution.py:62
  131.9 5.8 %collective-permute-start.14 = (f32[1024]{0:T(1024)S(1)}, f32[1024]{0:T(1024)S(1)}, u32[]{:S(2)}, u32[]{:S(2)}) collective-permute-start(f32[1024]{0:T(1024)S(1)} %max.73), channel_id=1, source_target_pairs={{0,2},{1,3},{2,4},{3,5},{4,6},{5,7},{6,8},{7,9},{8,10},{9,11},{10,... | collective-permute-start | bytes 12296 | tf_op jit(solution)/shard_map/ppermute | solution.py:13
  137.7 2.1 %collective-permute-start.13 = (f32[1024]{0:T(1024)S(1)}, f32[1024]{0:T(1024)S(1)}, u32[]{:S(2)}, u32[]{:S(2)}) collective-permute-start(f32[1024]{0:T(1024)S(1)} %maximum_maximum_fusion.1), channel_id=1, source_target_pairs={{0,31},{1,0},{2,1},{3,2},{4,3},{5,4},{6,5},{7,6},{8,7},{9,8},{10,9... | collective-permute-start | bytes 12296 | tf_op jit(solution)/shard_map/ppermute | solution.py:13
  139.8 4.0 %collective-permute-start.12 = (f32[1024]{0:T(1024)S(1)}, f32[1024]{0:T(1024)S(1)}, u32[]{:S(2)}, u32[]{:S(2)}) collective-permute-start(f32[1024]{0:T(1024)S(1)} %max.70), channel_id=1, source_target_pairs={{0,1},{1,2},{2,3},{3,4},{4,5},{5,6},{6,7},{7,8},{8,9},{9,10},{10,1... | collective-permute-start | bytes 12296 | tf_op jit(solution)/shard_map/ppermute | solution.py:13
  143.8 1.3 fusion.20
  145.9 0.5 copy-done.6
  146.5 1.4 fusion.22
  148.6 1.3 convert_subtract_fusion
  151.0 12.9 %collective-permute-start.17 = (f32[512]{0:T(512)S(1)}, f32[512]{0:T(512)S(1)}, u32[]{:S(2)}, u32[]{:S(2)}) collective-permute-start(f32[512]{0:T(512)S(1)} %get-tuple-element.387), channel_id=1, source_target_pairs={{0,3},{1,4},{2,5},{3,6},{4,7},{5,8},{6,9},{7,10},{8,11},{9,12},{10... | collective-permute-start | bytes 6152 | tf_op jit(solution)/shard_map/ppermute | solution.py:13
  164.1 1.2 collective-permute-done.17
  165.2 6.3 %collective-permute-done.18 = f32[512]{0:T(512)S(1)} collective-permute-done((f32[512]{0:T(512)S(1)}, f32[512]{0:T(512)S(1)}, u32[]{:S(2)}, u32[]{:S(2)}) %collective-permute-start.18) | collective-permute-done | bytes 2080 | tf_op jit(solution)/shard_map/ppermute | solution.py:13
  171.5 0.6 broadcast_add_fusion
  (79 shorter events, 1.6 us)
Async XLA Ops:
  0.0 1.9 %copy-start = (bf16[1024,768]{1,0:T(8,128)(2,1)S(1)}, bf16[1024,768]{1,0:T(8,128)(2,1)}, u32[]{:S(2)}) copy-start(bf16[1024,768]{1,0:T(8,128)(2,1)} %param.64) | copy-start | bytes 4718596
  2.3 3.2 %copy-start.5 = (s32[4]{0:T(128)S(1)}, s32[4]{0:T(128)}, u32[]{:S(2)}) copy-start(s32[4]{0:T(128)} %param.65) | copy-start | bytes 52
  2.4 21.8 %collective-permute-start.4 = (bf16[512,768]{1,0:T(8,128)(2,1)S(1)}, bf16[512,768]{1,0:T(8,128)(2,1)}, u32[]{:S(2)}, u32[]{:S(2)}) collective-permute-start(bf16[512,768]{1,0:T(8,128)(2,1)S(1)} %get-tuple-element.422), channel_id=1, source_target_pairs={{0,8},{1,9},{2,10},{3,11},{4,12},{5,13},{6,14},{7,15},{8,16},{9,17... | collective-permute-start | bytes 2359304 | tf_op jit(solution)/shard_map/ppermute | solution.py:13
  4.0 36.8 %collective-permute-start.5 = (bf16[512,768]{1,0:T(8,128)(2,1)S(1)}, bf16[512,768]{1,0:T(8,128)(2,1)}, u32[]{:S(2)}, u32[]{:S(2)}) collective-permute-start(bf16[512,768]{1,0:T(8,128)(2,1)S(1)} %get-tuple-element.421), channel_id=1, source_target_pairs={{0,8},{1,9},{2,10},{3,11},{4,12},{5,13},{6,14},{7,15},{8,16},{9,17... | collective-permute-start | bytes 2359304 | tf_op jit(solution)/shard_map/ppermute | solution.py:13
  5.6 37.9 %collective-permute-start = (bf16[528,768]{1,0:T(8,128)(2,1)S(1)}, bf16[528,768]{1,0:T(8,128)(2,1)}, u32[]{:S(2)}, u32[]{:S(2)}) collective-permute-start(bf16[528,768]{1,0:T(8,128)(2,1)S(1)} %get-tuple-element.436), channel_id=1, source_target_pairs={{1,0},{2,1},{3,2},{4,3},{5,4},{6,5},{7,6},{8,7},{9,8},{10,9},{11,1... | collective-permute-start | bytes 2433032 | tf_op jit(solution)/shard_map/ppermute | solution.py:13
  8.5 37.8 %collective-permute-start.2 = (bf16[528,768]{1,0:T(8,128)(2,1)S(1)}, bf16[528,768]{1,0:T(8,128)(2,1)}, u32[]{:S(2)}, u32[]{:S(2)}) collective-permute-start(bf16[528,768]{1,0:T(8,128)(2,1)S(1)} %get-tuple-element.436), channel_id=1, source_target_pairs={{0,1},{1,2},{2,3},{3,4},{4,5},{5,6},{6,7},{7,8},{8,9},{9,10},{10,1... | collective-permute-start | bytes 2433032 | tf_op jit(solution)/shard_map/ppermute | solution.py:13
  11.7 34.6 %collective-permute-start.1 = (bf16[528,768]{1,0:T(8,128)(2,1)S(1)}, bf16[528,768]{1,0:T(8,128)(2,1)}, u32[]{:S(2)}, u32[]{:S(2)}) collective-permute-start(bf16[528,768]{1,0:T(8,128)(2,1)S(1)} %get-tuple-element.435), channel_id=1, source_target_pairs={{1,0},{2,1},{3,2},{4,3},{5,4},{6,5},{7,6},{8,7},{9,8},{10,9},{11,1... | collective-permute-start | bytes 2433032 | tf_op jit(solution)/shard_map/ppermute | solution.py:13
  24.2 29.9 %collective-permute-start.3 = (bf16[528,768]{1,0:T(8,128)(2,1)S(1)}, bf16[528,768]{1,0:T(8,128)(2,1)}, u32[]{:S(2)}, u32[]{:S(2)}) collective-permute-start(bf16[528,768]{1,0:T(8,128)(2,1)S(1)} %get-tuple-element.435), channel_id=1, source_target_pairs={{0,1},{1,2},{2,3},{3,4},{4,5},{5,6},{6,7},{7,8},{8,9},{9,10},{10,1... | collective-permute-start | bytes 2433032 | tf_op jit(solution)/shard_map/ppermute | solution.py:13
  54.0 45.3 %collective-permute-start.7 = (bf16[528,768]{1,0:T(8,128)(2,1)}, bf16[528,768]{1,0:T(8,128)(2,1)}, u32[]{:S(2)}, u32[]{:S(2)}) collective-permute-start(bf16[528,768]{1,0:T(8,128)(2,1)} %collective-permute-done.1), channel_id=1, source_target_pairs={{1,0},{2,1},{3,2},{4,3},{5,4},{6,5},{7,6},{8,7},{9,8},{10,9},{11,1... | collective-permute-start | bytes 2433032 | tf_op jit(solution)/shard_map/ppermute | solution.py:13
  56.0 43.4 %collective-permute-start.9 = (bf16[528,768]{1,0:T(8,128)(2,1)}, bf16[528,768]{1,0:T(8,128)(2,1)}, u32[]{:S(2)}, u32[]{:S(2)}) collective-permute-start(bf16[528,768]{1,0:T(8,128)(2,1)} %collective-permute-done.3), channel_id=1, source_target_pairs={{0,1},{1,2},{2,3},{3,4},{4,5},{5,6},{6,7},{7,8},{8,9},{9,10},{10,1... | collective-permute-start | bytes 2433032 | tf_op jit(solution)/shard_map/ppermute | solution.py:13
  76.4 34.8 %collective-permute-start.6 = (bf16[528,768]{1,0:T(8,128)(2,1)}, bf16[528,768]{1,0:T(8,128)(2,1)}, u32[]{:S(2)}, u32[]{:S(2)}) collective-permute-start(bf16[528,768]{1,0:T(8,128)(2,1)} %collective-permute-done), channel_id=1, source_target_pairs={{1,0},{2,1},{3,2},{4,3},{5,4},{6,5},{7,6},{8,7},{9,8},{10,9},{11,1... | collective-permute-start | bytes 2433032 | tf_op jit(solution)/shard_map/ppermute | solution.py:13
  78.3 32.9 %collective-permute-start.8 = (bf16[528,768]{1,0:T(8,128)(2,1)}, bf16[528,768]{1,0:T(8,128)(2,1)}, u32[]{:S(2)}, u32[]{:S(2)}) collective-permute-start(bf16[528,768]{1,0:T(8,128)(2,1)} %collective-permute-done.2), channel_id=1, source_target_pairs={{0,1},{1,2},{2,3},{3,4},{4,5},{5,6},{6,7},{7,8},{8,9},{9,10},{10,1... | collective-permute-start | bytes 2433032 | tf_op jit(solution)/shard_map/ppermute | solution.py:13
  88.2 3.4 %copy-start.4 = (bf16[1024,768]{1,0:T(8,128)(2,1)S(1)}, bf16[1024,768]{1,0:T(8,128)(2,1)}, u32[]{:S(2)}) copy-start(bf16[1024,768]{1,0:T(8,128)(2,1)} %pad_maximum_fusion.4) | copy-start | bytes 4718596
  91.6 1.4 copy-start.1
  112.4 33.5 %collective-permute-start.10 = (bf16[528,768]{1,0:T(8,128)(2,1)}, bf16[528,768]{1,0:T(8,128)(2,1)}, u32[]{:S(2)}, u32[]{:S(2)}) collective-permute-start(bf16[528,768]{1,0:T(8,128)(2,1)} %collective-permute-done.6), channel_id=1, source_target_pairs={{1,0},{2,1},{3,2},{4,3},{5,4},{6,5},{7,6},{8,7},{9,8},{10,9},{11,1... | collective-permute-start | bytes 2433032 | tf_op jit(solution)/shard_map/ppermute | solution.py:13
  114.3 31.6 %collective-permute-start.11 = (bf16[528,768]{1,0:T(8,128)(2,1)}, bf16[528,768]{1,0:T(8,128)(2,1)}, u32[]{:S(2)}, u32[]{:S(2)}) collective-permute-start(bf16[528,768]{1,0:T(8,128)(2,1)} %collective-permute-done.9), channel_id=1, source_target_pairs={{0,1},{1,2},{2,3},{3,4},{4,5},{5,6},{6,7},{7,8},{8,9},{9,10},{10,1... | collective-permute-start | bytes 2433032 | tf_op jit(solution)/shard_map/ppermute | solution.py:13
  124.9 1.7 copy-start.2
  126.5 1.4 copy-start.3
  131.9 14.0 %collective-permute-start.14 = (f32[1024]{0:T(1024)S(1)}, f32[1024]{0:T(1024)S(1)}, u32[]{:S(2)}, u32[]{:S(2)}) collective-permute-start(f32[1024]{0:T(1024)S(1)} %max.73), channel_id=1, source_target_pairs={{0,2},{1,3},{2,4},{3,5},{4,6},{5,7},{6,8},{7,9},{8,10},{9,11},{10,... | collective-permute-start | bytes 12296 | tf_op jit(solution)/shard_map/ppermute | solution.py:13
  137.7 8.2 %collective-permute-start.13 = (f32[1024]{0:T(1024)S(1)}, f32[1024]{0:T(1024)S(1)}, u32[]{:S(2)}, u32[]{:S(2)}) collective-permute-start(f32[1024]{0:T(1024)S(1)} %maximum_maximum_fusion.1), channel_id=1, source_target_pairs={{0,31},{1,0},{2,1},{3,2},{4,3},{5,4},{6,5},{7,6},{8,7},{9,8},{10,9... | collective-permute-start | bytes 12296 | tf_op jit(solution)/shard_map/ppermute | solution.py:13
  139.8 6.1 %collective-permute-start.12 = (f32[1024]{0:T(1024)S(1)}, f32[1024]{0:T(1024)S(1)}, u32[]{:S(2)}, u32[]{:S(2)}) collective-permute-start(f32[1024]{0:T(1024)S(1)} %max.70), channel_id=1, source_target_pairs={{0,1},{1,2},{2,3},{3,4},{4,5},{5,6},{6,7},{7,8},{8,9},{9,10},{10,1... | collective-permute-start | bytes 12296 | tf_op jit(solution)/shard_map/ppermute | solution.py:13
  145.8 0.7 copy-start.6
  148.6 15.5 %collective-permute-start.15 = (f32[1024]{0:T(1024)S(1)}, f32[1024]{0:T(1024)S(1)}, u32[]{:S(2)}, u32[]{:S(2)}) collective-permute-start(f32[1024]{0:T(1024)S(1)} %max.80), channel_id=1, source_target_pairs={{0,24},{1,25},{2,26},{3,27},{4,28},{5,29},{6,30},{7,31},{8,0},{9,1... | collective-permute-start | bytes 12296 | tf_op jit(solution)/shard_map/ppermute | solution.py:13
  150.9 13.1 %collective-permute-start.16 = (f32[1024]{0:T(1024)S(1)}, f32[1024]{0:T(1024)S(1)}, u32[]{:S(2)}, u32[]{:S(2)}) collective-permute-start(f32[1024]{0:T(1024)S(1)} %max.82), channel_id=1, source_target_pairs={{0,30},{1,31},{2,0},{3,1},{4,2},{5,3},{6,4},{7,5},{8,6},{9,7},{10,... | collective-permute-start | bytes 12296 | tf_op jit(solution)/shard_map/ppermute | solution.py:13
  151.0 14.2 %collective-permute-start.17 = (f32[512]{0:T(512)S(1)}, f32[512]{0:T(512)S(1)}, u32[]{:S(2)}, u32[]{:S(2)}) collective-permute-start(f32[512]{0:T(512)S(1)} %get-tuple-element.387), channel_id=1, source_target_pairs={{0,3},{1,4},{2,5},{3,6},{4,7},{5,8},{6,9},{7,10},{8,11},{9,12},{10... | collective-permute-start | bytes 6152 | tf_op jit(solution)/shard_map/ppermute | solution.py:13
  163.9 7.6 %collective-permute-start.18 = (f32[512]{0:T(512)S(1)}, f32[512]{0:T(512)S(1)}, u32[]{:S(2)}, u32[]{:S(2)}) collective-permute-start(f32[512]{0:T(512)S(1)} %get-tuple-element.388), channel_id=1, source_target_pairs={{0,29},{1,30},{2,31},{3,0},{4,1},{5,2},{6,3},{7,4},{8,5},{9,6},{10... | collective-permute-start | bytes 6152 | tf_op jit(solution)/shard_map/ppermute | solution.py:13

commit v7 on v4

--- a/solution.py
+++ b/solution.py
@@ -46,7 +46,7 @@
     def part(pk, chosen):
         return jnp.concatenate([pk[chosen[0] * width:(chosen[-1] + 1) * width], pk[-extra:]], axis=0)
 
-    def tile(a, a_blocks, b, b_blocks, k, valid):
+    def tile(a, a_blocks, b, b_blocks, k, valid, guarded=True):
         nb = len(b_blocks)
         lags = b[nb * width, b_blocks[0]:b_blocks[-1] + 1].astype(jnp.int32)
         block_reach = k * blocks + jnp.array(b_blocks, jnp.int32) - lags
@@ -60,7 +60,7 @@
 
         def compute(unused):
             sims = jnp.dot(a, b.T, preferred_element_type=jnp.float32)
-            same = b_rows[None, :] <= a_rows[:, None]
+            same = (b_rows[None, :] <= a_rows[:, None]) & valid
             shifted = jnp.where(same, sims + 2.0, jnp.zeros_like(sims))
             return (jnp.max(shifted, axis=1)[: len(a_blocks) * width],
                     jnp.max(shifted, axis=0)[: nb * width])
@@ -69,6 +69,8 @@
             return (jnp.zeros((len(a_blocks) * width,), jnp.float32),
                     jnp.zeros((nb * width,), jnp.float32))
 
+        if not guarded:
+            return compute(0)
         return lax.cond(matched, compute, skipped, 0)
 
     far = jnp.concatenate([shift(unit[:half * width], "dev", stride, cyclic=True),
@@ -150,7 +152,7 @@
         behind.append(b_next)
     ready = [entry for entry in plan if entry[0] == hops]
     for e in ready:
-        row_part, column_part = tile(fetch(e[1]), e[2], fetch(e[3]), e[4], e[5], e[6])
+        row_part, column_part = tile(fetch(e[1]), e[2], fetch(e[3]), e[4], e[5], e[6], guarded=False)
         gather(e[7], e[2], row_part)
         gather(e[8], e[4], column_part)
 

time: 175 us -> 174 us (level)
  the two profiles are of different devices: /device:TPU:14 before, /device:TPU:4 now
where the time goes in v7:
time: 174 us; the launch traced here: 171 us
  waiting for transfers between devices  96.1 us (55%)
  starting transfers between devices  46.6 us (27%)
  matrix products  10.9 us (6%)
  other arithmetic  9.5 us (5%)
  between operations  4.16 us (2%)
  local copies, waits for them, and re-layouts  3.89 us (2%)
    ppermute x15, waiting for transfers between devices, shift(): return lax.ppermute(value, axis, pairs)  96.1 us
    ppermute x15, starting transfers between devices, shift(): return lax.ppermute(value, axis, pairs)  46.6 us
    dot_general x3, matrix products, compute(): sims = jnp.dot(a, b.T, preferred_element_type=jnp.float32)  8.88 us
    sub x4, other arithmetic, tile(): block_reach = k * blocks + jnp.array(b_blocks, jnp.int32) - lags  4.11 us
  transfers between devices with their start and end apart: 15, of which 6 were waited for; matrix products, arithmetic and copies ran while one was open for 8% of the time, Pallas kernels for 0%

profile of v7, /device:TPU:4, one launch (start us, length us, event | category | flops | bytes accessed | tf_op | source)
XLA Modules:
  0.0 171.4 jit_solution(6709466333599966778)
XLA Ops:
  0.0 1.9 %fusion.9 = f32[1024]{0:T(1024)S(1)} fusion(bf16[1024,768]{1,0:T(8,128)(2,1)} %param.60), kind=kLoop, calls=%fused_computation.33 | loop fusion | flops 2358272 | bytes 1576960 | tf_op jit(solution)/shard_map/reduce_sum | solution.py:18
  1.9 0.0 copy-start.1
  1.9 0.3 fusion.10
  2.3 0.3 copy-done.1
  2.6 0.1 fusion.13
  2.7 2.0 %collective-permute-start.1 = (bf16[1040,768]{1,0:T(8,128)(2,1)S(1)}, bf16[1040,768]{1,0:T(8,128)(2,1)}, u32[]{:S(2)}, u32[]{:S(2)}) collective-permute-start(bf16[1040,768]{1,0:T(8,128)(2,1)S(1)} %fusion.13), channel_id=1, source_target_pairs={{0,1},{1,2},{2,3},{3,4},{4,5},{5,6},{6,7},{7,8},{8,9},{9,10},{10,1... | collective-permute-start | bytes 4792328 | tf_op jit(solution)/shard_map/ppermute | solution.py:13
  4.7 5.8 %collective-permute-start = (bf16[1040,768]{1,0:T(8,128)(2,1)S(1)}, bf16[1040,768]{1,0:T(8,128)(2,1)}, u32[]{:S(2)}, u32[]{:S(2)}) collective-permute-start(bf16[1040,768]{1,0:T(8,128)(2,1)S(1)} %fusion.13), channel_id=1, source_target_pairs={{1,0},{2,1},{3,2},{4,3},{5,4},{6,5},{7,6},{8,7},{9,8},{10,9},{11,1... | collective-permute-start | bytes 4792328 | tf_op jit(solution)/shard_map/ppermute | solution.py:13
  10.5 0.1 fusion.33
  10.6 1.6 collective-permute-start.2
  12.2 0.1 collective-permute-start.3
  12.3 0.1 broadcast_bitcast_fusion.12
  12.4 2.1 %select_reduce_fusion = f32[1024]{0:T(1024)S(1)} fusion(s32[1024]{0:T(1024)S(1)} %bitcast.115, bf16[1024,768]{1,0:T(8,128)(2,1)S(1)} %fusion.10), kind=kOutput, calls=%fused_computation.24 | convolution fusion | flops 1616903168 | bytes 1581056 | tf_op jit(solution)/shard_map/dot_general | solution.py:35
  14.4 46.0 %collective-permute-done.2 = bf16[512,768]{1,0:T(8,128)(2,1)S(1)} collective-permute-done((bf16[512,768]{1,0:T(8,128)(2,1)S(1)}, bf16[512,768]{1,0:T(8,128)(2,1)S(1)}, u32[]{:S(2)}, u32[]{:S(2)}) %collective-permute-start.2) | collective-permute-done | bytes 786464 | tf_op jit(solution)/shard_map/ppermute | solution.py:13
  60.5 16.8 %collective-permute-done.3 = bf16[512,768]{1,0:T(8,128)(2,1)S(1)} collective-permute-done((bf16[512,768]{1,0:T(8,128)(2,1)S(1)}, bf16[512,768]{1,0:T(8,128)(2,1)S(1)}, u32[]{:S(2)}, u32[]{:S(2)}) %collective-permute-start.3) | collective-permute-done | bytes 786464 | tf_op jit(solution)/shard_map/ppermute | solution.py:13
  77.2 0.1 pad_maximum_fusion
  77.3 1.9 %collective-permute-start.4 = (bf16[1040,768]{1,0:T(8,128)(2,1)}, bf16[1040,768]{1,0:T(8,128)(2,1)}, u32[]{:S(2)}, u32[]{:S(2)}) collective-permute-start(bf16[1040,768]{1,0:T(8,128)(2,1)} %collective-permute-done), channel_id=1, source_target_pairs={{1,0},{2,1},{3,2},{4,3},{5,4},{6,5},{7,6},{8,7},{9,8},{10,9},{11,1... | collective-permute-start | bytes 4792328 | tf_op jit(solution)/shard_map/ppermute | solution.py:13
  79.3 2.1 %collective-permute-start.5 = (bf16[1040,768]{1,0:T(8,128)(2,1)}, bf16[1040,768]{1,0:T(8,128)(2,1)}, u32[]{:S(2)}, u32[]{:S(2)}) collective-permute-start(bf16[1040,768]{1,0:T(8,128)(2,1)} %collective-permute-done.1), channel_id=1, source_target_pairs={{0,1},{1,2},{2,3},{3,4},{4,5},{5,6},{6,7},{7,8},{8,9},{9,10},{10,1... | collective-permute-start | bytes 4792328 | tf_op jit(solution)/shard_map/ppermute | solution.py:13
  81.4 1.4 fusion.17
  84.7 3.6 %conditional.6 = (f32[1024]{0:T(1024)S(1)}, f32[1024]{0:T(1024)S(1)}) conditional(s32[]{:T(128)} %convert_element_type.70, () %tuple.111, (s32[4]{0:T(128)S(1)}, s32[4]{0:T(128)S(1)}, bf16[1024,768]{1,0:T(8,128)(2,1)S(1)}, bf16[1040,768]{1,0:T(8,128)(2,1)}) %tuple.112), branch_computations={%region_3.4_spmd, %region_4.7_spmd} | conditional | flops 1641101312 | bytes 3227892 | solution.py:74
  84.7 0.1 broadcast_bitcast_fusion
  84.8 3.5 %fusion.26 = (f32[1040]{0:T(1024)S(1)}, f32[1024]{0:T(1024)S(1)}) fusion(bf16[1024,768]{1,0:T(8,128)(2,1)S(1)} %get-tuple-element.260, bf16[1040,768]{1,0:T(8,128)(2,1)} %get-tuple-element.261, s32[1024]{0:T(1024)S(1)} %bitcast.112, s32[1040]{0:T(1024)S(1)} %concatenate.50), kind=kOutput, calls=%fused_computation.73 | convolution fusion | flops 1641101312 | bytes 3186816 | tf_op jit(solution)/shard_map/cond/branch_1_fun/dot_general | solution.py:62
  88.4 28.0 %collective-permute-done.4 = bf16[1040,768]{1,0:T(8,128)(2,1)} collective-permute-done((bf16[1040,768]{1,0:T(8,128)(2,1)}, bf16[1040,768]{1,0:T(8,128)(2,1)}, u32[]{:S(2)}, u32[]{:S(2)}) %collective-permute-start.4) | collective-permute-done | bytes 1597472 | tf_op jit(solution)/shard_map/ppermute | solution.py:13
  116.4 2.2 %collective-permute-done.5 = bf16[1040,768]{1,0:T(8,128)(2,1)} collective-permute-done((bf16[1040,768]{1,0:T(8,128)(2,1)}, bf16[1040,768]{1,0:T(8,128)(2,1)}, u32[]{:S(2)}, u32[]{:S(2)}) %collective-permute-start.5) | collective-permute-done | bytes 1597472 | tf_op jit(solution)/shard_map/ppermute | solution.py:13
  118.6 0.7 slice.174
  119.4 1.2 slice.173
  120.5 1.2 concatenate.69
  121.7 0.3 collective-permute-start.7
  122.0 1.0 pad_maximum_fusion.1
  123.0 6.0 %collective-permute-start.6 = (bf16[528,768]{1,0:T(8,128)(2,1)}, bf16[528,768]{1,0:T(8,128)(2,1)}, u32[]{:S(2)}, u32[]{:S(2)}) collective-permute-start(bf16[528,768]{1,0:T(8,128)(2,1)} %pad_maximum_fusion.1), channel_id=1, source_target_pairs={{1,0},{2,1},{3,2},{4,3},{5,4},{6,5},{7,6},{8,7},{9,8},{10,9},{11,1... | collective-permute-start | bytes 2433032 | tf_op jit(solution)/shard_map/ppermute | solution.py:13
  129.1 1.3 fusion.20
  131.7 8.0 %collective-permute-start.10 = (f32[1024]{0:T(1024)S(1)}, f32[1024]{0:T(1024)S(1)}, u32[]{:S(2)}, u32[]{:S(2)}) collective-permute-start(f32[1024]{0:T(1024)S(1)} %max.73), channel_id=1, source_target_pairs={{0,2},{1,3},{2,4},{3,5},{4,6},{5,7},{6,8},{7,9},{8,10},{9,11},{10,... | collective-permute-start | bytes 12296 | tf_op jit(solution)/shard_map/ppermute | solution.py:13
  139.7 0.1 collective-permute-start.9
  139.8 3.9 %collective-permute-start.8 = (f32[1024]{0:T(1024)S(1)}, f32[1024]{0:T(1024)S(1)}, u32[]{:S(2)}, u32[]{:S(2)}) collective-permute-start(f32[1024]{0:T(1024)S(1)} %max.70), channel_id=1, source_target_pairs={{0,1},{1,2},{2,3},{3,4},{4,5},{5,6},{6,7},{7,8},{8,9},{9,10},{10,1... | collective-permute-start | bytes 12296 | tf_op jit(solution)/shard_map/ppermute | solution.py:13
  143.8 1.3 fusion.14
  145.7 0.0 copy-start.2
  145.8 1.6 collective-permute-done.8
  147.5 0.7 convert_subtract_fusion
  148.1 0.1 broadcast_bitcast_fusion.13
  148.2 0.7 subtract_bitcast_fusion
  149.0 0.1 broadcast_bitcast_fusion.14
  149.1 3.0 %fusion.32 = (f32[528]{0:T(1024)S(1)}, f32[1040]{0:T(1024)S(1)}) fusion(bf16[1040,768]{1,0:T(8,128)(2,1)} %collective-permute-done.5, bf16[528,768]{1,0:T(8,128)(2,1)} %collective-permute-done.6, pred[]{:T(512)} %ge.15, s32[1040]{0:T(1024)S(1)} %concatenate.72, s32[528]{0:T(1024)S(1)} %concatenate.71), kind=kOutput, calls=%fused_computation.79 | convolution fusion | flops 846741504 | bytes 2420993 | tf_op jit(solution)/shard_map/dot_general | solution.py:62
  152.1 0.6 collective-permute-start.12
  152.6 2.4 %fusion.11 = (f32[528]{0:T(1024)S(1)}, f32[1024]{0:T(1024)S(1)}) fusion(s32[1024]{0:T(1024)S(1)} %bitcast.100, s32[528]{0:T(1024)S(1)} %concatenate.70, pred[]{:T(512)S(6)} %or.11, bf16[1024,768]{1,0:T(8,128)(2,1)S(1)} %pad_maximum_fusion, bf16[528,768]{1,0:T(8,128)(2,1)} %collective-permute-done.7), kind=kOutput, calls=%fused_computation.36 | convolution fusion | flops 833714688 | bytes 2396289 | tf_op jit(solution)/shard_map/dot_general | solution.py:62
  155.0 6.3 %collective-permute-start.11 = (f32[1024]{0:T(1024)S(1)}, f32[1024]{0:T(1024)S(1)}, u32[]{:S(2)}, u32[]{:S(2)}) collective-permute-start(f32[1024]{0:T(1024)S(1)} %max.80), channel_id=1, source_target_pairs={{0,24},{1,25},{2,26},{3,27},{4,28},{5,29},{6,30},{7,31},{8,0},{9,1... | collective-permute-start | bytes 12296 | tf_op jit(solution)/shard_map/ppermute | solution.py:13
  161.4 1.9 %collective-permute-start.13 = (f32[512]{0:T(512)S(1)}, f32[512]{0:T(512)S(1)}, u32[]{:S(2)}, u32[]{:S(2)}) collective-permute-start(f32[512]{0:T(512)S(1)} %slice.181), channel_id=1, source_target_pairs={{0,3},{1,4},{2,5},{3,6},{4,7},{5,8},{6,9},{7,10},{8,11},{9,12},{10... | collective-permute-start | bytes 6152 | tf_op jit(solution)/shard_map/ppermute | solution.py:13
  163.3 6.0 %collective-permute-start.14 = (f32[512]{0:T(512)S(1)}, f32[512]{0:T(512)S(1)}, u32[]{:S(2)}, u32[]{:S(2)}) collective-permute-start(f32[512]{0:T(512)S(1)} %slice.183), channel_id=1, source_target_pairs={{0,29},{1,30},{2,31},{3,0},{4,1},{5,2},{6,3},{7,4},{8,5},{9,6},{10... | collective-permute-start | bytes 6152 | tf_op jit(solution)/shard_map/ppermute | solution.py:13
  169.3 1.4 collective-permute-done.13
  170.8 0.6 broadcast_add_fusion
  (55 shorter events, 0.4 us)
Async XLA Ops:
  0.0 1.9 %copy-start = (bf16[1024,768]{1,0:T(8,128)(2,1)S(1)}, bf16[1024,768]{1,0:T(8,128)(2,1)}, u32[]{:S(2)}) copy-start(bf16[1024,768]{1,0:T(8,128)(2,1)} %param.60) | copy-start | bytes 4718596
  1.9 0.7 copy-start.1
  2.7 74.6 %collective-permute-start.1 = (bf16[1040,768]{1,0:T(8,128)(2,1)S(1)}, bf16[1040,768]{1,0:T(8,128)(2,1)}, u32[]{:S(2)}, u32[]{:S(2)}) collective-permute-start(bf16[1040,768]{1,0:T(8,128)(2,1)S(1)} %fusion.13), channel_id=1, source_target_pairs={{0,1},{1,2},{2,3},{3,4},{4,5},{5,6},{6,7},{7,8},{8,9},{9,10},{10,1... | collective-permute-start | bytes 4792328 | tf_op jit(solution)/shard_map/ppermute | solution.py:13
  4.7 72.7 %collective-permute-start = (bf16[1040,768]{1,0:T(8,128)(2,1)S(1)}, bf16[1040,768]{1,0:T(8,128)(2,1)}, u32[]{:S(2)}, u32[]{:S(2)}) collective-permute-start(bf16[1040,768]{1,0:T(8,128)(2,1)S(1)} %fusion.13), channel_id=1, source_target_pairs={{1,0},{2,1},{3,2},{4,3},{5,4},{6,5},{7,6},{8,7},{9,8},{10,9},{11,1... | collective-permute-start | bytes 4792328 | tf_op jit(solution)/shard_map/ppermute | solution.py:13
  10.6 49.8 %collective-permute-start.2 = (bf16[512,768]{1,0:T(8,128)(2,1)S(1)}, bf16[512,768]{1,0:T(8,128)(2,1)S(1)}, u32[]{:S(2)}, u32[]{:S(2)}) collective-permute-start(bf16[512,768]{1,0:T(8,128)(2,1)S(1)} %get-tuple-element.391), channel_id=1, source_target_pairs={{0,8},{1,9},{2,10},{3,11},{4,12},{5,13},{6,14},{7,15},{8,16},{9,17... | collective-permute-start | bytes 2359304 | tf_op jit(solution)/shard_map/ppermute | solution.py:13
  12.2 65.0 %collective-permute-start.3 = (bf16[512,768]{1,0:T(8,128)(2,1)S(1)}, bf16[512,768]{1,0:T(8,128)(2,1)S(1)}, u32[]{:S(2)}, u32[]{:S(2)}) collective-permute-start(bf16[512,768]{1,0:T(8,128)(2,1)S(1)} %get-tuple-element.392), channel_id=1, source_target_pairs={{0,8},{1,9},{2,10},{3,11},{4,12},{5,13},{6,14},{7,15},{8,16},{9,17... | collective-permute-start | bytes 2359304 | tf_op jit(solution)/shard_map/ppermute | solution.py:13
  77.3 39.1 %collective-permute-start.4 = (bf16[1040,768]{1,0:T(8,128)(2,1)}, bf16[1040,768]{1,0:T(8,128)(2,1)}, u32[]{:S(2)}, u32[]{:S(2)}) collective-permute-start(bf16[1040,768]{1,0:T(8,128)(2,1)} %collective-permute-done), channel_id=1, source_target_pairs={{1,0},{2,1},{3,2},{4,3},{5,4},{6,5},{7,6},{8,7},{9,8},{10,9},{11,1... | collective-permute-start | bytes 4792328 | tf_op jit(solution)/shard_map/ppermute | solution.py:13
  79.3 39.3 %collective-permute-start.5 = (bf16[1040,768]{1,0:T(8,128)(2,1)}, bf16[1040,768]{1,0:T(8,128)(2,1)}, u32[]{:S(2)}, u32[]{:S(2)}) collective-permute-start(bf16[1040,768]{1,0:T(8,128)(2,1)} %collective-permute-done.1), channel_id=1, source_target_pairs={{0,1},{1,2},{2,3},{3,4},{4,5},{5,6},{6,7},{7,8},{8,9},{9,10},{10,1... | collective-permute-start | bytes 4792328 | tf_op jit(solution)/shard_map/ppermute | solution.py:13
  121.7 25.7 %collective-permute-start.7 = (bf16[528,768]{1,0:T(8,128)(2,1)S(1)}, bf16[528,768]{1,0:T(8,128)(2,1)}, u32[]{:S(2)}, u32[]{:S(2)}) collective-permute-start(bf16[528,768]{1,0:T(8,128)(2,1)S(1)} %concatenate.69), channel_id=1, source_target_pairs={{0,1},{1,2},{2,3},{3,4},{4,5},{5,6},{6,7},{7,8},{8,9},{9,10},{10,1... | collective-permute-start | bytes 2433032 | tf_op jit(solution)/shard_map/ppermute | solution.py:13
  123.0 24.5 %collective-permute-start.6 = (bf16[528,768]{1,0:T(8,128)(2,1)}, bf16[528,768]{1,0:T(8,128)(2,1)}, u32[]{:S(2)}, u32[]{:S(2)}) collective-permute-start(bf16[528,768]{1,0:T(8,128)(2,1)} %pad_maximum_fusion.1), channel_id=1, source_target_pairs={{1,0},{2,1},{3,2},{4,3},{5,4},{6,5},{7,6},{8,7},{9,8},{10,9},{11,1... | collective-permute-start | bytes 2433032 | tf_op jit(solution)/shard_map/ppermute | solution.py:13
  131.7 14.1 %collective-permute-start.10 = (f32[1024]{0:T(1024)S(1)}, f32[1024]{0:T(1024)S(1)}, u32[]{:S(2)}, u32[]{:S(2)}) collective-permute-start(f32[1024]{0:T(1024)S(1)} %max.73), channel_id=1, source_target_pairs={{0,2},{1,3},{2,4},{3,5},{4,6},{5,7},{6,8},{7,9},{8,10},{9,11},{10,... | collective-permute-start | bytes 12296 | tf_op jit(solution)/shard_map/ppermute | solution.py:13
  139.7 6.1 %collective-permute-start.9 = (f32[1024]{0:T(1024)S(1)}, f32[1024]{0:T(1024)S(1)}, u32[]{:S(2)}, u32[]{:S(2)}) collective-permute-start(f32[1024]{0:T(1024)S(1)} %maximum_maximum_fusion.1), channel_id=1, source_target_pairs={{0,31},{1,0},{2,1},{3,2},{4,3},{5,4},{6,5},{7,6},{8,7},{9,8},{10,9... | collective-permute-start | bytes 12296 | tf_op jit(solution)/shard_map/ppermute | solution.py:13
  139.8 7.6 %collective-permute-start.8 = (f32[1024]{0:T(1024)S(1)}, f32[1024]{0:T(1024)S(1)}, u32[]{:S(2)}, u32[]{:S(2)}) collective-permute-start(f32[1024]{0:T(1024)S(1)} %max.70), channel_id=1, source_target_pairs={{0,1},{1,2},{2,3},{3,4},{4,5},{5,6},{6,7},{7,8},{8,9},{9,10},{10,1... | collective-permute-start | bytes 12296 | tf_op jit(solution)/shard_map/ppermute | solution.py:13
  145.7 2.5 %copy-start.2 = (s32[1,2]{1,0:T(1,128)S(1)}, s32[1,2]{1,0:T(1,128)}, u32[]{:S(2)}) copy-start(s32[1,2]{1,0:T(1,128)} %constant.393) | copy-start | bytes 28
  152.1 17.2 %collective-permute-start.12 = (f32[1024]{0:T(1024)S(1)}, f32[1024]{0:T(1024)S(1)}, u32[]{:S(2)}, u32[]{:S(2)}) collective-permute-start(f32[1024]{0:T(1024)S(1)} %slice_maximum_fusion), channel_id=1, source_target_pairs={{0,30},{1,31},{2,0},{3,1},{4,2},{5,3},{6,4},{7,5},{8,6},{9,7},{10,... | collective-permute-start | bytes 12296 | tf_op jit(solution)/shard_map/ppermute | solution.py:13
  155.0 14.3 %collective-permute-start.11 = (f32[1024]{0:T(1024)S(1)}, f32[1024]{0:T(1024)S(1)}, u32[]{:S(2)}, u32[]{:S(2)}) collective-permute-start(f32[1024]{0:T(1024)S(1)} %max.80), channel_id=1, source_target_pairs={{0,24},{1,25},{2,26},{3,27},{4,28},{5,29},{6,30},{7,31},{8,0},{9,1... | collective-permute-start | bytes 12296 | tf_op jit(solution)/shard_map/ppermute | solution.py:13
  161.4 9.4 %collective-permute-start.13 = (f32[512]{0:T(512)S(1)}, f32[512]{0:T(512)S(1)}, u32[]{:S(2)}, u32[]{:S(2)}) collective-permute-start(f32[512]{0:T(512)S(1)} %slice.181), channel_id=1, source_target_pairs={{0,3},{1,4},{2,5},{3,6},{4,7},{5,8},{6,9},{7,10},{8,11},{9,12},{10... | collective-permute-start | bytes 6152 | tf_op jit(solution)/shard_map/ppermute | solution.py:13
  163.3 7.5 %collective-permute-start.14 = (f32[512]{0:T(512)S(1)}, f32[512]{0:T(512)S(1)}, u32[]{:S(2)}, u32[]{:S(2)}) collective-permute-start(f32[512]{0:T(512)S(1)} %slice.183), channel_id=1, source_target_pairs={{0,29},{1,30},{2,31},{3,0},{4,1},{5,2},{6,3},{7,4},{8,5},{9,6},{10... | collective-permute-start | bytes 6152 | tf_op jit(solution)/shard_map/ppermute | solution.py:13
